TPU v7x, 128 devices: a whole 4x4x4 slice. The times are simulated.
128 devices in a mesh: expert: 32 (over y, x, core), dp: 4 (over z).
Axes of the slice: x: 4, y: 4, z: 4, core: 2. Of those that a mesh axis runs over, the one named last changes fastest.
Arguments:
- tokens: bfloat16 [16384, 2048], P(('expert', 'dp')), may hold values from -6 to 6
- expert_ids: int32 [16384, 8], P(('expert', 'dp')), may hold values from 0 to 63, all different within a row; in each aligned block of 128 rows (0 to 127, 128 to 255, ...) at most 20 rows name the same one
- gate_probs: float32 [16384, 8], P(('expert', 'dp')), may hold values from 0.02 to 0.4
- cotangent: bfloat16 [16384, 2048], P(('expert', 'dp')), may hold values from -6 to 6
- weight_in: bfloat16 [64, 2048, 768], P('expert'), may hold values from -0.125 to 0.125
- weight_down: bfloat16 [64, 384, 2048], P('expert'), may hold values from -0.3125 to 0.3125
- swap_flag: int32 [32], replicated, may hold values from 0 to 1, as said below
Outputs:
- layer_out: bfloat16 [16384, 2048], P(('expert', 'dp'))
- gate_grads: float32 [16384, 8], P(('expert', 'dp'))
- token_grads: bfloat16 [16384, 2048], P(('expert', 'dp'))
- grad_in: float32 [64, 2048, 768], P('expert', 'dp')
- grad_down: float32 [64, 384, 2048], P('expert', None, 'dp')
Inputs may be any that keep to these rules, and one draw needn't show every extreme that they name: `expert_ids`: each row names 8 different experts. Among the 128 rows of one device no expert is named more than 20 times, and in some of these aligned blocks an expert is named exactly 20 times. swap_flag[i] = swap_flag[i XOR 2]. Where swap_flag[i] is 1, index i of the expert axis takes over the 2 experts of index i XOR 2; experts j * 2 to (j + 1) * 2 - 1 start on index j.
All inputs are finite; a program needn't handle non-finite values.
Results may differ from a plain program's by a relative error of at most 0.0085.
Values may be sent and summed in bfloat16 or wider, within the bound.
No kernel may reach another device: no remote copies, remote signals or barrier semaphores. Data moves between devices by JAX's collectives and lax.ppermute only.
A program may use at most 128 MiB of HBM per device.

v0:
```python
import jax
import jax.numpy as jnp
from jax import lax
from jax.sharding import PartitionSpec as P

FF = 384
EXPERTS = 64
TOP = 8
CAP = 20


def swapped(block, axis, apart):
    count = lax.axis_size(axis)
    route = []
    for low in range(count):
        high = low | 1 << apart
        if high != low and high < count:
            route += [(low, high), (high, low)]
    return lax.ppermute(block, axis, route)


def body(tokens, expert_ids, gate_probs, cotangent, weight_in, weight_down, swap_flag):
    row_count = tokens.shape[0]
    model_width = tokens.shape[1]
    per_device = weight_in.shape[0]
    groups = lax.axis_size("expert")
    device_ids = jnp.arange(groups, dtype=jnp.int32)
    my_index = lax.axis_index("expert")
    my_flag = jnp.sum(jnp.where(device_ids == my_index, swap_flag, 0))
    expert_range = jnp.arange(EXPERTS, dtype=jnp.int32)
    home_device = expert_range // per_device
    moved_flag = jnp.sum(
        jnp.where(home_device[:, None] == device_ids[None, :], swap_flag[None, :], 0), axis=1
    )
    target_device = jnp.bitwise_xor(home_device, 2 * moved_flag)
    partner_in, partner_down = swapped((weight_in, weight_down), "expert", 1)
    use_in = jnp.where(my_flag == 1, partner_in, weight_in)
    use_down = jnp.where(my_flag == 1, partner_down, weight_down)
    dest_place = target_device * per_device + expert_range % per_device
    flat_ids = expert_ids.reshape(-1)
    onehot = (flat_ids[:, None] == expert_range[None, :]).astype(jnp.int32)
    slot_rank = jnp.sum((jnp.cumsum(onehot, axis=0) - onehot) * onehot, axis=1)
    place_of = jnp.sum(onehot * dest_place[None, :], axis=1)
    slot_index = place_of * CAP + slot_rank
    token_copies = jnp.repeat(tokens, TOP, axis=0)
    grad_rows = (gate_probs[:, :, None] * cotangent[:, None, :].astype(jnp.float32)).astype(
        jnp.bfloat16
    )
    grad_rows = grad_rows.reshape(row_count * TOP, model_width)
    empty_rows = jnp.zeros((EXPERTS * CAP, model_width), jnp.bfloat16)
    send_x = (
        empty_rows.at[slot_index].set(token_copies).reshape(groups, per_device, CAP, model_width)
    )
    send_grad = (
        empty_rows.at[slot_index].set(grad_rows).reshape(groups, per_device, CAP, model_width)
    )
    recv_x, recv_grad = (
        lax.all_to_all(send_x, "expert", split_axis=0, concat_axis=0, tiled=True),
        lax.all_to_all(send_grad, "expert", split_axis=0, concat_axis=0, tiled=True),
    )
    projected = jnp.einsum("nscd,sdf->nscf", recv_x, use_in, preferred_element_type=jnp.float32)
    pre_gate = projected[..., :FF]
    up_part = projected[..., FF:]
    sigmoid_gate = jax.nn.sigmoid(pre_gate)
    activated = pre_gate * sigmoid_gate
    hidden = (activated * up_part).astype(jnp.bfloat16)
    expert_out = jnp.einsum(
        "nscf,sfd->nscd", hidden, use_down, preferred_element_type=jnp.float32
    ).astype(jnp.bfloat16)
    hidden_grad = jnp.einsum(
        "nscd,sfd->nscf", recv_grad, use_down, preferred_element_type=jnp.float32
    )
    gate_grad = hidden_grad * up_part * sigmoid_gate * (1.0 + pre_gate * (1.0 - sigmoid_gate))
    proj_grad = jnp.concatenate([gate_grad, hidden_grad * activated], axis=-1).astype(jnp.bfloat16)
    row_grad = jnp.einsum(
        "nscf,sdf->nscd", proj_grad, use_in, preferred_element_type=jnp.float32
    ).astype(jnp.bfloat16)
    home_out, home_grad = (
        lax.all_to_all(expert_out, "expert", split_axis=0, concat_axis=0, tiled=True),
        lax.all_to_all(row_grad, "expert", split_axis=0, concat_axis=0, tiled=True),
    )
    grad_first = jnp.einsum("nscd,nscf->sdf", recv_x, proj_grad, preferred_element_type=jnp.float32)
    grad_second = jnp.einsum(
        "nscf,nscd->sfd", hidden, recv_grad, preferred_element_type=jnp.float32
    )
    reduced_in, reduced_down = (
        lax.psum_scatter(
            grad_first.astype(jnp.bfloat16), "dp", scatter_dimension=1, tiled=True
        ).astype(jnp.float32),
        lax.psum_scatter(
            grad_second.astype(jnp.bfloat16), "dp", scatter_dimension=2, tiled=True
        ).astype(jnp.float32),
    )
    out_rows = home_out.reshape(EXPERTS * CAP, model_width)[slot_index]
    out_rows = out_rows.astype(jnp.float32).reshape(row_count, TOP, model_width)
    layer_out = jnp.sum(gate_probs[:, :, None] * out_rows, axis=1).astype(jnp.bfloat16)
    gate_grads = jnp.sum(cotangent[:, None, :].astype(jnp.float32) * out_rows, axis=2)
    back_rows = home_grad.reshape(EXPERTS * CAP, model_width)[slot_index]
    back_rows = back_rows.astype(jnp.float32).reshape(row_count, TOP, model_width)
    token_grads = jnp.sum(back_rows, axis=1).astype(jnp.bfloat16)
    return (layer_out, gate_grads, token_grads, reduced_in, reduced_down)


def solution(mesh):
    in_specs = (
        P(("expert", "dp"), None),
        P(("expert", "dp"), None),
        P(("expert", "dp"), None),
        P(("expert", "dp"), None),
        P("expert", None, None),
        P("expert", None, None),
        P(),
    )
    out_specs = (
        P(("expert", "dp"), None),
        P(("expert", "dp"), None),
        P(("expert", "dp"), None),
        P("expert", "dp", None),
        P("expert", None, "dp"),
    )
    return jax.shard_map(body, mesh=mesh, in_specs=in_specs, out_specs=out_specs, check_vma=False)
```

profile of v0, /device:TPU:0, one launch (start us, length us, event | category | flops | bytes accessed | tf_op | source)
XLA Modules:
  0.0 607.0 jit_solution(2073382475805539429)
XLA Ops:
  7.2 1.7 collective-permute-start.1
  8.9 0.8 copy.55
  9.9 18.0 %reduce-window.6 = s32[64,8,128]{2,1,0:T(8,128)S(1)} reduce-window(s32[64,8,128]{2,1,0:T(8,128)S(1)} %fusion.41, s32[]{:T(128)} %constant.48.clone.1), window={size=1x1x128 pad=0_0x0_0x127_0}, to_apply=%region_3.4 | reduce-window | flops 8323072 | bytes 524292 | tf_op jit(solution)/shard_map/reduce-window
  27.9 0.1 slice.20
  28.0 0.1 copy.57
  28.3 0.8 select_reduce_fusion.1
  29.1 0.1 broadcast_add_fusion
  29.2 0.1 select_reduce_fusion
  29.3 9.6 %scatter_custom_fusion = bf16[1280,2048]{1,0:T(8,128)(2,1)} fusion(s32[1024]{0:T(1024)S(1)} %bitcast.84, bf16[]{:T(256)} %constant.50.clone.1, bf16[128,2048]{1,0:T(8,128)(2,1)S(1)} %copy-done), kind=kCustom, calls=%fused_computation.27 | custom fusion | bytes 5767170 | tf_op jit(solution)/shard_map/scatter | solution.py:52
  38.9 8.9 %reshape.132 = bf16[32,2,20,2048]{3,2,1,0:T(8,128)(2,1)} reshape(bf16[1280,2048]{1,0:T(8,128)(2,1)} %scatter_custom_fusion) | data formatting | bytes 10485760 | tf_op jit(solution)/shard_map/reshape | solution.py:52
  47.9 11.1 %copy.59 = bf16[32,2,20,2048]{3,1,2,0:T(2,128)(2,1)} copy(bf16[32,2,20,2048]{3,2,1,0:T(8,128)(2,1)} %reshape.132) | data formatting | bytes 10485760 | tf_op jit(solution)/shard_map/reshape | solution.py:52
  59.0 7.3 %all-to-all-start = ((bf16[32,2,20,2048]{3,1,2,0:T(2,128)(2,1)}), bf16[32,2,20,2048]{3,1,2,0:T(2,128)(2,1)}, u32[]{:S(2)}, u32[]{:S(2)}) async-start(bf16[32,2,20,2048]{3,1,2,0:T(2,128)(2,1)} %copy.59), calls=%async_computation | async-start | bytes 10485760 | tf_op jit(solution)/shard_map/all_to_all | solution.py:58
  66.3 2.3 collective-permute-start
  68.6 0.1 copy.54
  68.9 10.1 %scatter_custom_fusion.1 = bf16[1280,2048]{1,0:T(8,128)(2,1)} fusion(s32[1024]{0:T(1024)S(1)} %bitcast.85, f32[1024]{0:T(1024)S(1)} %mul.109, f32[128,2048]{1,0:T(8,128)S(1)} %convert_element_type.69, bf16[]{:T(256)} %constant.50.clone.1), kind=kCustom, calls=%fused_computation.25 | custom fusion | flops 4194304 | bytes 6295554 | tf_op jit(solution)/shard_map/scatter | solution.py:55
  79.0 8.9 %reshape.134 = bf16[32,2,20,2048]{3,2,1,0:T(8,128)(2,1)} reshape(bf16[1280,2048]{1,0:T(8,128)(2,1)} %scatter_custom_fusion.1) | data formatting | bytes 10485760 | tf_op jit(solution)/shard_map/reshape | solution.py:55
  88.0 11.1 %copy.64 = bf16[32,2,20,2048]{3,1,2,0:T(2,128)(2,1)} copy(bf16[32,2,20,2048]{3,2,1,0:T(8,128)(2,1)} %reshape.134) | data formatting | bytes 10485760 | tf_op jit(solution)/shard_map/reshape | solution.py:55
  99.1 0.6 fusion.43
  100.4 104.2 %all-to-all-done = bf16[32,2,20,2048]{3,1,2,0:T(2,128)(2,1)} async-done(((bf16[32,2,20,2048]{3,1,2,0:T(2,128)(2,1)}), bf16[32,2,20,2048]{3,1,2,0:T(2,128)(2,1)}, u32[]{:S(2)}, u32[]{:S(2)}) %all-to-all-start) | async-done | bytes 5242912 | tf_op jit(solution)/shard_map/all_to_all | solution.py:58
  204.6 4.9 all-to-all-start.2
  209.5 0.2 reduce-scatter.5.cloned.1.call-start
  209.7 12.5 %fusion.28 = f32[32,2,20,768]{3,0,2,1:T(8,128)} fusion(bf16[32,2,20,2048]{3,1,2,0:T(2,128)(2,1)} %all-to-all-done, bf16[2,2048,768]{2,1,0:T(8,128)(2,1)} %collective-permute-done.1, bf16[2,2048,768]{2,1,0:T(8,128)(2,1)} %param.11, pred[]{:T(512)S(6)} %eq.52), kind=kOutput, calls=%fused_computation.37 | convolution fusion | flops 4029677568 | bytes 21757952 | tf_op jit(solution)/shard_map/nscd,sdf->nscf/dot_general | solution.py:61
  222.3 47.3 %collective-permute-done = bf16[2,384,2048]{2,1,0:T(8,128)(2,1)} collective-permute-done((bf16[2,384,2048]{2,1,0:T(8,128)(2,1)}, bf16[2,384,2048]{2,1,0:T(8,128)(2,1)}, u32[]{:S(2)}, u32[]{:S(2)}) %collective-permute-start) | collective-permute-done | bytes 3145760 | tf_op jit(solution)/shard_map/ppermute | solution.py:19
  269.6 58.7 %all-to-all-done.2 = bf16[32,2,20,2048]{3,1,2,0:T(2,128)(2,1)} async-done(((bf16[32,2,20,2048]{3,1,2,0:T(2,128)(2,1)}), bf16[32,2,20,2048]{3,1,2,0:T(2,128)(2,1)}, u32[]{:S(2)}, u32[]{:S(2)}) %all-to-all-start.2) | async-done | bytes 5242912 | tf_op jit(solution)/shard_map/all_to_all | solution.py:59
  328.2 11.6 %fusion.35 = (bf16[32,2,20,384]{3,0,2,1:T(8,128)(2,1)S(1)}, bf16[32,2,20,384]{3,0,2,1:T(8,128)(2,1)S(1)}, bf16[32,2,20,384]{3,0,2,1:T(8,128)(2,1)S(1)}) fusion(f32[32,2,20,768]{3,0,2,1:T(8,128)} %fusion.28, bf16[32,2,20,2048]{3,1,2,0:T(2,128)(2,1)} %all-to-all-done.2, bf16[2,384,2048]{2,1,0:T(8,128)(2,1)} %collective-permute-done, ...), kind=kOutput, calls=%fused_computation.43 | convolution fusion | flops 2022211584 | bytes 18415616 | tf_op jit(solution)/shard_map/nscd,sfd->nscf/dot_general | solution.py:70
  339.8 1.0 copy-done.9
  340.8 10.8 %bitcast_convert_fusion.1 = bf16[2,384,2048]{2,1,0:T(8,128)(2,1)} fusion(bf16[32,2,20,384]{3,0,2,1:T(8,128)(2,1)S(1)} %get-tuple-element.26, bf16[32,2,20,2048]{3,1,2,0:T(2,128)(2,1)} %all-to-all-done.2), kind=kOutput, calls=%fused_computation.11 | convolution fusion | flops 2014838784 | bytes 9371648 | tf_op jit(solution)/shard_map/nscf,nscd->sfd/dot_general | solution.py:83
  351.7 0.4 reduce-scatter.3.cloned.1.call-start
  352.1 26.8 %bitcast_convert_fusion = bf16[2,2048,768]{2,1,0:T(8,128)(2,1)} fusion(bf16[32,2,20,2048]{3,1,2,0:T(2,128)(2,1)} %all-to-all-done, bf16[32,2,20,384]{3,0,2,1:T(8,128)(2,1)S(1)} %get-tuple-element.25, bf16[32,2,20,384]{3,0,2,1:T(8,128)(2,1)S(1)} %get-tuple-element.24), kind=kOutput, calls=%fused_computation.4 | convolution fusion | flops 4033609728 | bytes 13500416 | tf_op jit(solution)/shard_map/nscd,nscf->sdf/dot_general | solution.py:82
  378.9 9.1 %convert_bitcast_fusion = bf16[32,2,20,2048]{3,0,2,1:T(8,128)(2,1)} fusion(bf16[2,2048,768]{2,1,0:T(8,128)(2,1)} %collective-permute-done.1, bf16[2,2048,768]{2,1,0:T(8,128)(2,1)} %param.11, pred[]{:T(512)S(6)} %eq.52, bf16[32,2,20,384]{3,0,2,1:T(8,128)(2,1)S(1)} %get-tuple-element.25, bf16[32,2,20,384]{3,0,2,1:T(8,128)(2,1)S(1)} %get-tuple-element.24), kind=kOutput, calls=%fused_computation.17 | convolution fusion | flops 4036231168 | bytes 19791872 | tf_op jit(solution)/shard_map/nscf,sdf->nscd/dot_general | solution.py:75
  388.1 10.4 %copy.66 = bf16[32,2,20,2048]{3,1,2,0:T(2,128)(2,1)} copy(bf16[32,2,20,2048]{3,0,2,1:T(8,128)(2,1)} %convert_bitcast_fusion) | data formatting | bytes 10485760 | tf_op jit(solution)/shard_map/convert_element_type | solution.py:77
  398.4 5.3 all-to-all-start.3
  403.7 6.6 %convert_bitcast_fusion.1 = bf16[32,2,20,2048]{3,0,2,1:T(8,128)(2,1)} fusion(bf16[32,2,20,384]{3,0,2,1:T(8,128)(2,1)S(1)} %copy-done.10, bf16[2,384,2048]{2,1,0:T(8,128)(2,1)} %collective-permute-done, bf16[2,384,2048]{2,1,0:T(8,128)(2,1)} %param.12, pred[]{:T(512)S(6)} %eq.52), kind=kOutput, calls=%fused_computation.18 | convolution fusion | flops 2017460224 | bytes 12517377 | tf_op jit(solution)/shard_map/nscf,sfd->nscd/dot_general | solution.py:67
  410.3 10.2 %copy.61 = bf16[32,2,20,2048]{3,1,2,0:T(2,128)(2,1)} copy(bf16[32,2,20,2048]{3,0,2,1:T(8,128)(2,1)} %convert_bitcast_fusion.1) | data formatting | bytes 10485760 | tf_op jit(solution)/shard_map/convert_element_type | solution.py:69
  420.6 49.0 %all-to-all-done.3 = bf16[32,2,20,2048]{3,1,2,0:T(2,128)(2,1)} async-done(((bf16[32,2,20,2048]{3,1,2,0:T(2,128)(2,1)}), bf16[32,2,20,2048]{3,1,2,0:T(2,128)(2,1)}, u32[]{:S(2)}, u32[]{:S(2)}) %all-to-all-start.3) | async-done | bytes 5242912 | tf_op jit(solution)/shard_map/all_to_all | solution.py:80
  469.5 5.1 all-to-all-start.1
  474.7 7.8 %copy.67 = bf16[32,2,20,2048]{3,2,1,0:T(8,128)(2,1)} copy(bf16[32,2,20,2048]{3,1,2,0:T(2,128)(2,1)} %all-to-all-done.3) | data formatting | bytes 10485760 | tf_op jit(solution)/shard_map/all_to_all | solution.py:80
  482.5 9.0 %reshape.135 = bf16[1280,2048]{1,0:T(8,128)(2,1)} reshape(bf16[32,2,20,2048]{3,2,1,0:T(8,128)(2,1)} %copy.67) | data formatting | bytes 10485760 | tf_op jit(solution)/shard_map/reshape | solution.py:98
  491.5 49.0 %all-to-all-done.1 = bf16[32,2,20,2048]{3,1,2,0:T(2,128)(2,1)} async-done(((bf16[32,2,20,2048]{3,1,2,0:T(2,128)(2,1)}), bf16[32,2,20,2048]{3,1,2,0:T(2,128)(2,1)}, u32[]{:S(2)}, u32[]{:S(2)}) %all-to-all-start.1) | async-done | bytes 5242912 | tf_op jit(solution)/shard_map/all_to_all | solution.py:79
  540.5 7.8 %copy.62 = bf16[32,2,20,2048]{3,2,1,0:T(8,128)(2,1)} copy(bf16[32,2,20,2048]{3,1,2,0:T(2,128)(2,1)} %all-to-all-done.1) | data formatting | bytes 10485760 | tf_op jit(solution)/shard_map/all_to_all | solution.py:79
  548.3 9.0 %reshape.133 = bf16[1280,2048]{1,0:T(8,128)(2,1)} reshape(bf16[32,2,20,2048]{3,2,1,0:T(8,128)(2,1)} %copy.62) | data formatting | bytes 10485760 | tf_op jit(solution)/shard_map/reshape | solution.py:94
  557.3 12.0 %gather_fusion.1 = bf16[1024,2048]{1,0:T(8,128)(2,1)} fusion(bf16[1280,2048]{1,0:T(8,128)(2,1)} %reshape.135, s32[1024]{0:T(1024)S(1)} %broadcast_clamp_fusion), kind=kCustom, calls=%fused_computation.1 | custom fusion | bytes 8392704 | tf_op jit(solution)/shard_map/gather | solution.py:98
  569.2 12.1 %gather_fusion = bf16[1024,2048]{1,0:T(8,128)(2,1)} fusion(bf16[1280,2048]{1,0:T(8,128)(2,1)} %reshape.133, s32[1024]{0:T(1024)S(1)} %broadcast_clamp_fusion), kind=kCustom, calls=%fused_computation | custom fusion | bytes 8392704 | tf_op jit(solution)/shard_map/gather | solution.py:94
  581.3 6.0 fusion.1
  587.3 0.7 copy.70
  588.0 5.9 bitcast_reduce_fusion
  593.9 2.5 convert_element_type.76
  596.4 3.3 convert_element_type.74
  (39 shorter events, 0.6 us)
Async XLA Ops:
  7.2 22.2 %copy-start = (bf16[128,2048]{1,0:T(8,128)(2,1)S(1)}, bf16[128,2048]{1,0:T(8,128)(2,1)}, u32[]{:S(2)}) copy-start(bf16[128,2048]{1,0:T(8,128)(2,1)} %param.7) | copy-start | bytes 1572868
  7.2 202.5 %collective-permute-start.1 = (bf16[2,2048,768]{2,1,0:T(8,128)(2,1)}, bf16[2,2048,768]{2,1,0:T(8,128)(2,1)}, u32[]{:S(2)}, u32[]{:S(2)}) collective-permute-start(bf16[2,2048,768]{2,1,0:T(8,128)(2,1)} %param.11), channel_id=1, source_target_pairs={{0,8},{8,0},{4,12},{12,4},{16,24},{24,16},{20,28},{28,20},{32,40},... | collective-permute-start | bytes 18874376 | tf_op jit(solution)/shard_map/ppermute | solution.py:19
  59.0 9.6 %copy-start.7 = (f32[128,8]{0,1:T(8,128)S(1)}, f32[128,8]{0,1:T(8,128)}, u32[]{:S(2)}) copy-start(f32[128,8]{0,1:T(8,128)} %param.9) | copy-start | bytes 12292
  59.0 9.8 %copy-start.6 = (bf16[128,2048]{1,0:T(8,128)(2,1)S(1)}, bf16[128,2048]{1,0:T(8,128)(2,1)}, u32[]{:S(2)}) copy-start(bf16[128,2048]{1,0:T(8,128)(2,1)} %param.10) | copy-start | bytes 1572868
  59.0 145.6 %all-to-all-start = ((bf16[32,2,20,2048]{3,1,2,0:T(2,128)(2,1)}), bf16[32,2,20,2048]{3,1,2,0:T(2,128)(2,1)}, u32[]{:S(2)}, u32[]{:S(2)}) async-start(bf16[32,2,20,2048]{3,1,2,0:T(2,128)(2,1)} %copy.59), calls=%async_computation | async-start | bytes 10485760 | tf_op jit(solution)/shard_map/all_to_all | solution.py:58
  66.3 203.3 %collective-permute-start = (bf16[2,384,2048]{2,1,0:T(8,128)(2,1)}, bf16[2,384,2048]{2,1,0:T(8,128)(2,1)}, u32[]{:S(2)}, u32[]{:S(2)}) collective-permute-start(bf16[2,384,2048]{2,1,0:T(8,128)(2,1)} %param.12), channel_id=1, source_target_pairs={{0,8},{8,0},{4,12},{12,4},{16,24},{24,16},{20,28},{28,20},{32,40},... | collective-permute-start | bytes 9437192 | tf_op jit(solution)/shard_map/ppermute | solution.py:19
  68.7 19.3 %copy-start.4 = (f32[128,8]{1,0:T(8,128)}, f32[128,8]{1,0:T(8,128)S(1)}, u32[]{:S(2)}) copy-start(f32[128,8]{1,0:T(8,128)S(1)} %copy.54) | copy-start | bytes 12292
  68.9 19.1 %copy-start.2 = (f32[128,2048]{1,0:T(8,128)}, f32[128,2048]{1,0:T(8,128)S(1)}, u32[]{:S(2)}) copy-start(f32[128,2048]{1,0:T(8,128)S(1)} %convert_element_type.69) | copy-start | bytes 3145732
  88.0 11.1 %copy-start.8 = (s32[32]{0:T(128)S(1)}, s32[32]{0:T(128)}, u32[]{:S(2)}) copy-start(s32[32]{0:T(128)} %param.13) | copy-start | bytes 388
  204.6 123.6 %all-to-all-start.2 = ((bf16[32,2,20,2048]{3,1,2,0:T(2,128)(2,1)}), bf16[32,2,20,2048]{3,1,2,0:T(2,128)(2,1)}, u32[]{:S(2)}, u32[]{:S(2)}) async-start(bf16[32,2,20,2048]{3,1,2,0:T(2,128)(2,1)} %copy.64), calls=%async_computation.2 | async-start | bytes 10485760 | tf_op jit(solution)/shard_map/all_to_all | solution.py:59
  209.5 384.4 %reduce-scatter.5.cloned.1.call-start = ((), (), s32[]{:S(2)}) async-start(), calls=%async_computation.7 | async-start | bytes 3932160 | tf_op jit(solution)/shard_map/reduce_scatter | solution.py:90
  339.8 1.0 copy-start.9
  351.7 244.7 %reduce-scatter.3.cloned.1.call-start = ((), (), s32[]{:S(2)}) async-start(), calls=%async_computation.6 | async-start | bytes 7864320 | tf_op jit(solution)/shard_map/reduce_scatter | solution.py:87
  398.4 5.3 copy-start.10
  398.4 71.1 %all-to-all-start.3 = ((bf16[32,2,20,2048]{3,1,2,0:T(2,128)(2,1)}), bf16[32,2,20,2048]{3,1,2,0:T(2,128)(2,1)}, u32[]{:S(2)}, u32[]{:S(2)}) async-start(bf16[32,2,20,2048]{3,1,2,0:T(2,128)(2,1)} %copy.66), calls=%async_computation.3 | async-start | bytes 10485760 | tf_op jit(solution)/shard_map/all_to_all | solution.py:80
  469.5 71.0 %all-to-all-start.1 = ((bf16[32,2,20,2048]{3,1,2,0:T(2,128)(2,1)}), bf16[32,2,20,2048]{3,1,2,0:T(2,128)(2,1)}, u32[]{:S(2)}, u32[]{:S(2)}) async-start(bf16[32,2,20,2048]{3,1,2,0:T(2,128)(2,1)} %copy.61), calls=%async_computation.1 | async-start | bytes 10485760 | tf_op jit(solution)/shard_map/all_to_all | solution.py:79
  569.2 12.1 %copy-start.3 = (f32[128,2048]{1,0:T(8,128)S(1)}, f32[128,2048]{1,0:T(8,128)}, u32[]{:S(2)}) copy-start(f32[128,2048]{1,0:T(8,128)} %copy-done.2) | copy-start | bytes 3145732
  569.2 12.1 %copy-start.5 = (f32[128,8]{1,0:T(8,128)S(1)}, f32[128,8]{1,0:T(8,128)}, u32[]{:S(2)}) copy-start(f32[128,8]{1,0:T(8,128)} %copy-done.4) | copy-start | bytes 12292
  588.0 11.7 %copy-start.1 = (bf16[128,2048]{1,0:T(8,128)(2,1)S(1)}, bf16[128,2048]{1,0:T(8,128)(2,1)}, u32[]{:S(2)}) copy-start(bf16[128,2048]{1,0:T(8,128)(2,1)} %param.7) | copy-start | bytes 1572868
Sparse Core Ops, SparseCore 0:
  351.8 37.1 reduce-scatter.4
  391.4 63.7 reduce-scatter.2
where the time goes:
time: 615 us; the launch traced here: 607 us
  waiting for transfers between devices  308 us (50%)
  local copies, waits for them, and re-layouts  131 us (21%)
  matrix products  77.5 us (13%)
  other arithmetic  47.6 us (8%)
  starting transfers between devices  27.2 us (4%)
  between operations  15.4 us (3%)
    all_to_all x1, waiting for transfers between devices, body(): lax.all_to_all(send_x, 'expert', split_axis=0, concat_axis=0, tiled=True)  104 us
    all_to_all x1, waiting for transfers between devices, body(): lax.all_to_all(send_grad, 'expert', split_axis=0, concat_axis=0, tiled=True)  58.7 us
    all_to_all x1, waiting for transfers between devices, body(): lax.all_to_all(expert_out, 'expert', split_axis=0, concat_axis=0, tiled=T...  49 us
    all_to_all x1, waiting for transfers between devices, body(): lax.all_to_all(row_grad, 'expert', split_axis=0, concat_axis=0, tiled=True)  49 us
    ppermute x2, waiting for transfers between devices, swapped(): return lax.ppermute(block, axis, route)  47.3 us
    dot_general x1, matrix products, body(): jnp.einsum('nscd,nscf->sdf', recv_x, proj_grad, preferred_element_type=jn...  26.8 us
    reshape x2, local copies, waits for them, and re-layouts, body(): empty_rows.at[slot_index].set(grad_rows)  20 us
    reshape x2, local copies, waits for them, and re-layouts, body(): empty_rows.at[slot_index].set(token_copies)  20 us
  transfers between devices with their start and end apart: 8, of which 5 were waited for; matrix products, arithmetic and copies ran while one was open for 38% of the time, Pallas kernels for 0%

commit v1 on v0

v1 whole, which is shorter than its diff:
```python
import jax
import jax.numpy as jnp
from jax import lax
from jax.sharding import PartitionSpec as P

FF = 384
TOP = 8
CAP = 20


def swapped(block, axis, apart):
    count = lax.axis_size(axis)
    route = []
    for low in range(count):
        high = low | 1 << apart
        if high != low and high < count:
            route += [(low, high), (high, low)]
    return lax.ppermute(block, axis, route)


def body(tokens, expert_ids, gate_probs, cotangent, weight_in, weight_down, swap_flag):
    row_count = tokens.shape[0]
    model_width = tokens.shape[1]
    per_device = weight_in.shape[0]
    groups = lax.axis_size("expert")
    experts = groups * per_device
    device_ids = jnp.arange(groups, dtype=jnp.int32)
    my_index = lax.axis_index("expert")
    my_flag = jnp.sum(jnp.where(device_ids == my_index, swap_flag, 0))
    expert_range = jnp.arange(experts, dtype=jnp.int32)
    chosen = expert_ids[:, :, None] == expert_range[None, None, :]
    member = jnp.any(chosen, axis=1)
    row_range = jnp.arange(row_count, dtype=jnp.int32)
    lower = (row_range[:, None] > row_range[None, :]).astype(jnp.bfloat16)
    earlier = jnp.dot(lower, member.astype(jnp.bfloat16), preferred_element_type=jnp.float32)
    rank = earlier.astype(jnp.int32)
    slot_hit = member[:, :, None] & (rank[:, :, None] == jnp.arange(CAP, dtype=jnp.int32)[None, None, :])
    gather_rows = slot_hit.reshape(row_count, experts * CAP).astype(jnp.bfloat16)
    prob_of = jnp.sum(jnp.where(chosen, gate_probs[:, :, None], 0.0), axis=1)
    slot_prob = jnp.sum(jnp.where(slot_hit, prob_of[:, :, None], 0.0), axis=0).reshape(experts * CAP)
    send_x = jnp.dot(gather_rows.T, tokens, preferred_element_type=jnp.float32).astype(jnp.bfloat16)
    send_c = jnp.dot(gather_rows.T, cotangent, preferred_element_type=jnp.float32)
    send_grad = (slot_prob[:, None] * send_c).astype(jnp.bfloat16)
    send_x = send_x.reshape(groups, per_device, CAP, model_width)
    send_grad = send_grad.reshape(groups, per_device, CAP, model_width)
    recv_x = lax.all_to_all(send_x, "expert", split_axis=0, concat_axis=0, tiled=True)
    recv_grad = lax.all_to_all(send_grad, "expert", split_axis=0, concat_axis=0, tiled=True)
    projected = jnp.einsum("nscd,sdf->nscf", recv_x, weight_in, preferred_element_type=jnp.float32)
    pre_gate = projected[..., :FF]
    up_part = projected[..., FF:]
    sigmoid_gate = jax.nn.sigmoid(pre_gate)
    activated = pre_gate * sigmoid_gate
    hidden = (activated * up_part).astype(jnp.bfloat16)
    expert_out = jnp.einsum(
        "nscf,sfd->nscd", hidden, weight_down, preferred_element_type=jnp.float32
    ).astype(jnp.bfloat16)
    home_out = lax.all_to_all(expert_out, "expert", split_axis=0, concat_axis=0, tiled=True)
    hidden_grad = jnp.einsum(
        "nscd,sfd->nscf", recv_grad, weight_down, preferred_element_type=jnp.float32
    )
    gate_grad = hidden_grad * up_part * sigmoid_gate * (1.0 + pre_gate * (1.0 - sigmoid_gate))
    proj_grad = jnp.concatenate([gate_grad, hidden_grad * activated], axis=-1).astype(jnp.bfloat16)
    row_grad = jnp.einsum(
        "nscf,sdf->nscd", proj_grad, weight_in, preferred_element_type=jnp.float32
    ).astype(jnp.bfloat16)
    home_grad = lax.all_to_all(row_grad, "expert", split_axis=0, concat_axis=0, tiled=True)
    grad_first = jnp.einsum("nscd,nscf->sdf", recv_x, proj_grad, preferred_element_type=jnp.float32)
    grad_second = jnp.einsum(
        "nscf,nscd->sfd", hidden, recv_grad, preferred_element_type=jnp.float32
    )
    reduced_in = lax.psum_scatter(
        grad_first.astype(jnp.bfloat16), "dp", scatter_dimension=1, tiled=True
    )
    reduced_down = lax.psum_scatter(
        grad_second.astype(jnp.bfloat16), "dp", scatter_dimension=2, tiled=True
    )
    partner_in, partner_down = swapped((reduced_in, reduced_down), "expert", 1)
    held_in = jnp.where(my_flag == 1, partner_in, reduced_in).astype(jnp.float32)
    held_down = jnp.where(my_flag == 1, partner_down, reduced_down).astype(jnp.float32)
    out_rows = home_out.reshape(experts * CAP, model_width)
    back_rows = home_grad.reshape(experts * CAP, model_width)
    combine = jnp.where(slot_hit, prob_of[:, :, None], 0.0).reshape(row_count, experts * CAP)
    layer_out = jnp.dot(
        combine, out_rows.astype(jnp.float32), precision=lax.Precision.HIGHEST,
        preferred_element_type=jnp.float32,
    ).astype(jnp.bfloat16)
    scores = jnp.dot(cotangent, out_rows.T, preferred_element_type=jnp.float32)
    rank_of = jnp.sum(jnp.where(chosen, rank[:, None, :], 0), axis=2)
    slot_of = expert_ids * CAP + rank_of
    gate_grads = jnp.take_along_axis(scores, slot_of, axis=1)
    token_grads = jnp.dot(gather_rows, back_rows, preferred_element_type=jnp.float32).astype(
        jnp.bfloat16
    )
    return (layer_out, gate_grads, token_grads, held_in, held_down)


def solution(mesh):
    in_specs = (
        P(("expert", "dp"), None),
        P(("expert", "dp"), None),
        P(("expert", "dp"), None),
        P(("expert", "dp"), None),
        P("expert", None, None),
        P("expert", None, None),
        P(),
    )
    out_specs = (
        P(("expert", "dp"), None),
        P(("expert", "dp"), None),
        P(("expert", "dp"), None),
        P("expert", "dp", None),
        P("expert", None, "dp"),
    )
    return jax.shard_map(body, mesh=mesh, in_specs=in_specs, out_specs=out_specs, check_vma=False)
```

time: 615 us -> 449 us (0.73)
  waiting for transfers between devices: 308 us -> 179 us
  other arithmetic: 47.6 us -> 10.5 us
  matrix products: 77.5 us -> 103 us
  local copies, waits for them, and re-layouts: 131 us -> 109 us
    all_to_all x1, waiting for transfers between devices: 104 us -> 39.8 us  [body(): lax.all_to_all(send_x, 'expert', split_axis=0, concat_axis=0, tiled=True)]
    ppermute x2, waiting for transfers between devices: 47.3 us -> 19.9 us  [swapped(): return lax.ppermute(block, axis, route)]
    dot_general x4 -> x10, matrix products: 39.8 us -> 64.8 us  [the longest x1 13.9 us: body(): jnp.einsum('nscd,sdf->nscf', recv_x, weight_in, preferred_element_type=jn...]
    another operation x3 -> x0, other arithmetic: 18.2 us -> none
    all_to_all x1, waiting for transfers between devices: 49 us -> 32.1 us  [body(): lax.all_to_all(row_grad, 'expert', split_axis=0, concat_axis=0, tiled=True)]
    gather x2 -> x5, local copies, waits for them, and re-layouts: 24 us -> 7.34 us  [body(): gate_grads = jnp.take_along_axis(scores, slot_of, axis=1)]
    all_to_all x1, waiting for transfers between devices: 49 us -> 35.5 us  [body(): lax.all_to_all(expert_out, 'expert', split_axis=0, concat_axis=0, tiled=T...]
    reduce_sum x4 -> x3, other arithmetic: 12.8 us -> 1.12 us  [the longest x1 1.05 us: body(): jnp.sum(jnp.where(slot_hit, prob_of[:, :, None], 0.0), axis=0)]
  transfers between devices with their start and end apart: 8 -> 8, of which waited for: 5 -> 5; matrix products, arithmetic and copies ran while one was open for 38% -> 33% of each run, Pallas kernels for 0% -> 0%
where the time goes in v1:
time: 449 us; the launch traced here: 441 us
  waiting for transfers between devices  179 us (40%)
  local copies, waits for them, and re-layouts  109 us (24%)
  matrix products  103 us (23%)
  starting transfers between devices  25.1 us (6%)
  between operations  15.4 us (3%)
  other arithmetic  10.5 us (2%)
    all_to_all x1, waiting for transfers between devices, body(): lax.all_to_all(send_grad, 'expert', split_axis=0, concat_axis=0, tiled=True)  51.7 us
    all_to_all x1, waiting for transfers between devices, body(): lax.all_to_all(send_x, 'expert', split_axis=0, concat_axis=0, tiled=True)  39.8 us
    all_to_all x1, waiting for transfers between devices, body(): lax.all_to_all(expert_out, 'expert', split_axis=0, concat_axis=0, tiled=T...  35.5 us
    all_to_all x1, waiting for transfers between devices, body(): lax.all_to_all(row_grad, 'expert', split_axis=0, concat_axis=0, tiled=True)  32.1 us
    dot_general x1, matrix products, body(): jnp.einsum('nscd,nscf->sdf', recv_x, proj_grad, preferred_element_type=jn...  26.8 us
    reshape x2, local copies, waits for them, and re-layouts, body(): send_grad = send_grad.reshape(groups, per_device, CAP, model_width)  20.1 us
    reshape x2, local copies, waits for them, and re-layouts, body(): send_x = send_x.reshape(groups, per_device, CAP, model_width)  20 us
    ppermute x2, waiting for transfers between devices, swapped(): return lax.ppermute(block, axis, route)  19.9 us
  transfers between devices with their start and end apart: 8, of which 5 were waited for; matrix products, arithmetic and copies ran while one was open for 33% of the time, Pallas kernels for 0%

profile of v1, /device:TPU:0, one launch (start us, length us, event | category | flops | bytes accessed | tf_op | source)
XLA Modules:
  0.0 441.2 jit_solution(15301354997534634674)
XLA Ops:
  7.2 0.9 fusion.27
  8.2 1.0 eq.65
  9.2 2.0 eq.68
  11.2 0.7 and.38
  12.1 1.4 compare_and_fusion
  13.5 4.9 %convolution_convert_fusion = bf16[1280,2048]{1,0:T(8,128)(2,1)} fusion(pred[128,1280]{0,1:T(32,128)(4,1)S(1)} %compare_and_fusion, bf16[128,2048]{1,0:T(8,128)(2,1)} %param.7), kind=kOutput, calls=%fused_computation.3 | convolution fusion | flops 673710080 | bytes 5931008 | tf_op jit(solution)/shard_map/dot_general | solution.py:41
  18.4 8.9 %reshape.116 = bf16[32,2,20,2048]{3,2,1,0:T(8,128)(2,1)} reshape(bf16[1280,2048]{1,0:T(8,128)(2,1)} %convolution_convert_fusion) | data formatting | bytes 10485760 | tf_op jit(solution)/shard_map/reshape | solution.py:44
  27.3 11.1 %copy.58 = bf16[32,2,20,2048]{3,1,2,0:T(2,128)(2,1)} copy(bf16[32,2,20,2048]{3,2,1,0:T(8,128)(2,1)} %reshape.116) | data formatting | bytes 10485760 | tf_op jit(solution)/shard_map/reshape | solution.py:44
  38.4 7.7 %all-to-all-start = ((bf16[32,2,20,2048]{3,1,2,0:T(2,128)(2,1)}), bf16[32,2,20,2048]{3,1,2,0:T(2,128)(2,1)}, u32[]{:S(2)}, u32[]{:S(2)}) async-start(bf16[32,2,20,2048]{3,1,2,0:T(2,128)(2,1)} %copy.58), calls=%async_computation | async-start | bytes 10485760 | tf_op jit(solution)/shard_map/all_to_all | solution.py:46
  46.1 1.0 fusion.28
  47.3 4.8 %multiply_convert_fusion = bf16[1280,2048]{1,0:T(8,128)(2,1)} fusion(pred[128,1280]{0,1:T(32,128)(4,1)S(1)} %compare_and_fusion, bf16[128,2048]{1,0:T(8,128)(2,1)} %param.10, f32[1280]{0:T(1024)S(1)} %mul.41), kind=kOutput, calls=%fused_computation.2 | convolution fusion | flops 676331520 | bytes 5936128 | tf_op jit(solution)/shard_map/dot_general | solution.py:42
  52.1 8.9 %reshape.119 = bf16[32,2,20,2048]{3,2,1,0:T(8,128)(2,1)} reshape(bf16[1280,2048]{1,0:T(8,128)(2,1)} %multiply_convert_fusion) | data formatting | bytes 10485760 | tf_op jit(solution)/shard_map/reshape | solution.py:45
  61.0 11.2 %copy.64 = bf16[32,2,20,2048]{3,1,2,0:T(2,128)(2,1)} copy(bf16[32,2,20,2048]{3,2,1,0:T(8,128)(2,1)} %reshape.119) | data formatting | bytes 10485760 | tf_op jit(solution)/shard_map/reshape | solution.py:45
  72.2 39.8 %all-to-all-done = bf16[32,2,20,2048]{3,1,2,0:T(2,128)(2,1)} async-done(((bf16[32,2,20,2048]{3,1,2,0:T(2,128)(2,1)}), bf16[32,2,20,2048]{3,1,2,0:T(2,128)(2,1)}, u32[]{:S(2)}, u32[]{:S(2)}) %all-to-all-start) | async-done | bytes 5242912 | tf_op jit(solution)/shard_map/all_to_all | solution.py:46
  112.0 4.9 %all-to-all-start.2 = ((bf16[32,2,20,2048]{3,1,2,0:T(2,128)(2,1)}), bf16[32,2,20,2048]{3,1,2,0:T(2,128)(2,1)}, u32[]{:S(2)}, u32[]{:S(2)}) async-start(bf16[32,2,20,2048]{3,1,2,0:T(2,128)(2,1)} %copy.64), calls=%async_computation.2 | async-start | bytes 10485760 | tf_op jit(solution)/shard_map/all_to_all | solution.py:47
  116.8 0.3 reduce-scatter.3.cloned.1.call-start
  117.1 13.9 %fusion.16 = f32[32,2,20,768]{3,0,2,1:T(8,128)} fusion(bf16[2,2048,768]{2,1,0:T(8,128)(2,1)} %param.11, bf16[32,2,20,2048]{3,1,2,0:T(2,128)(2,1)} %all-to-all-done), kind=kOutput, calls=%fused_computation.22 | convolution fusion | flops 4026531840 | bytes 15466496 | tf_op jit(solution)/shard_map/nscd,sdf->nscf/dot_general | solution.py:48
  131.0 51.7 %all-to-all-done.2 = bf16[32,2,20,2048]{3,1,2,0:T(2,128)(2,1)} async-done(((bf16[32,2,20,2048]{3,1,2,0:T(2,128)(2,1)}), bf16[32,2,20,2048]{3,1,2,0:T(2,128)(2,1)}, u32[]{:S(2)}, u32[]{:S(2)}) %all-to-all-start.2) | async-done | bytes 5242912 | tf_op jit(solution)/shard_map/all_to_all | solution.py:47
  182.7 11.8 %fusion.23 = (bf16[32,2,20,384]{3,0,2,1:T(8,128)(2,1)S(1)}, bf16[32,2,20,384]{3,0,2,1:T(8,128)(2,1)S(1)}, bf16[32,2,20,384]{3,0,2,1:T(8,128)(2,1)}) fusion(f32[32,2,20,768]{3,0,2,1:T(8,128)} %fusion.16, bf16[2,384,2048]{2,1,0:T(8,128)(2,1)S(1)} %copy-done, bf16[32,2,20,2048]{3,1,2,0:T(2,128)(2,1)} %all-to-all-done.2), kind=kOutput, calls=%fused_computation.28 | convolution fusion | flops 2020638720 | bytes 15269888 | tf_op jit(solution)/shard_map/nscd,sfd->nscf/dot_general | solution.py:58
  194.5 1.0 copy-done.11
  195.5 0.3 copy-done.13
  195.8 26.8 %bitcast_convert_fusion = bf16[2,2048,768]{2,1,0:T(8,128)(2,1)} fusion(bf16[32,2,20,2048]{3,1,2,0:T(2,128)(2,1)} %all-to-all-done, bf16[32,2,20,384]{3,0,2,1:T(8,128)(2,1)S(1)} %get-tuple-element.21, bf16[32,2,20,384]{3,0,2,1:T(8,128)(2,1)S(1)} %get-tuple-element.20), kind=kOutput, calls=%fused_computation.1 | convolution fusion | flops 4033609728 | bytes 13500416 | tf_op jit(solution)/shard_map/nscd,nscf->sdf/dot_general | solution.py:67
  222.6 6.0 %convert_bitcast_fusion.1 = bf16[32,2,20,2048]{3,0,2,1:T(8,128)(2,1)} fusion(bf16[32,2,20,384]{3,0,2,1:T(8,128)(2,1)} %get-tuple-element.22, bf16[2,384,2048]{2,1,0:T(8,128)(2,1)S(1)} %copy-done), kind=kOutput, calls=%fused_computation.10 | convolution fusion | flops 2015887360 | bytes 9371648 | tf_op jit(solution)/shard_map/nscf,sfd->nscd/dot_general | solution.py:54
  228.6 11.1 %copy.60 = bf16[32,2,20,2048]{3,1,2,0:T(2,128)(2,1)} copy(bf16[32,2,20,2048]{3,0,2,1:T(8,128)(2,1)} %convert_bitcast_fusion.1) | data formatting | bytes 10485760 | tf_op jit(solution)/shard_map/convert_element_type | solution.py:56
  239.7 5.0 %all-to-all-start.1 = ((bf16[32,2,20,2048]{3,1,2,0:T(2,128)(2,1)}), bf16[32,2,20,2048]{3,1,2,0:T(2,128)(2,1)}, u32[]{:S(2)}, u32[]{:S(2)}) async-start(bf16[32,2,20,2048]{3,1,2,0:T(2,128)(2,1)} %copy.60), calls=%async_computation.1 | async-start | bytes 10485760 | tf_op jit(solution)/shard_map/all_to_all | solution.py:57
  244.8 11.0 %bitcast_convert_fusion.1 = bf16[2,384,2048]{2,1,0:T(8,128)(2,1)} fusion(bf16[32,2,20,384]{3,0,2,1:T(8,128)(2,1)S(1)} %copy-done.10, bf16[32,2,20,2048]{3,1,2,0:T(2,128)(2,1)} %all-to-all-done.2), kind=kOutput, calls=%fused_computation.4 | convolution fusion | flops 2014838784 | bytes 9371648 | tf_op jit(solution)/shard_map/nscf,nscd->sfd/dot_general | solution.py:68
  255.9 9.1 %convert_bitcast_fusion = bf16[32,2,20,2048]{3,0,2,1:T(8,128)(2,1)} fusion(bf16[2,2048,768]{2,1,0:T(8,128)(2,1)} %param.11, bf16[32,2,20,384]{3,0,2,1:T(8,128)(2,1)S(1)} %copy-done.14, bf16[32,2,20,384]{3,0,2,1:T(8,128)(2,1)S(1)} %copy-done.12), kind=kOutput, calls=%fused_computation.9 | convolution fusion | flops 4033085440 | bytes 13500416 | tf_op jit(solution)/shard_map/nscf,sdf->nscd/dot_general | solution.py:63
  265.0 10.2 %copy.67 = bf16[32,2,20,2048]{3,1,2,0:T(2,128)(2,1)} copy(bf16[32,2,20,2048]{3,0,2,1:T(8,128)(2,1)} %convert_bitcast_fusion) | data formatting | bytes 10485760 | tf_op jit(solution)/shard_map/convert_element_type | solution.py:65
  275.1 35.5 %all-to-all-done.1 = bf16[32,2,20,2048]{3,1,2,0:T(2,128)(2,1)} async-done(((bf16[32,2,20,2048]{3,1,2,0:T(2,128)(2,1)}), bf16[32,2,20,2048]{3,1,2,0:T(2,128)(2,1)}, u32[]{:S(2)}, u32[]{:S(2)}) %all-to-all-start.1) | async-done | bytes 5242912 | tf_op jit(solution)/shard_map/all_to_all | solution.py:57
  310.6 4.9 %all-to-all-start.3 = ((bf16[32,2,20,2048]{3,1,2,0:T(2,128)(2,1)}), bf16[32,2,20,2048]{3,1,2,0:T(2,128)(2,1)}, u32[]{:S(2)}, u32[]{:S(2)}) async-start(bf16[32,2,20,2048]{3,1,2,0:T(2,128)(2,1)} %copy.67), calls=%async_computation.3 | async-start | bytes 10485760 | tf_op jit(solution)/shard_map/all_to_all | solution.py:66
  315.5 0.2 fusion.26
  316.1 0.9 select_n.53
  316.9 0.6 fusion.29
  318.2 7.9 %copy.61 = bf16[32,2,20,2048]{3,2,1,0:T(8,128)(2,1)} copy(bf16[32,2,20,2048]{3,1,2,0:T(2,128)(2,1)} %all-to-all-done.1) | data formatting | bytes 10485760 | tf_op jit(solution)/shard_map/all_to_all | solution.py:57
  326.1 9.0 %reshape.117 = bf16[1280,2048]{1,0:T(8,128)(2,1)} reshape(bf16[32,2,20,2048]{3,2,1,0:T(8,128)(2,1)} %copy.61) | data formatting | bytes 10485760 | tf_op jit(solution)/shard_map/reshape | solution.py:80
  335.2 1.8 collective-permute-start
  337.0 4.0 convolution_bitcast_fusion
  341.1 7.0 %gather_fusion = f32[1024]{0:T(1024)S(1)} fusion(f32[128,1280]{0,1:T(8,128)S(1)} %convolution_bitcast_fusion, s32[1024]{0:T(1024)S(1)} %reshape.121), kind=kCustom, calls=%fused_computation | custom fusion | bytes 16384 | tf_op jit(solution)/shard_map/jit(take_along_axis)/gather | solution.py:90
  348.2 0.5 collective-permute-start.1
  348.7 0.6 and_select_fusion
  349.3 32.1 %all-to-all-done.3 = bf16[32,2,20,2048]{3,1,2,0:T(2,128)(2,1)} async-done(((bf16[32,2,20,2048]{3,1,2,0:T(2,128)(2,1)}), bf16[32,2,20,2048]{3,1,2,0:T(2,128)(2,1)}, u32[]{:S(2)}, u32[]{:S(2)}) %all-to-all-start.3) | async-done | bytes 5242912 | tf_op jit(solution)/shard_map/all_to_all | solution.py:66
  381.4 7.8 %copy.68 = bf16[32,2,20,2048]{3,2,1,0:T(8,128)(2,1)} copy(bf16[32,2,20,2048]{3,1,2,0:T(2,128)(2,1)} %all-to-all-done.3) | data formatting | bytes 10485760 | tf_op jit(solution)/shard_map/all_to_all | solution.py:66
  389.2 9.0 %reshape.120 = bf16[1280,2048]{1,0:T(8,128)(2,1)} reshape(bf16[32,2,20,2048]{3,2,1,0:T(8,128)(2,1)} %copy.68) | data formatting | bytes 10485760 | tf_op jit(solution)/shard_map/reshape | solution.py:81
  398.2 4.3 convolution_convert_fusion.1
  402.5 5.8 %convolution_convert_fusion.2 = bf16[128,2048]{1,0:T(8,128)(2,1)} fusion(f32[128,1280]{0,1:T(8,128)S(1)} %copy-done.3, bf16[1280,2048]{1,0:T(8,128)(2,1)} %reshape.117), kind=kOutput, calls=%fused_computation.21 | convolution fusion | flops 4026793984 | bytes 6422528 | tf_op jit(solution)/shard_map/dot_general | solution.py:83
  408.4 19.9 %collective-permute-done.1 = bf16[2,384,512]{2,1,0:T(8,128)(2,1)} collective-permute-done((bf16[2,384,512]{2,1,0:T(8,128)(2,1)}, bf16[2,384,512]{2,1,0:T(8,128)(2,1)}, u32[]{:S(2)}, u32[]{:S(2)}) %collective-permute-start.1) | collective-permute-done | bytes 786464 | tf_op jit(solution)/shard_map/ppermute | solution.py:18
  428.3 2.4 select_convert_fusion.1
  430.7 3.3 select_convert_fusion
  (47 shorter events, 1.0 us)
Async XLA Ops:
  7.2 175.6 %copy-start = (bf16[2,384,2048]{2,1,0:T(8,128)(2,1)S(1)}, bf16[2,384,2048]{2,1,0:T(8,128)(2,1)}, u32[]{:S(2)}) copy-start(bf16[2,384,2048]{2,1,0:T(8,128)(2,1)} %param.12) | copy-start | bytes 9437188
  38.4 7.7 %copy-start.7 = (s32[128,8]{0,1:T(8,128)S(1)}, s32[128,8]{0,1:T(8,128)}, u32[]{:S(2)}) copy-start(s32[128,8]{0,1:T(8,128)} %param.8) | copy-start | bytes 12292
  38.4 7.7 %copy-start.8 = (f32[128,8]{0,1:T(8,128)S(1)}, f32[128,8]{0,1:T(8,128)}, u32[]{:S(2)}) copy-start(f32[128,8]{0,1:T(8,128)} %param.9) | copy-start | bytes 12292
  38.4 73.6 %all-to-all-start = ((bf16[32,2,20,2048]{3,1,2,0:T(2,128)(2,1)}), bf16[32,2,20,2048]{3,1,2,0:T(2,128)(2,1)}, u32[]{:S(2)}, u32[]{:S(2)}) async-start(bf16[32,2,20,2048]{3,1,2,0:T(2,128)(2,1)} %copy.58), calls=%async_computation | async-start | bytes 10485760 | tf_op jit(solution)/shard_map/all_to_all | solution.py:46
  112.0 70.8 %all-to-all-start.2 = ((bf16[32,2,20,2048]{3,1,2,0:T(2,128)(2,1)}), bf16[32,2,20,2048]{3,1,2,0:T(2,128)(2,1)}, u32[]{:S(2)}, u32[]{:S(2)}) async-start(bf16[32,2,20,2048]{3,1,2,0:T(2,128)(2,1)} %copy.64), calls=%async_computation.2 | async-start | bytes 10485760 | tf_op jit(solution)/shard_map/all_to_all | solution.py:47
  116.8 218.3 %reduce-scatter.3.cloned.1.call-start = ((), (), s32[]{:S(2)}) async-start(), calls=%async_computation.6 | async-start | bytes 7864320 | tf_op jit(solution)/shard_map/reduce_scatter | solution.py:71
  194.5 1.0 copy-start.11
  194.5 1.3 copy-start.13
  239.7 5.1 %copy-start.10 = (bf16[32,2,20,384]{3,0,2,1:T(8,128)(2,1)S(1)}, bf16[32,2,20,384]{3,0,2,1:T(8,128)(2,1)}, u32[]{:S(2)}) copy-start(bf16[32,2,20,384]{3,0,2,1:T(8,128)(2,1)} %get-tuple-element.22) | copy-start | bytes 2949124
  239.7 70.9 %all-to-all-start.1 = ((bf16[32,2,20,2048]{3,1,2,0:T(2,128)(2,1)}), bf16[32,2,20,2048]{3,1,2,0:T(2,128)(2,1)}, u32[]{:S(2)}, u32[]{:S(2)}) async-start(bf16[32,2,20,2048]{3,1,2,0:T(2,128)(2,1)} %copy.60), calls=%async_computation.1 | async-start | bytes 10485760 | tf_op jit(solution)/shard_map/all_to_all | solution.py:57
  244.7 11.1 %copy-start.12 = (bf16[32,2,20,384]{3,0,2,1:T(8,128)(2,1)S(1)}, bf16[32,2,20,384]{3,0,2,1:T(8,128)(2,1)}, u32[]{:S(2)}) copy-start(bf16[32,2,20,384]{3,0,2,1:T(8,128)(2,1)} %copy-done.11) | copy-start | bytes 2949124
  244.7 11.1 %copy-start.14 = (bf16[32,2,20,384]{3,0,2,1:T(8,128)(2,1)S(1)}, bf16[32,2,20,384]{3,0,2,1:T(8,128)(2,1)}, u32[]{:S(2)}) copy-start(bf16[32,2,20,384]{3,0,2,1:T(8,128)(2,1)} %copy-done.13) | copy-start | bytes 2949124
  244.8 103.5 %reduce-scatter.5.cloned.1.call-start = ((), (), s32[]{:S(2)}) async-start(), calls=%async_computation.7 | async-start | bytes 3932160 | tf_op jit(solution)/shard_map/reduce_scatter | solution.py:74
  275.1 40.9 %copy-start.2 = (f32[128,64,20]{0,2,1:T(8,128)S(1)}, f32[128,64,20]{0,2,1:T(8,128)}, u32[]{:S(2)}) copy-start(f32[128,64,20]{0,2,1:T(8,128)} %get-tuple-element.24) | copy-start | bytes 1966084
  275.1 41.8 %copy-start.9 = (s32[32]{0:T(128)S(1)}, s32[32]{0:T(128)}, u32[]{:S(2)}) copy-start(s32[32]{0:T(128)} %param.13) | copy-start | bytes 388
  310.6 70.8 %all-to-all-start.3 = ((bf16[32,2,20,2048]{3,1,2,0:T(2,128)(2,1)}), bf16[32,2,20,2048]{3,1,2,0:T(2,128)(2,1)}, u32[]{:S(2)}, u32[]{:S(2)}) async-start(bf16[32,2,20,2048]{3,1,2,0:T(2,128)(2,1)} %copy.67), calls=%async_computation.3 | async-start | bytes 10485760 | tf_op jit(solution)/shard_map/all_to_all | solution.py:66
  326.1 10.9 %copy-start.4 = (bf16[128,2048]{1,0:T(8,128)(2,1)S(1)}, bf16[128,2048]{1,0:T(8,128)(2,1)}, u32[]{:S(2)}) copy-start(bf16[128,2048]{1,0:T(8,128)(2,1)} %param.10) | copy-start | bytes 1572868
  335.2 95.5 %collective-permute-start = (bf16[2,512,768]{2,1,0:T(8,128)(2,1)}, bf16[2,512,768]{2,1,0:T(8,128)(2,1)}, u32[]{:S(2)}, u32[]{:S(2)}) collective-permute-start(bf16[2,512,768]{2,1,0:T(8,128)(2,1)} %reduce-scatter.3.cloned.1.call-done), channel_id=1, source_target_pairs={{0,8},{8,0},{4,12},{12,4},{16,24},{24,16},{20,28},{28,20},{32,40},... | collective-permute-start | bytes 4718600 | tf_op jit(solution)/shard_map/ppermute | solution.py:18
  348.2 80.0 %collective-permute-start.1 = (bf16[2,384,512]{2,1,0:T(8,128)(2,1)}, bf16[2,384,512]{2,1,0:T(8,128)(2,1)}, u32[]{:S(2)}, u32[]{:S(2)}) collective-permute-start(bf16[2,384,512]{2,1,0:T(8,128)(2,1)} %reduce-scatter.5.cloned.1.call-done), channel_id=1, source_target_pairs={{0,8},{8,0},{4,12},{12,4},{16,24},{24,16},{20,28},{28,20},{32,40},... | collective-permute-start | bytes 2359304 | tf_op jit(solution)/shard_map/ppermute | solution.py:18
  398.2 4.3 copy-start.3
  398.2 30.1 %copy-start.6 = (bf16[2,384,512]{2,1,0:T(8,128)(2,1)S(1)}, bf16[2,384,512]{2,1,0:T(8,128)(2,1)}, u32[]{:S(2)}) copy-start(bf16[2,384,512]{2,1,0:T(8,128)(2,1)} %reduce-scatter.5.cloned.1.call-done) | copy-start | bytes 2359300
  402.5 28.1 %copy-start.5 = (bf16[2,512,768]{2,1,0:T(8,128)(2,1)S(1)}, bf16[2,512,768]{2,1,0:T(8,128)(2,1)}, u32[]{:S(2)}) copy-start(bf16[2,512,768]{2,1,0:T(8,128)(2,1)} %reduce-scatter.3.cloned.1.call-done) | copy-start | bytes 4718596
  402.5 31.4 %copy-start.1 = (bf16[2,384,2048]{2,1,0:T(8,128)(2,1)S(1)}, bf16[2,384,2048]{2,1,0:T(8,128)(2,1)}, u32[]{:S(2)}) copy-start(bf16[2,384,2048]{2,1,0:T(8,128)(2,1)} %param.12) | copy-start | bytes 9437188
Sparse Core Ops, SparseCore 0:
  222.7 61.7 reduce-scatter.2
  287.6 38.0 reduce-scatter.4

commit v2 on v1

--- a/solution.py
+++ b/solution.py
@@ -34,6 +34,8 @@
     lower = (row_range[:, None] > row_range[None, :]).astype(jnp.bfloat16)
     earlier = jnp.dot(lower, member.astype(jnp.bfloat16), preferred_element_type=jnp.float32)
     rank = earlier.astype(jnp.int32)
+    odd = (expert_range % 2 == 1)[None, :]
+    rank = jnp.where(odd, CAP - 1 - rank, rank)
     slot_hit = member[:, :, None] & (rank[:, :, None] == jnp.arange(CAP, dtype=jnp.int32)[None, None, :])
     gather_rows = slot_hit.reshape(row_count, experts * CAP).astype(jnp.bfloat16)
     prob_of = jnp.sum(jnp.where(chosen, gate_probs[:, :, None], 0.0), axis=1)
@@ -41,33 +43,55 @@
     send_x = jnp.dot(gather_rows.T, tokens, preferred_element_type=jnp.float32).astype(jnp.bfloat16)
     send_c = jnp.dot(gather_rows.T, cotangent, preferred_element_type=jnp.float32)
     send_grad = (slot_prob[:, None] * send_c).astype(jnp.bfloat16)
-    send_x = send_x.reshape(groups, per_device, CAP, model_width)
-    send_grad = send_grad.reshape(groups, per_device, CAP, model_width)
+    lanes = per_device * CAP
+    send_x = send_x.reshape(groups, lanes, model_width)
+    send_grad = send_grad.reshape(groups, lanes, model_width)
     recv_x = lax.all_to_all(send_x, "expert", split_axis=0, concat_axis=0, tiled=True)
     recv_grad = lax.all_to_all(send_grad, "expert", split_axis=0, concat_axis=0, tiled=True)
-    projected = jnp.einsum("nscd,sdf->nscf", recv_x, weight_in, preferred_element_type=jnp.float32)
-    pre_gate = projected[..., :FF]
-    up_part = projected[..., FF:]
-    sigmoid_gate = jax.nn.sigmoid(pre_gate)
-    activated = pre_gate * sigmoid_gate
-    hidden = (activated * up_part).astype(jnp.bfloat16)
-    expert_out = jnp.einsum(
-        "nscf,sfd->nscd", hidden, weight_down, preferred_element_type=jnp.float32
-    ).astype(jnp.bfloat16)
-    home_out = lax.all_to_all(expert_out, "expert", split_axis=0, concat_axis=0, tiled=True)
-    hidden_grad = jnp.einsum(
-        "nscd,sfd->nscf", recv_grad, weight_down, preferred_element_type=jnp.float32
-    )
-    gate_grad = hidden_grad * up_part * sigmoid_gate * (1.0 + pre_gate * (1.0 - sigmoid_gate))
-    proj_grad = jnp.concatenate([gate_grad, hidden_grad * activated], axis=-1).astype(jnp.bfloat16)
-    row_grad = jnp.einsum(
-        "nscf,sdf->nscd", proj_grad, weight_in, preferred_element_type=jnp.float32
-    ).astype(jnp.bfloat16)
-    home_grad = lax.all_to_all(row_grad, "expert", split_axis=0, concat_axis=0, tiled=True)
-    grad_first = jnp.einsum("nscd,nscf->sdf", recv_x, proj_grad, preferred_element_type=jnp.float32)
-    grad_second = jnp.einsum(
-        "nscf,nscd->sfd", hidden, recv_grad, preferred_element_type=jnp.float32
-    )
+    window = CAP + 4
+    shift = lanes - window
+    place = jnp.arange(window, dtype=jnp.int32)[None, :, None]
+    outs, backs, firsts, seconds = [], [], [], []
+    for local in range(per_device):
+        low = local * shift
+        rows_x = recv_x[:, low:low + window].reshape(groups * window, model_width)
+        own = (place < CAP) if local == 0 else (place >= window - CAP)
+        rows_grad = jnp.where(own, recv_grad[:, low:low + window], jnp.zeros((), jnp.bfloat16))
+        rows_grad = rows_grad.reshape(groups * window, model_width)
+        first_weight = weight_in[local]
+        second_weight = weight_down[local]
+        projected = jnp.dot(rows_x, first_weight, preferred_element_type=jnp.float32)
+        pre_gate = projected[:, :FF]
+        up_part = projected[:, FF:]
+        sigmoid_gate = jax.nn.sigmoid(pre_gate)
+        activated = pre_gate * sigmoid_gate
+        hidden = (activated * up_part).astype(jnp.bfloat16)
+        expert_out = jnp.dot(hidden, second_weight, preferred_element_type=jnp.float32).astype(
+            jnp.bfloat16
+        )
+        hidden_grad = jnp.dot(rows_grad, second_weight.T, preferred_element_type=jnp.float32)
+        gate_grad = hidden_grad * up_part * sigmoid_gate * (1.0 + pre_gate * (1.0 - sigmoid_gate))
+        proj_grad = jnp.concatenate([gate_grad, hidden_grad * activated], axis=-1).astype(
+            jnp.bfloat16
+        )
+        row_grad = jnp.dot(proj_grad, first_weight.T, preferred_element_type=jnp.float32).astype(
+            jnp.bfloat16
+        )
+        outs.append(expert_out.reshape(groups, window, model_width))
+        backs.append(row_grad.reshape(groups, window, model_width))
+        firsts.append(jnp.dot(rows_x.T, proj_grad, preferred_element_type=jnp.float32))
+        seconds.append(jnp.dot(hidden.T, rows_grad, preferred_element_type=jnp.float32))
+
+    def merged(pieces):
+        tile = window - shift
+        seam = jnp.arange(tile, dtype=jnp.int32)[None, :, None] < CAP - shift
+        middle = jnp.where(seam, pieces[0][:, shift:], pieces[1][:, :tile])
+        return jnp.concatenate([pieces[0][:, :shift], middle, pieces[1][:, tile:]], axis=1)
+
+    home_out = lax.all_to_all(merged(outs), "expert", split_axis=0, concat_axis=0, tiled=True)
+    home_grad = lax.all_to_all(merged(backs), "expert", split_axis=0, concat_axis=0, tiled=True)
+    grad_first = jnp.stack(firsts)
+    grad_second = jnp.stack(seconds)
     reduced_in = lax.psum_scatter(
         grad_first.astype(jnp.bfloat16), "dp", scatter_dimension=1, tiled=True
     )

time: 449 us -> 396 us (0.88); the launches traced: 441 us -> 395 us
  local copies, waits for them, and re-layouts: 109 us -> 21.5 us
  waiting for transfers between devices: 179 us -> 251 us
  matrix products: 103 us -> 60.6 us
  other arithmetic: 10.5 us -> 22 us
    reshape x6 -> x0, local copies, waits for them, and re-layouts: 58.1 us -> none  [the longest x2 20.1 us: body(): send_grad = send_grad.reshape(groups, per_device, CAP, model_width)]
    dot_general x6 -> x12, matrix products: 78.6 us -> 38.9 us  [the longest x2 12.4 us: body(): jnp.dot(rows_x, first_weight, preferred_element_type=jnp.float32)]
    all_to_all x2, waiting for transfers between devices: 67.5 us -> 103 us  [the longest x1 53 us: body(): lax.all_to_all(merged(outs), 'expert', split_axis=0, concat_axis=0, tiled...]
    all_to_all x1, waiting for transfers between devices: 39.8 us -> 61.6 us  [body(): lax.all_to_all(send_x, 'expert', split_axis=0, concat_axis=0, tiled=True)]
    convert_element_type x2 -> x0, local copies, waits for them, and re-layouts: 21.3 us -> none  [the longest x1 11.1 us: body(): expert_out = jnp.einsum('nscf,sfd->nscd', hidden, weight_down, preferred_...]
    ppermute x2, waiting for transfers between devices: 19.9 us -> 36.9 us  [swapped(): return lax.ppermute(block, axis, route)]
    all_to_all x2 -> x0, local copies, waits for them, and re-layouts: 15.7 us -> none  [the longest x1 7.9 us: body(): lax.all_to_all(expert_out, 'expert', split_axis=0, concat_axis=0, tiled=T...]
    slice x0 -> x5, local copies, waits for them, and re-layouts: none -> 6.15 us  [the longest x1 3.59 us: body(): rows_x = recv_x[:, low:low + window].reshape(groups * window, model_width)]
  transfers between devices with their start and end apart: 8 -> 8, of which waited for: 5 -> 5; matrix products, arithmetic and copies ran while one was open for 33% -> 18% of each run, Pallas kernels for 0% -> 0%
where the time goes in v2:
time: 396 us; the launch traced here: 395 us
  waiting for transfers between devices  251 us (63%)
  matrix products  60.6 us (15%)
  starting transfers between devices  24.9 us (6%)
  other arithmetic  22 us (6%)
  local copies, waits for them, and re-layouts  21.5 us (5%)
  between operations  15.4 us (4%)
    all_to_all x1, waiting for transfers between devices, body(): lax.all_to_all(send_x, 'expert', split_axis=0, concat_axis=0, tiled=True)  61.6 us
    all_to_all x1, waiting for transfers between devices, body(): lax.all_to_all(merged(outs), 'expert', split_axis=0, concat_axis=0, tiled...  53 us
    all_to_all x1, waiting for transfers between devices, body(): lax.all_to_all(send_grad, 'expert', split_axis=0, concat_axis=0, tiled=True)  49.7 us
    all_to_all x1, waiting for transfers between devices, body(): lax.all_to_all(merged(backs), 'expert', split_axis=0, concat_axis=0, tile...  49.6 us
    ppermute x2, waiting for transfers between devices, swapped(): return lax.ppermute(block, axis, route)  36.9 us
    dot_general x2, matrix products, body(): jnp.dot(rows_x, first_weight, preferred_element_type=jnp.float32)  12.4 us
  transfers between devices with their start and end apart: 8, of which 5 were waited for; matrix products, arithmetic and copies ran while one was open for 18% of the time, Pallas kernels for 0%

profile of v2, /device:TPU:0, one launch (start us, length us, event | category | flops | bytes accessed | tf_op | source)
XLA Modules:
  0.0 395.2 jit_solution(3609753212046363361)
XLA Ops:
  7.2 0.8 fusion.27
  8.8 3.8 convolution_convert_fusion
  12.6 7.7 %all-to-all-start = ((bf16[32,40,2048]{2,1,0:T(8,128)(2,1)}), bf16[32,40,2048]{2,1,0:T(8,128)(2,1)}, u32[]{:S(2)}, u32[]{:S(2)}) async-start(bf16[32,40,2048]{2,1,0:T(8,128)(2,1)} %bitcast.82), calls=%async_computation | async-start | bytes 10485760 | tf_op jit(solution)/shard_map/all_to_all | solution.py:49
  20.8 3.8 multiply_convert_fusion
  24.6 61.6 %all-to-all-done = bf16[32,40,2048]{2,1,0:T(8,128)(2,1)} async-done(((bf16[32,40,2048]{2,1,0:T(8,128)(2,1)}), bf16[32,40,2048]{2,1,0:T(8,128)(2,1)}, u32[]{:S(2)}, u32[]{:S(2)}) %all-to-all-start) | async-done | bytes 5242912 | tf_op jit(solution)/shard_map/all_to_all | solution.py:49
  86.2 4.9 %all-to-all-start.2 = ((bf16[32,40,2048]{2,1,0:T(8,128)(2,1)}), bf16[32,40,2048]{2,1,0:T(8,128)(2,1)}, u32[]{:S(2)}, u32[]{:S(2)}) async-start(bf16[32,40,2048]{2,1,0:T(8,128)(2,1)} %bitcast.81), calls=%async_computation.2 | async-start | bytes 10485760 | tf_op jit(solution)/shard_map/all_to_all | solution.py:50
  91.1 3.6 fusion.35
  94.8 8.3 %fusion.4 = f32[768,768]{0,1:T(8,128)} fusion(bf16[768,2048]{1,0:T(8,128)(2,1)S(1)} %bitcast.97, bf16[2,2048,768]{2,1,0:T(8,128)(2,1)} %param.11), kind=kOutput, calls=%fused_computation.19 | convolution fusion | flops 2415919104 | bytes 8650752 | tf_op jit(solution)/shard_map/dot_general | solution.py:63
  103.1 4.2 %fusion.1 = f32[768,768]{0,1:T(8,128)} fusion(bf16[768,2048]{1,0:T(8,128)(2,1)S(1)} %bitcast.95, bf16[2,2048,768]{2,1,0:T(8,128)(2,1)S(1)} %bitcast.100), kind=kOutput, calls=%fused_computation.16 | convolution fusion | flops 2415919104 | bytes 8650752 | tf_op jit(solution)/shard_map/dot_general | solution.py:63
  107.2 49.7 %all-to-all-done.2 = bf16[32,40,2048]{2,1,0:T(8,128)(2,1)} async-done(((bf16[32,40,2048]{2,1,0:T(8,128)(2,1)}), bf16[32,40,2048]{2,1,0:T(8,128)(2,1)}, u32[]{:S(2)}, u32[]{:S(2)}) %all-to-all-start.2) | async-done | bytes 5242912 | tf_op jit(solution)/shard_map/all_to_all | solution.py:50
  156.9 3.3 slice_select_fusion.1
  160.3 0.4 copy-done.16
  160.7 1.2 copy-done.23
  161.9 1.8 multiply_convert_fusion.4
  163.8 0.5 copy-done.22
  164.3 2.6 multiply_convert_fusion.2
  167.0 2.9 fusion.6
  169.9 2.9 fusion.7
  172.9 3.2 pad_maximum_fusion
  176.2 3.2 convolution_convert_fusion.6
  179.7 1.6 copy-done.17
  181.4 1.8 convolution_convert_fusion.5
  183.4 0.8 slice-done.3
  184.9 2.9 convolution_convert_fusion.4
  187.8 3.1 convolution_convert_fusion.3
  191.4 1.2 copy-done.2
  192.6 2.9 pad_maximum_fusion.1
  195.5 4.9 %all-to-all-start.1 = ((bf16[32,40,2048]{2,1,0:T(8,128)(2,1)}), bf16[32,40,2048]{2,1,0:T(8,128)(2,1)}, u32[]{:S(2)}, u32[]{:S(2)}) async-start(bf16[32,40,2048]{2,1,0:T(8,128)(2,1)} %pad_maximum_fusion.1), calls=%async_computation.1 | async-start | bytes 10485760 | tf_op jit(solution)/shard_map/all_to_all | solution.py:91
  200.5 3.6 fusion.12
  204.1 1.4 fusion.13
  205.5 2.0 pad_maximum_fusion.3
  207.5 1.9 slice.93
  209.5 0.7 copy-done.3
  210.4 2.8 pad_maximum_fusion.2
  213.3 53.0 %all-to-all-done.1 = bf16[32,40,2048]{2,1,0:T(8,128)(2,1)} async-done(((bf16[32,40,2048]{2,1,0:T(8,128)(2,1)}), bf16[32,40,2048]{2,1,0:T(8,128)(2,1)}, u32[]{:S(2)}, u32[]{:S(2)}) %all-to-all-start.1) | async-done | bytes 5242912 | tf_op jit(solution)/shard_map/all_to_all | solution.py:91
  266.3 4.9 %all-to-all-start.3 = ((bf16[32,40,2048]{2,1,0:T(8,128)(2,1)}), bf16[32,40,2048]{2,1,0:T(8,128)(2,1)}, u32[]{:S(2)}, u32[]{:S(2)}) async-start(bf16[32,40,2048]{2,1,0:T(8,128)(2,1)} %pad_maximum_fusion.2), calls=%async_computation.3 | async-start | bytes 10485760 | tf_op jit(solution)/shard_map/all_to_all | solution.py:92
  271.8 0.6 fusion.30
  273.1 1.7 collective-permute-start
  274.8 4.1 %convolution_bitcast_fusion = f32[128,1280]{0,1:T(8,128)S(1)} fusion(bf16[1280,2048]{1,0:T(8,128)(2,1)} %bitcast.9, bf16[128,2048]{1,0:T(8,128)(2,1)S(1)} %copy-done), kind=kOutput, calls=%fused_computation.31 | convolution fusion | flops 671088640 | bytes 6422528 | tf_op jit(solution)/shard_map/dot_general | solution.py:111
  278.9 7.0 %gather_fusion = f32[1024]{0:T(1024)S(1)} fusion(f32[128,1280]{0,1:T(8,128)S(1)} %convolution_bitcast_fusion, s32[1024]{0:T(1024)S(1)} %reshape.178), kind=kCustom, calls=%fused_computation | custom fusion | bytes 16384 | tf_op jit(solution)/shard_map/jit(take_along_axis)/gather | solution.py:114
  286.0 0.8 collective-permute-start.1
  286.8 0.6 and_select_fusion
  287.4 49.6 %all-to-all-done.3 = bf16[32,40,2048]{2,1,0:T(8,128)(2,1)} async-done(((bf16[32,40,2048]{2,1,0:T(8,128)(2,1)}), bf16[32,40,2048]{2,1,0:T(8,128)(2,1)}, u32[]{:S(2)}, u32[]{:S(2)}) %all-to-all-start.3) | async-done | bytes 5242912 | tf_op jit(solution)/shard_map/all_to_all | solution.py:92
  337.1 4.2 %convolution_convert_fusion.9 = bf16[128,2048]{1,0:T(8,128)(2,1)} fusion(pred[128,1280]{0,1:T(32,128)(4,1)S(1)} %and.54, bf16[1280,2048]{1,0:T(8,128)(2,1)} %bitcast.17), kind=kOutput, calls=%fused_computation.32 | convolution fusion | flops 671350784 | bytes 5931008 | tf_op jit(solution)/shard_map/dot_general | solution.py:115
  341.3 5.7 %convolution_convert_fusion.10 = bf16[128,2048]{1,0:T(8,128)(2,1)} fusion(f32[128,1280]{0,1:T(8,128)S(1)} %select_n.84, bf16[1280,2048]{1,0:T(8,128)(2,1)} %bitcast.9), kind=kOutput, calls=%fused_computation.33 | convolution fusion | flops 4026793984 | bytes 6422528 | tf_op jit(solution)/shard_map/dot_general | solution.py:107
  347.0 36.9 %collective-permute-done.1 = bf16[2,384,512]{2,1,0:T(8,128)(2,1)S(1)} collective-permute-done((bf16[2,384,512]{2,1,0:T(8,128)(2,1)}, bf16[2,384,512]{2,1,0:T(8,128)(2,1)S(1)}, u32[]{:S(2)}, u32[]{:S(2)}) %collective-permute-start.1) | collective-permute-done | bytes 786464 | tf_op jit(solution)/shard_map/ppermute | solution.py:18
  383.9 1.2 select_convert_fusion.1
  385.1 3.3 select_convert_fusion
  (101 shorter events, 4.0 us)
Async XLA Ops:
  7.2 13.6 %copy-start = (bf16[128,2048]{1,0:T(8,128)(2,1)S(1)}, bf16[128,2048]{1,0:T(8,128)(2,1)}, u32[]{:S(2)}) copy-start(bf16[128,2048]{1,0:T(8,128)(2,1)} %param.10) | copy-start | bytes 1572868
  7.2 1.6 copy-start.13
  12.6 7.7 %copy-start.14 = (s32[128,8]{0,1:T(8,128)S(1)}, s32[128,8]{0,1:T(8,128)}, u32[]{:S(2)}) copy-start(s32[128,8]{0,1:T(8,128)} %param.8) | copy-start | bytes 12292
  12.6 7.7 %copy-start.15 = (f32[128,8]{0,1:T(8,128)S(1)}, f32[128,8]{0,1:T(8,128)}, u32[]{:S(2)}) copy-start(f32[128,8]{0,1:T(8,128)} %param.9) | copy-start | bytes 12292
  12.6 73.6 %all-to-all-start = ((bf16[32,40,2048]{2,1,0:T(8,128)(2,1)}), bf16[32,40,2048]{2,1,0:T(8,128)(2,1)}, u32[]{:S(2)}, u32[]{:S(2)}) async-start(bf16[32,40,2048]{2,1,0:T(8,128)(2,1)} %bitcast.82), calls=%async_computation | async-start | bytes 10485760 | tf_op jit(solution)/shard_map/all_to_all | solution.py:49
  86.2 70.8 %all-to-all-start.2 = ((bf16[32,40,2048]{2,1,0:T(8,128)(2,1)}), bf16[32,40,2048]{2,1,0:T(8,128)(2,1)}, u32[]{:S(2)}, u32[]{:S(2)}) async-start(bf16[32,40,2048]{2,1,0:T(8,128)(2,1)} %bitcast.81), calls=%async_computation.2 | async-start | bytes 10485760 | tf_op jit(solution)/shard_map/all_to_all | solution.py:50
  91.1 182.0 %reduce-scatter.3.cloned.1.call-start = ((), (), s32[]{:S(2)}) async-start(), calls=%async_computation.6 | async-start | bytes 7864320 | tf_op jit(solution)/shard_map/reduce_scatter | solution.py:95
  91.1 11.9 %slice-start = ((s8[6291456]{0:T(1024)(128)(4,1)}), s8[4194304]{0:T(1024)(128)(4,1)S(1)}, s32[]{:S(2)}) async-start(s8[6291456]{0:T(1024)(128)(4,1)} %bitcast.99), calls=%async_computation.8 | async-start | bytes 8388608
  94.7 8.3 %copy-start.9 = (bf16[32,24,2048]{2,1,0:T(8,128)(2,1)}, bf16[32,24,2048]{2,1,0:T(8,128)(2,1)S(1)}, u32[]{:S(2)}) copy-start(bf16[32,24,2048]{2,1,0:T(8,128)(2,1)S(1)} %get-tuple-element.12) | copy-start | bytes 9437188
  94.8 8.3 %copy-start.7 = (bf16[32,24,2048]{2,1,0:T(8,128)(2,1)}, bf16[32,24,2048]{2,1,0:T(8,128)(2,1)S(1)}, u32[]{:S(2)}) copy-start(bf16[32,24,2048]{2,1,0:T(8,128)(2,1)S(1)} %get-tuple-element.13) | copy-start | bytes 9437188
  94.8 8.3 %slice-start.1 = ((s8[6291456]{0:T(1024)(128)(4,1)}), s8[2097152]{0:T(1024)(128)(4,1)S(1)}, s32[]{:S(2)}) async-start(s8[6291456]{0:T(1024)(128)(4,1)} %bitcast.99), calls=%async_computation.9 | async-start | bytes 4194304
  156.9 3.8 copy-start.16
  156.9 5.0 %copy-start.23 = (f32[768,768]{0,1:T(8,128)S(1)}, f32[768,768]{0,1:T(8,128)}, u32[]{:S(2)}) copy-start(f32[768,768]{0,1:T(8,128)} %fusion.4) | copy-start | bytes 7077892
  160.2 3.6 copy-start.6
  160.2 3.6 copy-start.4
  161.9 2.4 copy-start.22
  163.8 3.1 copy-start.24
  163.8 3.1 copy-start.26
  163.8 12.3 %copy-start.19 = (bf16[768,384]{0,1:T(8,128)(2,1)}, bf16[768,384]{0,1:T(8,128)(2,1)S(1)}, u32[]{:S(2)}) copy-start(bf16[768,384]{0,1:T(8,128)(2,1)S(1)} %get-tuple-element.18) | copy-start | bytes 1769476
  164.3 2.6 copy-start.10
  166.9 3.0 copy-start.28
  166.9 3.0 copy-start.30
  167.0 3.0 copy-start.8
  179.4 1.9 copy-start.17
  179.4 2.0 copy-start.20
  179.4 4.0 %slice-start.2 = ((s8[6291456]{0:T(1024)(128)(4,1)}), s8[4194304]{0:T(1024)(128)(4,1)S(1)}, s32[]{:S(2)}) async-start(s8[6291456]{0:T(1024)(128)(4,1)} %bitcast.101), calls=%async_computation.10 | async-start | bytes 8388608
  181.4 2.8 slice-start.3
  183.3 1.3 copy-start.25
  183.3 1.6 copy-start.27
  184.9 2.9 copy-start.29
  184.9 2.9 copy-start.31
  187.8 3.2 copy-start.1
  191.0 1.7 copy-start.2
  195.5 70.8 %all-to-all-start.1 = ((bf16[32,40,2048]{2,1,0:T(8,128)(2,1)}), bf16[32,40,2048]{2,1,0:T(8,128)(2,1)}, u32[]{:S(2)}, u32[]{:S(2)}) async-start(bf16[32,40,2048]{2,1,0:T(8,128)(2,1)} %pad_maximum_fusion.1), calls=%async_computation.1 | async-start | bytes 10485760 | tf_op jit(solution)/shard_map/all_to_all | solution.py:91
  200.4 85.6 %reduce-scatter.5.cloned.1.call-start = ((), (), s32[]{:S(2)}) async-start(), calls=%async_computation.7 | async-start | bytes 3932160 | tf_op jit(solution)/shard_map/reduce_scatter | solution.py:98
  200.5 3.6 copy-start.5
  200.5 3.6 copy-start.21
  207.5 2.7 copy-start.3
  213.3 58.5 %copy-start.18 = (s32[32]{0:T(128)S(1)}, s32[32]{0:T(128)}, u32[]{:S(2)}) copy-start(s32[32]{0:T(128)} %param.13) | copy-start | bytes 388
  266.3 70.8 %all-to-all-start.3 = ((bf16[32,40,2048]{2,1,0:T(8,128)(2,1)}), bf16[32,40,2048]{2,1,0:T(8,128)(2,1)}, u32[]{:S(2)}, u32[]{:S(2)}) async-start(bf16[32,40,2048]{2,1,0:T(8,128)(2,1)} %pad_maximum_fusion.2), calls=%async_computation.3 | async-start | bytes 10485760 | tf_op jit(solution)/shard_map/all_to_all | solution.py:92
  273.1 112.0 %collective-permute-start = (bf16[2,512,768]{2,1,0:T(8,128)(2,1)}, bf16[2,512,768]{2,1,0:T(8,128)(2,1)}, u32[]{:S(2)}, u32[]{:S(2)}) collective-permute-start(bf16[2,512,768]{2,1,0:T(8,128)(2,1)} %reduce-scatter.3.cloned.1.call-done), channel_id=1, source_target_pairs={{0,8},{8,0},{4,12},{12,4},{16,24},{24,16},{20,28},{28,20},{32,40},... | collective-permute-start | bytes 4718600 | tf_op jit(solution)/shard_map/ppermute | solution.py:18
  286.0 97.8 %collective-permute-start.1 = (bf16[2,384,512]{2,1,0:T(8,128)(2,1)}, bf16[2,384,512]{2,1,0:T(8,128)(2,1)S(1)}, u32[]{:S(2)}, u32[]{:S(2)}) collective-permute-start(bf16[2,384,512]{2,1,0:T(8,128)(2,1)} %reduce-scatter.5.cloned.1.call-done), channel_id=1, source_target_pairs={{0,8},{8,0},{4,12},{12,4},{16,24},{24,16},{20,28},{28,20},{32,40},... | collective-permute-start | bytes 2359304 | tf_op jit(solution)/shard_map/ppermute | solution.py:18
  341.3 42.6 %copy-start.12 = (bf16[2,384,512]{2,1,0:T(8,128)(2,1)S(1)}, bf16[2,384,512]{2,1,0:T(8,128)(2,1)}, u32[]{:S(2)}) copy-start(bf16[2,384,512]{2,1,0:T(8,128)(2,1)} %reduce-scatter.5.cloned.1.call-done) | copy-start | bytes 2359300
  347.0 38.1 %copy-start.11 = (bf16[2,512,768]{2,1,0:T(8,128)(2,1)S(1)}, bf16[2,512,768]{2,1,0:T(8,128)(2,1)}, u32[]{:S(2)}) copy-start(bf16[2,512,768]{2,1,0:T(8,128)(2,1)} %reduce-scatter.3.cloned.1.call-done) | copy-start | bytes 4718596
Sparse Core Ops, SparseCore 0:
  176.3 61.7 reduce-scatter.2
  240.5 38.0 reduce-scatter.4

commit v3 on v2

--- a/solution.py
+++ b/solution.py
@@ -51,36 +51,20 @@
     window = CAP + 4
     shift = lanes - window
     place = jnp.arange(window, dtype=jnp.int32)[None, :, None]
-    outs, backs, firsts, seconds = [], [], [], []
+    forwards = []
     for local in range(per_device):
         low = local * shift
         rows_x = recv_x[:, low:low + window].reshape(groups * window, model_width)
-        own = (place < CAP) if local == 0 else (place >= window - CAP)
-        rows_grad = jnp.where(own, recv_grad[:, low:low + window], jnp.zeros((), jnp.bfloat16))
-        rows_grad = rows_grad.reshape(groups * window, model_width)
-        first_weight = weight_in[local]
-        second_weight = weight_down[local]
-        projected = jnp.dot(rows_x, first_weight, preferred_element_type=jnp.float32)
+        projected = jnp.dot(rows_x, weight_in[local], preferred_element_type=jnp.float32)
         pre_gate = projected[:, :FF]
         up_part = projected[:, FF:]
         sigmoid_gate = jax.nn.sigmoid(pre_gate)
         activated = pre_gate * sigmoid_gate
         hidden = (activated * up_part).astype(jnp.bfloat16)
-        expert_out = jnp.dot(hidden, second_weight, preferred_element_type=jnp.float32).astype(
+        expert_out = jnp.dot(hidden, weight_down[local], preferred_element_type=jnp.float32).astype(
             jnp.bfloat16
         )
-        hidden_grad = jnp.dot(rows_grad, second_weight.T, preferred_element_type=jnp.float32)
-        gate_grad = hidden_grad * up_part * sigmoid_gate * (1.0 + pre_gate * (1.0 - sigmoid_gate))
-        proj_grad = jnp.concatenate([gate_grad, hidden_grad * activated], axis=-1).astype(
-            jnp.bfloat16
-        )
-        row_grad = jnp.dot(proj_grad, first_weight.T, preferred_element_type=jnp.float32).astype(
-            jnp.bfloat16
-        )
-        outs.append(expert_out.reshape(groups, window, model_width))
-        backs.append(row_grad.reshape(groups, window, model_width))
-        firsts.append(jnp.dot(rows_x.T, proj_grad, preferred_element_type=jnp.float32))
-        seconds.append(jnp.dot(hidden.T, rows_grad, preferred_element_type=jnp.float32))
+        forwards.append((rows_x, pre_gate, up_part, sigmoid_gate, activated, hidden, expert_out))
 
     def merged(pieces):
         tile = window - shift
@@ -88,8 +72,27 @@
         middle = jnp.where(seam, pieces[0][:, shift:], pieces[1][:, :tile])
         return jnp.concatenate([pieces[0][:, :shift], middle, pieces[1][:, tile:]], axis=1)
 
-    home_out = lax.all_to_all(merged(outs), "expert", split_axis=0, concat_axis=0, tiled=True)
-    home_grad = lax.all_to_all(merged(backs), "expert", split_axis=0, concat_axis=0, tiled=True)
+    send_out = merged([f[-1].reshape(groups, window, model_width) for f in forwards])
+    send_out, recv_grad = lax.optimization_barrier((send_out, recv_grad))
+    home_out = lax.all_to_all(send_out, "expert", split_axis=0, concat_axis=0, tiled=True)
+    backs, firsts, seconds = [], [], []
+    for local in range(per_device):
+        low = local * shift
+        rows_x, pre_gate, up_part, sigmoid_gate, activated, hidden, _ = forwards[local]
+        own = (place < CAP) if local == 0 else (place >= window - CAP)
+        rows_grad = jnp.where(own, recv_grad[:, low:low + window], jnp.zeros((), jnp.bfloat16))
+        rows_grad = rows_grad.reshape(groups * window, model_width)
+        hidden_grad = jnp.dot(rows_grad, weight_down[local].T, preferred_element_type=jnp.float32)
+        gate_grad = hidden_grad * up_part * sigmoid_gate * (1.0 + pre_gate * (1.0 - sigmoid_gate))
+        proj_grad = jnp.concatenate([gate_grad, hidden_grad * activated], axis=-1).astype(
+            jnp.bfloat16
+        )
+        row_grad = jnp.dot(proj_grad, weight_in[local].T, preferred_element_type=jnp.float32).astype(
+            jnp.bfloat16
+        )
+        backs.append(row_grad.reshape(groups, window, model_width))
+        firsts.append(jnp.dot(rows_x.T, proj_grad, preferred_element_type=jnp.float32))
+        seconds.append(jnp.dot(hidden.T, rows_grad, preferred_element_type=jnp.float32))
     grad_first = jnp.stack(firsts)
     grad_second = jnp.stack(seconds)
     reduced_in = lax.psum_scatter(
@@ -98,6 +101,8 @@
     reduced_down = lax.psum_scatter(
         grad_second.astype(jnp.bfloat16), "dp", scatter_dimension=2, tiled=True
     )
+    send_back, reduced_in = lax.optimization_barrier((merged(backs), reduced_in))
+    home_grad = lax.all_to_all(send_back, "expert", split_axis=0, concat_axis=0, tiled=True)
     partner_in, partner_down = swapped((reduced_in, reduced_down), "expert", 1)
     held_in = jnp.where(my_flag == 1, partner_in, reduced_in).astype(jnp.float32)
     held_down = jnp.where(my_flag == 1, partner_down, reduced_down).astype(jnp.float32)

time: 396 us -> 386 us (0.975); the launches traced: 395 us -> 381 us
  waiting for transfers between devices: 251 us -> 235 us
    all_to_all x2, waiting for transfers between devices: 103 us -> 8.82 us  [the longest x1 8.82 us: body(): lax.all_to_all(send_out, 'expert', split_axis=0, concat_axis=0, tiled=True)]
    reduce_scatter x1, waiting for transfers between devices: 0.02 us -> 34.1 us  [body(): lax.psum_scatter(grad_first.astype(jnp.bfloat16), 'dp', scatter_dimension...]
    ppermute x2, waiting for transfers between devices: 36.9 us -> 66.5 us  [swapped(): return lax.ppermute(block, axis, route)]
    reduce_scatter x1, waiting for transfers between devices: 0.01 us -> 21.6 us  [body(): lax.psum_scatter(grad_second.astype(jnp.bfloat16), 'dp', scatter_dimensio...]
    all_to_all x1, waiting for transfers between devices: 49.7 us -> 42.4 us  [body(): lax.all_to_all(send_grad, 'expert', split_axis=0, concat_axis=0, tiled=True)]
  transfers between devices with their start and end apart: 8 -> 8, of which waited for: 5 -> 6; matrix products, arithmetic and copies ran while one was open for 18% -> 19% of each run, Pallas kernels for 0% -> 0%
where the time goes in v3:
time: 386 us; the launch traced here: 381 us
  waiting for transfers between devices  235 us (61%)
  matrix products  60 us (16%)
  starting transfers between devices  25.8 us (7%)
  other arithmetic  25.4 us (7%)
  local copies, waits for them, and re-layouts  19.2 us (5%)
  between operations  15.8 us (4%)
    ppermute x2, waiting for transfers between devices, swapped(): return lax.ppermute(block, axis, route)  66.5 us
    all_to_all x1, waiting for transfers between devices, body(): lax.all_to_all(send_x, 'expert', split_axis=0, concat_axis=0, tiled=True)  61.5 us
    all_to_all x1, waiting for transfers between devices, body(): lax.all_to_all(send_grad, 'expert', split_axis=0, concat_axis=0, tiled=True)  42.4 us
    reduce_scatter x1, waiting for transfers between devices, body(): lax.psum_scatter(grad_first.astype(jnp.bfloat16), 'dp', scatter_dimension...  34.1 us
    reduce_scatter x1, waiting for transfers between devices, body(): lax.psum_scatter(grad_second.astype(jnp.bfloat16), 'dp', scatter_dimensio...  21.6 us
    dot_general x2, matrix products, body(): jnp.dot(proj_grad, weight_in[local].T, preferred_element_type=jnp.float32)  10 us
    dot_general x2, matrix products, body(): jnp.dot(rows_x, weight_in[local], preferred_element_type=jnp.float32)  9.7 us
    all_to_all x1, waiting for transfers between devices, body(): lax.all_to_all(send_out, 'expert', split_axis=0, concat_axis=0, tiled=True)  8.82 us
  transfers between devices with their start and end apart: 8, of which 6 were waited for; matrix products, arithmetic and copies ran while one was open for 19% of the time, Pallas kernels for 0%

profile of v3, /device:TPU:0, one launch (start us, length us, event | category | flops | bytes accessed | tf_op | source)
XLA Modules:
  0.0 381.0 jit_solution(3107016578722737181)
XLA Ops:
  7.2 0.8 fusion.27
  8.8 3.8 convolution_convert_fusion
  12.6 7.7 %all-to-all-start = ((bf16[32,40,2048]{2,1,0:T(8,128)(2,1)}), bf16[32,40,2048]{2,1,0:T(8,128)(2,1)}, u32[]{:S(2)}, u32[]{:S(2)}) async-start(bf16[32,40,2048]{2,1,0:T(8,128)(2,1)} %bitcast.82), calls=%async_computation | async-start | bytes 10485760 | tf_op jit(solution)/shard_map/all_to_all | solution.py:49
  20.8 3.9 %multiply_convert_fusion = bf16[1280,2048]{1,0:T(8,128)(2,1)} fusion(pred[128,1280]{0,1:T(32,128)(4,1)S(1)} %compare_and_fusion, bf16[128,2048]{1,0:T(8,128)(2,1)S(1)} %copy-done, f32[1280]{0:T(1024)S(1)} %mul.62), kind=kOutput, calls=%fused_computation.1 | convolution fusion | flops 676331520 | bytes 5936128 | tf_op jit(solution)/shard_map/dot_general | solution.py:44
  24.7 61.5 %all-to-all-done = bf16[32,40,2048]{2,1,0:T(8,128)(2,1)} async-done(((bf16[32,40,2048]{2,1,0:T(8,128)(2,1)}), bf16[32,40,2048]{2,1,0:T(8,128)(2,1)}, u32[]{:S(2)}, u32[]{:S(2)}) %all-to-all-start) | async-done | bytes 5242912 | tf_op jit(solution)/shard_map/all_to_all | solution.py:49
  86.2 4.9 %all-to-all-start.1 = ((bf16[32,40,2048]{2,1,0:T(8,128)(2,1)}), bf16[32,40,2048]{2,1,0:T(8,128)(2,1)}, u32[]{:S(2)}, u32[]{:S(2)}) async-start(bf16[32,40,2048]{2,1,0:T(8,128)(2,1)} %bitcast.81), calls=%async_computation.1 | async-start | bytes 10485760 | tf_op jit(solution)/shard_map/all_to_all | solution.py:50
  91.3 3.4 fusion.35
  94.8 7.0 %fusion.1 = f32[768,768]{0,1:T(8,128)S(1)} fusion(bf16[768,2048]{1,0:T(8,128)(2,1)S(1)} %bitcast.93, bf16[2,2048,768]{2,1,0:T(8,128)(2,1)} %param.11), kind=kOutput, calls=%fused_computation.14 | convolution fusion | flops 2415919104 | bytes 8650752 | tf_op jit(solution)/shard_map/dot_general | solution.py:58
  101.8 1.4 copy-done.8
  103.6 1.8 convolution_convert_fusion.5
  106.2 2.7 fusion.4
  109.3 1.8 convolution_convert_fusion.6
  111.5 3.1 pad_maximum_fusion.1
  114.5 42.4 %all-to-all-done.1 = bf16[32,40,2048]{2,1,0:T(8,128)(2,1)} async-done(((bf16[32,40,2048]{2,1,0:T(8,128)(2,1)}), bf16[32,40,2048]{2,1,0:T(8,128)(2,1)}, u32[]{:S(2)}, u32[]{:S(2)}) %all-to-all-start.1) | async-done | bytes 5242912 | tf_op jit(solution)/shard_map/all_to_all | solution.py:50
  157.0 3.3 slice_select_fusion.1
  160.5 1.4 copy-done.20
  161.9 1.7 multiply_convert_fusion.2
  164.3 1.7 multiply_convert_fusion.4
  166.2 2.9 fusion.7
  169.2 2.9 fusion.6
  172.1 3.2 pad_maximum_fusion
  175.3 4.9 %all-to-all-start.2 = ((bf16[32,40,2048]{2,1,0:T(8,128)(2,1)}), bf16[32,40,2048]{2,1,0:T(8,128)(2,1)}, u32[]{:S(2)}, u32[]{:S(2)}) async-start(bf16[32,40,2048]{2,1,0:T(8,128)(2,1)} %pad_maximum_fusion.1), calls=%async_computation.2 | async-start | bytes 10485760 | tf_op jit(solution)/shard_map/all_to_all | solution.py:77
  180.3 4.0 %fusion.13 = bf16[1,384,2048]{2,1,0:T(8,128)(2,1)S(1)} fusion(bf16[768,384]{0,1:T(8,128)(2,1)S(1)} %multiply_convert_fusion.5, bf16[768,2048]{1,0:T(8,128)(2,1)} %bitcast.98), kind=kOutput, calls=%fused_computation.30 | convolution fusion | flops 1208745984 | bytes 5308416 | tf_op jit(solution)/shard_map/dot_general | solution.py:95
  184.3 1.4 fusion.12
  185.7 1.9 pad_maximum_fusion.3
  187.7 1.0 copy-done.23
  188.7 5.1 %convolution_convert_fusion.3 = bf16[768,2048]{1,0:T(8,128)(2,1)S(1)} fusion(bf16[2,2048,768]{2,1,0:T(8,128)(2,1)} %param.11, bf16[768,384]{0,1:T(8,128)(2,1)S(1)} %copy-done.23, bf16[768,384]{0,1:T(8,128)(2,1)S(1)} %get-tuple-element.24), kind=kOutput, calls=%fused_computation.8 | convolution fusion | flops 2419851264 | bytes 7471104 | tf_op jit(solution)/shard_map/dot_general | solution.py:90
  194.0 0.9 copy-done.25
  195.1 4.9 %convolution_convert_fusion.4 = bf16[768,2048]{1,0:T(8,128)(2,1)S(1)} fusion(bf16[2,2048,768]{2,1,0:T(8,128)(2,1)} %param.11, bf16[768,384]{0,1:T(8,128)(2,1)S(1)} %copy-done.27, bf16[768,384]{0,1:T(8,128)(2,1)S(1)} %copy-done.25), kind=kOutput, calls=%fused_computation.9 | convolution fusion | flops 2419851264 | bytes 7471104 | tf_op jit(solution)/shard_map/dot_general | solution.py:90
  200.4 2.8 pad_maximum_fusion.2
  203.2 34.1 %reduce-scatter.3.cloned.1.call-done = bf16[2,512,768]{2,1,0:T(8,128)(2,1)} async-done(((bf16[2,2048,768]{2,1,0:T(8,128)(2,1)}), bf16[2,512,768]{2,1,0:T(8,128)(2,1)}) %reduce-scatter.3.cloned.1.call-update) | async-done | bytes 1572880 | tf_op jit(solution)/shard_map/reduce_scatter | solution.py:98
  237.3 8.8 %all-to-all-done.2 = bf16[32,40,2048]{2,1,0:T(8,128)(2,1)} async-done(((bf16[32,40,2048]{2,1,0:T(8,128)(2,1)}), bf16[32,40,2048]{2,1,0:T(8,128)(2,1)}, u32[]{:S(2)}, u32[]{:S(2)}) %all-to-all-start.2) | async-done | bytes 5242912 | tf_op jit(solution)/shard_map/all_to_all | solution.py:77
  246.1 4.9 %all-to-all-start.3 = ((bf16[32,40,2048]{2,1,0:T(8,128)(2,1)}), bf16[32,40,2048]{2,1,0:T(8,128)(2,1)}, u32[]{:S(2)}, u32[]{:S(2)}) async-start(bf16[32,40,2048]{2,1,0:T(8,128)(2,1)} %pad_maximum_fusion.2), calls=%async_computation.4 | async-start | bytes 10485760 | tf_op jit(solution)/shard_map/all_to_all | solution.py:105
  251.1 0.8 select_reduce_fusion
  252.1 1.7 collective-permute-start
  253.8 0.9 fusion.26
  254.8 0.7 and.54
  255.5 0.6 fusion.30
  256.8 21.6 %reduce-scatter.5.cloned.1.call-done = bf16[2,384,512]{2,1,0:T(8,128)(2,1)} async-done(((bf16[2,384,2048]{2,1,0:T(8,128)(2,1)}), bf16[2,384,512]{2,1,0:T(8,128)(2,1)}) %reduce-scatter.5.cloned.1.call-update) | async-done | bytes 786448 | tf_op jit(solution)/shard_map/reduce_scatter | solution.py:101
  278.4 1.5 collective-permute-start.1
  279.8 4.0 %convolution_bitcast_fusion = f32[128,1280]{0,1:T(8,128)S(1)} fusion(bf16[1280,2048]{1,0:T(8,128)(2,1)} %bitcast.10, bf16[128,2048]{1,0:T(8,128)(2,1)S(1)} %copy-done), kind=kOutput, calls=%fused_computation.31 | convolution fusion | flops 671088640 | bytes 6422528 | tf_op jit(solution)/shard_map/dot_general | solution.py:116
  283.9 7.0 %gather_fusion = f32[1024]{0:T(1024)S(1)} fusion(f32[128,1280]{0,1:T(8,128)S(1)} %convolution_bitcast_fusion, s32[1024]{0:T(1024)S(1)} %reshape.178), kind=kCustom, calls=%fused_computation | custom fusion | bytes 16384 | tf_op jit(solution)/shard_map/jit(take_along_axis)/gather | solution.py:119
  291.0 0.6 and_select_fusion
  291.7 5.7 %convolution_convert_fusion.10 = bf16[128,2048]{1,0:T(8,128)(2,1)} fusion(f32[128,1280]{0,1:T(8,128)S(1)} %select_n.84, bf16[1280,2048]{1,0:T(8,128)(2,1)} %bitcast.10), kind=kOutput, calls=%fused_computation.33 | convolution fusion | flops 4026793984 | bytes 6422528 | tf_op jit(solution)/shard_map/dot_general | solution.py:112
  297.4 66.5 %collective-permute-done.1 = bf16[2,384,512]{2,1,0:T(8,128)(2,1)} collective-permute-done((bf16[2,384,512]{2,1,0:T(8,128)(2,1)}, bf16[2,384,512]{2,1,0:T(8,128)(2,1)}, u32[]{:S(2)}, u32[]{:S(2)}) %collective-permute-start.1) | collective-permute-done | bytes 786464 | tf_op jit(solution)/shard_map/ppermute | solution.py:18
  363.8 2.4 select_convert_fusion.1
  366.2 3.3 select_convert_fusion
  369.5 4.2 %convolution_convert_fusion.9 = bf16[128,2048]{1,0:T(8,128)(2,1)} fusion(pred[128,1280]{0,1:T(32,128)(4,1)S(1)} %copy-done.14, bf16[1280,2048]{1,0:T(8,128)(2,1)} %bitcast.19), kind=kOutput, calls=%fused_computation.32 | convolution fusion | flops 671350784 | bytes 5931008 | tf_op jit(solution)/shard_map/dot_general | solution.py:120
  (91 shorter events, 5.3 us)
Async XLA Ops:
  7.2 13.6 %copy-start = (bf16[128,2048]{1,0:T(8,128)(2,1)S(1)}, bf16[128,2048]{1,0:T(8,128)(2,1)}, u32[]{:S(2)}) copy-start(bf16[128,2048]{1,0:T(8,128)(2,1)} %param.10) | copy-start | bytes 1572868
  7.2 1.6 copy-start.16
  8.2 12.2 %copy-start.15 = (s32[128,64]{0,1:T(8,128)}, s32[128,64]{0,1:T(8,128)S(1)}, u32[]{:S(2)}) copy-start(s32[128,64]{0,1:T(8,128)S(1)} %subtract_select_fusion) | copy-start | bytes 98308
  12.6 7.7 %copy-start.17 = (s32[128,8]{0,1:T(8,128)S(1)}, s32[128,8]{0,1:T(8,128)}, u32[]{:S(2)}) copy-start(s32[128,8]{0,1:T(8,128)} %param.8) | copy-start | bytes 12292
  12.6 7.7 %copy-start.18 = (f32[128,8]{0,1:T(8,128)S(1)}, f32[128,8]{0,1:T(8,128)}, u32[]{:S(2)}) copy-start(f32[128,8]{0,1:T(8,128)} %param.9) | copy-start | bytes 12292
  12.6 73.6 %all-to-all-start = ((bf16[32,40,2048]{2,1,0:T(8,128)(2,1)}), bf16[32,40,2048]{2,1,0:T(8,128)(2,1)}, u32[]{:S(2)}, u32[]{:S(2)}) async-start(bf16[32,40,2048]{2,1,0:T(8,128)(2,1)} %bitcast.82), calls=%async_computation | async-start | bytes 10485760 | tf_op jit(solution)/shard_map/all_to_all | solution.py:49
  86.2 70.8 %all-to-all-start.1 = ((bf16[32,40,2048]{2,1,0:T(8,128)(2,1)}), bf16[32,40,2048]{2,1,0:T(8,128)(2,1)}, u32[]{:S(2)}, u32[]{:S(2)}) async-start(bf16[32,40,2048]{2,1,0:T(8,128)(2,1)} %bitcast.81), calls=%async_computation.1 | async-start | bytes 10485760 | tf_op jit(solution)/shard_map/all_to_all | solution.py:50
  91.1 146.2 %reduce-scatter.3.cloned.1.call-start = ((), (), s32[]{:S(2)}) async-start(), calls=%async_computation.6 | async-start | bytes 7864320 | tf_op jit(solution)/shard_map/reduce_scatter | solution.py:98
  94.8 7.0 %copy-start.3 = (bf16[32,24,2048]{2,1,0:T(8,128)(2,1)}, bf16[32,24,2048]{2,1,0:T(8,128)(2,1)S(1)}, u32[]{:S(2)}) copy-start(bf16[32,24,2048]{2,1,0:T(8,128)(2,1)S(1)} %get-tuple-element.21) | copy-start | bytes 9437188
  94.8 10.8 %copy-start.1 = (bf16[32,24,2048]{2,1,0:T(8,128)(2,1)}, bf16[32,24,2048]{2,1,0:T(8,128)(2,1)S(1)}, u32[]{:S(2)}) copy-start(bf16[32,24,2048]{2,1,0:T(8,128)(2,1)S(1)} %get-tuple-element.20) | copy-start | bytes 9437188
  94.8 8.8 %copy-start.19 = (bf16[2,384,2048]{2,1,0:T(8,128)(2,1)S(1)}, bf16[2,384,2048]{2,1,0:T(8,128)(2,1)}, u32[]{:S(2)}) copy-start(bf16[2,384,2048]{2,1,0:T(8,128)(2,1)} %param.12) | copy-start | bytes 9437188
  101.8 1.4 copy-start.8
  103.2 2.4 slice-start
  103.6 2.6 slice-start.1
  108.9 2.2 copy-start.10
  157.0 3.5 copy-start.9
  157.0 5.0 %copy-start.20 = (bf16[2,384,2048]{2,1,0:T(8,128)(2,1)S(1)}, bf16[2,384,2048]{2,1,0:T(8,128)(2,1)}, u32[]{:S(2)}) copy-start(bf16[2,384,2048]{2,1,0:T(8,128)(2,1)} %param.12) | copy-start | bytes 9437188
  160.2 3.4 copy-start.7
  160.3 3.4 copy-start.5
  161.9 2.4 copy-start.11
  163.7 2.4 copy-start.22
  164.3 1.9 copy-start.4
  166.0 3.1 copy-start.24
  166.0 3.1 copy-start.26
  166.2 3.0 copy-start.2
  175.3 70.8 %all-to-all-start.2 = ((bf16[32,40,2048]{2,1,0:T(8,128)(2,1)}), bf16[32,40,2048]{2,1,0:T(8,128)(2,1)}, u32[]{:S(2)}, u32[]{:S(2)}) async-start(bf16[32,40,2048]{2,1,0:T(8,128)(2,1)} %pad_maximum_fusion.1), calls=%async_computation.2 | async-start | bytes 10485760 | tf_op jit(solution)/shard_map/all_to_all | solution.py:77
  180.2 98.1 %reduce-scatter.5.cloned.1.call-start = ((), (), s32[]{:S(2)}) async-start(), calls=%async_computation.7 | async-start | bytes 3932160 | tf_op jit(solution)/shard_map/reduce_scatter | solution.py:101
  180.3 4.0 %copy-start.6 = (bf16[32,24,2048]{2,1,0:T(8,128)(2,1)S(1)}, bf16[32,24,2048]{2,1,0:T(8,128)(2,1)}, u32[]{:S(2)}) copy-start(bf16[32,24,2048]{2,1,0:T(8,128)(2,1)} %copy-done.5) | copy-start | bytes 9437188
  187.7 1.1 copy-start.23
  193.9 1.1 copy-start.25
  193.9 1.2 copy-start.27
  203.2 52.3 %copy-start.21 = (s32[32]{0:T(128)S(1)}, s32[32]{0:T(128)}, u32[]{:S(2)}) copy-start(s32[32]{0:T(128)} %param.13) | copy-start | bytes 388
  237.3 14.8 %copy-start.12 = (bf16[2,512,768]{2,1,0:T(8,128)(2,1)S(1)}, bf16[2,512,768]{2,1,0:T(8,128)(2,1)}, u32[]{:S(2)}) copy-start(bf16[2,512,768]{2,1,0:T(8,128)(2,1)} %reduce-scatter.3.cloned.1.call-done) | copy-start | bytes 4718596
  246.1 123.4 %all-to-all-start.3 = ((bf16[32,40,2048]{2,1,0:T(8,128)(2,1)}), bf16[32,40,2048]{2,1,0:T(8,128)(2,1)}, u32[]{:S(2)}, u32[]{:S(2)}) async-start(bf16[32,40,2048]{2,1,0:T(8,128)(2,1)} %pad_maximum_fusion.2), calls=%async_computation.4 | async-start | bytes 10485760 | tf_op jit(solution)/shard_map/all_to_all | solution.py:105
  252.1 114.1 %collective-permute-start = (bf16[2,512,768]{2,1,0:T(8,128)(2,1)S(1)}, bf16[2,512,768]{2,1,0:T(8,128)(2,1)}, u32[]{:S(2)}, u32[]{:S(2)}) collective-permute-start(bf16[2,512,768]{2,1,0:T(8,128)(2,1)S(1)} %copy-done.12), channel_id=1, source_target_pairs={{0,8},{8,0},{4,12},{12,4},{16,24},{24,16},{20,28},{28,20},{32,40},... | collective-permute-start | bytes 4718600 | tf_op jit(solution)/shard_map/ppermute | solution.py:18
  278.4 85.5 %collective-permute-start.1 = (bf16[2,384,512]{2,1,0:T(8,128)(2,1)}, bf16[2,384,512]{2,1,0:T(8,128)(2,1)}, u32[]{:S(2)}, u32[]{:S(2)}) collective-permute-start(bf16[2,384,512]{2,1,0:T(8,128)(2,1)} %reduce-scatter.5.cloned.1.call-done), channel_id=1, source_target_pairs={{0,8},{8,0},{4,12},{12,4},{16,24},{24,16},{20,28},{28,20},{32,40},... | collective-permute-start | bytes 2359304 | tf_op jit(solution)/shard_map/ppermute | solution.py:18
  291.6 72.2 %copy-start.13 = (bf16[2,384,512]{2,1,0:T(8,128)(2,1)S(1)}, bf16[2,384,512]{2,1,0:T(8,128)(2,1)}, u32[]{:S(2)}) copy-start(bf16[2,384,512]{2,1,0:T(8,128)(2,1)} %reduce-scatter.5.cloned.1.call-done) | copy-start | bytes 2359300
  366.2 3.3 copy-start.14
Sparse Core Ops, SparseCore 0:
  175.5 61.7 reduce-scatter.2
  240.3 38.0 reduce-scatter.4

commit v4 on v3

--- a/solution.py
+++ b/solution.py
@@ -54,17 +54,18 @@
     forwards = []
     for local in range(per_device):
         low = local * shift
-        rows_x = recv_x[:, low:low + window].reshape(groups * window, model_width)
-        projected = jnp.dot(rows_x, weight_in[local], preferred_element_type=jnp.float32)
-        pre_gate = projected[:, :FF]
-        up_part = projected[:, FF:]
+        rows_x = recv_x[:, low:low + window]
+        projected = jnp.einsum("ncd,df->ncf", rows_x, weight_in[local], preferred_element_type=jnp.float32)
+        pre_gate = projected[..., :FF]
+        up_part = projected[..., FF:]
         sigmoid_gate = jax.nn.sigmoid(pre_gate)
         activated = pre_gate * sigmoid_gate
-        hidden = (activated * up_part).astype(jnp.bfloat16)
-        expert_out = jnp.dot(hidden, weight_down[local], preferred_element_type=jnp.float32).astype(
-            jnp.bfloat16
-        )
-        forwards.append((rows_x, pre_gate, up_part, sigmoid_gate, activated, hidden, expert_out))
+        own = (place < CAP) if local == 0 else (place >= window - CAP)
+        hidden = jnp.where(own, activated * up_part, 0.0).astype(jnp.bfloat16)
+        expert_out = jnp.einsum(
+            "ncf,fd->ncd", hidden, weight_down[local], preferred_element_type=jnp.float32
+        ).astype(jnp.bfloat16)
+        forwards.append((rows_x, pre_gate, up_part, sigmoid_gate, activated, hidden, own, expert_out))
 
     def merged(pieces):
         tile = window - shift
@@ -72,27 +73,28 @@
         middle = jnp.where(seam, pieces[0][:, shift:], pieces[1][:, :tile])
         return jnp.concatenate([pieces[0][:, :shift], middle, pieces[1][:, tile:]], axis=1)
 
-    send_out = merged([f[-1].reshape(groups, window, model_width) for f in forwards])
+    send_out = merged([f[-1] for f in forwards])
     send_out, recv_grad = lax.optimization_barrier((send_out, recv_grad))
     home_out = lax.all_to_all(send_out, "expert", split_axis=0, concat_axis=0, tiled=True)
     backs, firsts, seconds = [], [], []
     for local in range(per_device):
         low = local * shift
-        rows_x, pre_gate, up_part, sigmoid_gate, activated, hidden, _ = forwards[local]
-        own = (place < CAP) if local == 0 else (place >= window - CAP)
-        rows_grad = jnp.where(own, recv_grad[:, low:low + window], jnp.zeros((), jnp.bfloat16))
-        rows_grad = rows_grad.reshape(groups * window, model_width)
-        hidden_grad = jnp.dot(rows_grad, weight_down[local].T, preferred_element_type=jnp.float32)
+        rows_x, pre_gate, up_part, sigmoid_gate, activated, hidden, own, _ = forwards[local]
+        rows_grad = recv_grad[:, low:low + window]
+        hidden_grad = jnp.einsum(
+            "ncd,fd->ncf", rows_grad, weight_down[local], preferred_element_type=jnp.float32
+        )
+        hidden_grad = jnp.where(own, hidden_grad, 0.0)
         gate_grad = hidden_grad * up_part * sigmoid_gate * (1.0 + pre_gate * (1.0 - sigmoid_gate))
         proj_grad = jnp.concatenate([gate_grad, hidden_grad * activated], axis=-1).astype(
             jnp.bfloat16
         )
-        row_grad = jnp.dot(proj_grad, weight_in[local].T, preferred_element_type=jnp.float32).astype(
-            jnp.bfloat16
-        )
-        backs.append(row_grad.reshape(groups, window, model_width))
-        firsts.append(jnp.dot(rows_x.T, proj_grad, preferred_element_type=jnp.float32))
-        seconds.append(jnp.dot(hidden.T, rows_grad, preferred_element_type=jnp.float32))
+        row_grad = jnp.einsum(
+            "ncf,df->ncd", proj_grad, weight_in[local], preferred_element_type=jnp.float32
+        ).astype(jnp.bfloat16)
+        backs.append(row_grad)
+        firsts.append(jnp.einsum("ncd,ncf->df", rows_x, proj_grad, preferred_element_type=jnp.float32))
+        seconds.append(jnp.einsum("ncf,ncd->fd", hidden, rows_grad, preferred_element_type=jnp.float32))
     grad_first = jnp.stack(firsts)
     grad_second = jnp.stack(seconds)
     reduced_in = lax.psum_scatter(

time: 386 us -> 390 us (1.010)
  matrix products: 60 us -> 71.6 us
  local copies, waits for them, and re-layouts: 19.2 us -> 14.3 us
    dot_general x12, matrix products: 38.2 us -> 49.8 us  [the longest x2 10.2 us: body(): jnp.einsum('ncd,df->ncf', rows_x, weight_in[local], preferred_element_typ...]
  transfers between devices with their start and end apart: 8 -> 8, of which waited for: 6 -> 6; matrix products, arithmetic and copies ran while one was open for 19% -> 18% of each run, Pallas kernels for 0% -> 0%
where the time goes in v4:
time: 390 us; the launch traced here: 385 us
  waiting for transfers between devices  235 us (60%)
  matrix products  71.6 us (18%)
  starting transfers between devices  26.6 us (7%)
  other arithmetic  22.1 us (6%)
  between operations  15.5 us (4%)
  local copies, waits for them, and re-layouts  14.3 us (4%)
    ppermute x2, waiting for transfers between devices, swapped(): return lax.ppermute(block, axis, route)  66.3 us
    all_to_all x1, waiting for transfers between devices, body(): lax.all_to_all(send_x, 'expert', split_axis=0, concat_axis=0, tiled=True)  61.6 us
    all_to_all x1, waiting for transfers between devices, body(): lax.all_to_all(send_grad, 'expert', split_axis=0, concat_axis=0, tiled=True)  44.2 us
    reduce_scatter x1, waiting for transfers between devices, body(): lax.psum_scatter(grad_first.astype(jnp.bfloat16), 'dp', scatter_dimension...  32.5 us
    reduce_scatter x1, waiting for transfers between devices, body(): lax.psum_scatter(grad_second.astype(jnp.bfloat16), 'dp', scatter_dimensio...  21.6 us
    dot_general x2, matrix products, body(): jnp.einsum('ncd,df->ncf', rows_x, weight_in[local], preferred_element_typ...  10.2 us
    dot_general x2, matrix products, body(): jnp.einsum('ncd,ncf->df', rows_x, proj_grad, preferred_element_type=jnp.f...  9.63 us
    dot_general x2, matrix products, body(): jnp.einsum('ncf,df->ncd', proj_grad, weight_in[local], preferred_element_...  9.62 us
  transfers between devices with their start and end apart: 8, of which 6 were waited for; matrix products, arithmetic and copies ran while one was open for 18% of the time, Pallas kernels for 0%

profile of v4, /device:TPU:0, one launch (start us, length us, event | category | flops | bytes accessed | tf_op | source)
XLA Modules:
  0.0 385.0 jit_solution(1423108387890136888)
XLA Ops:
  7.2 0.8 fusion.49
  8.8 3.9 %convolution_convert_fusion = bf16[1280,2048]{1,0:T(8,128)(2,1)} fusion(pred[128,1280]{0,1:T(32,128)(4,1)S(1)} %compare_and_fusion, bf16[128,2048]{1,0:T(8,128)(2,1)S(1)} %copy-done.8), kind=kOutput, calls=%fused_computation.2 | convolution fusion | flops 673710080 | bytes 5931008 | tf_op jit(solution)/shard_map/dot_general | solution.py:43
  12.7 7.7 %all-to-all-start = ((bf16[32,40,2048]{2,1,0:T(8,128)(2,1)}), bf16[32,40,2048]{2,1,0:T(8,128)(2,1)}, u32[]{:S(2)}, u32[]{:S(2)}) async-start(bf16[32,40,2048]{2,1,0:T(8,128)(2,1)} %bitcast.90), calls=%async_computation | async-start | bytes 10485760 | tf_op jit(solution)/shard_map/all_to_all | solution.py:49
  20.9 3.8 multiply_convert_fusion
  24.7 61.6 %all-to-all-done = bf16[32,40,2048]{2,1,0:T(8,128)(2,1)} async-done(((bf16[32,40,2048]{2,1,0:T(8,128)(2,1)}), bf16[32,40,2048]{2,1,0:T(8,128)(2,1)}, u32[]{:S(2)}, u32[]{:S(2)}) %all-to-all-start) | async-done | bytes 5242912 | tf_op jit(solution)/shard_map/all_to_all | solution.py:49
  86.3 4.9 %all-to-all-start.1 = ((bf16[32,40,2048]{2,1,0:T(8,128)(2,1)}), bf16[32,40,2048]{2,1,0:T(8,128)(2,1)}, u32[]{:S(2)}, u32[]{:S(2)}) async-start(bf16[32,40,2048]{2,1,0:T(8,128)(2,1)} %bitcast.89), calls=%async_computation.1 | async-start | bytes 10485760 | tf_op jit(solution)/shard_map/all_to_all | solution.py:50
  91.1 0.6 reduce-scatter.3.cloned.1.call-start
  91.8 5.6 %fusion.1 = f32[32,24,768]{2,1,0:T(8,128)S(1)} fusion(bf16[32,40,2048]{2,1,0:T(8,128)(2,1)} %all-to-all-done, bf16[2,2048,768]{2,1,0:T(8,128)(2,1)} %param.11), kind=kOutput, calls=%fused_computation.16 | convolution fusion | flops 2415919104 | bytes 8650752 | tf_op jit(solution)/shard_map/ncd,df->ncf/dot_general | solution.py:58
  97.4 1.4 copy-done.3
  99.2 1.8 convolution_convert_fusion.3
  101.2 0.6 slice-done.1
  101.8 4.6 %fusion.4 = f32[32,24,768]{2,1,0:T(8,128)S(1)} fusion(bf16[32,40,2048]{2,1,0:T(8,128)(2,1)} %all-to-all-done, bf16[2,2048,768]{2,1,0:T(8,128)(2,1)S(1)} %bitcast.92), kind=kOutput, calls=%fused_computation.19 | convolution fusion | flops 2415919104 | bytes 8650752 | tf_op jit(solution)/shard_map/ncd,df->ncf/dot_general | solution.py:58
  106.7 1.0 copy-done.1
  107.7 1.8 convolution_convert_fusion.4
  109.9 3.0 pad_maximum_fusion.1
  112.8 44.2 %all-to-all-done.1 = bf16[32,40,2048]{2,1,0:T(8,128)(2,1)} async-done(((bf16[32,40,2048]{2,1,0:T(8,128)(2,1)}), bf16[32,40,2048]{2,1,0:T(8,128)(2,1)}, u32[]{:S(2)}, u32[]{:S(2)}) %all-to-all-start.1) | async-done | bytes 5242912 | tf_op jit(solution)/shard_map/all_to_all | solution.py:50
  157.0 5.3 %multiply_convert_fusion.2 = (bf16[32,24,384]{2,1,0:T(8,128)(2,1)S(1)}, bf16[32,24,384]{2,1,0:T(8,128)(2,1)S(1)}) fusion(f32[32,24,768]{2,1,0:T(8,128)} %copy-done.3, bf16[2,384,2048]{2,1,0:T(8,128)(2,1)} %param.12, bf16[32,40,2048]{2,1,0:T(8,128)(2,1)} %all-to-all-done.1, pred[24]{0:T(512)(128)(4,1)S(1)} %iota_compare_fusion.6), kind=kOutput, calls=%fused_computation.56 | convolution fusion | flops 1212088320 | bytes 8257560 | tf_op jit(solution)/shard_map/ncd,fd->ncf/dot_general | solution.py:84
  162.4 4.2 %multiply_convert_fusion.4 = (bf16[32,24,384]{2,1,0:T(8,128)(2,1)S(1)}, bf16[32,24,384]{2,1,0:T(8,128)(2,1)S(1)}) fusion(f32[32,24,768]{2,1,0:T(8,128)S(1)} %copy-done.2, bf16[2,384,2048]{2,1,0:T(8,128)(2,1)S(1)} %copy-done.12, bf16[32,40,2048]{2,1,0:T(8,128)(2,1)} %all-to-all-done.1, pred[24]{0:T(512)(128)(4,1)S(1)} %iota_compare_fusion.8), kind=kOutput, calls=%fused_computation.58 | convolution fusion | flops 1212088320 | bytes 8258048 | tf_op jit(solution)/shard_map/ncd,fd->ncf/dot_general | solution.py:84
  166.6 5.0 %fusion.7 = bf16[1,2048,768]{2,1,0:T(8,128)(2,1)S(1)} fusion(bf16[32,40,2048]{2,1,0:T(8,128)(2,1)} %all-to-all-done, bf16[32,24,384]{2,1,0:T(8,128)(2,1)S(1)} %get-tuple-element.21, bf16[32,24,384]{2,1,0:T(8,128)(2,1)S(1)} %get-tuple-element.20), kind=kOutput, calls=%fused_computation.22 | convolution fusion | flops 2419851264 | bytes 7471104 | tf_op jit(solution)/shard_map/ncd,ncf->df/dot_general | solution.py:96
  171.7 4.6 %fusion.6 = bf16[1,2048,768]{2,1,0:T(8,128)(2,1)S(1)} fusion(bf16[32,40,2048]{2,1,0:T(8,128)(2,1)} %all-to-all-done, bf16[32,24,384]{2,1,0:T(8,128)(2,1)S(1)} %get-tuple-element.19, bf16[32,24,384]{2,1,0:T(8,128)(2,1)S(1)} %get-tuple-element.18), kind=kOutput, calls=%fused_computation.21 | convolution fusion | flops 2419851264 | bytes 7471104 | tf_op jit(solution)/shard_map/ncd,ncf->df/dot_general | solution.py:96
  176.3 3.2 pad_maximum_fusion
  179.5 4.9 %all-to-all-start.2 = ((bf16[32,40,2048]{2,1,0:T(8,128)(2,1)}), bf16[32,40,2048]{2,1,0:T(8,128)(2,1)}, u32[]{:S(2)}, u32[]{:S(2)}) async-start(bf16[32,40,2048]{2,1,0:T(8,128)(2,1)} %pad_maximum_fusion.1), calls=%async_computation.2 | async-start | bytes 10485760 | tf_op jit(solution)/shard_map/all_to_all | solution.py:78
  184.7 4.0 %fusion.25 = bf16[1,384,2048]{2,1,0:T(8,128)(2,1)S(1)} fusion(bf16[32,24,384]{2,1,0:T(8,128)(2,1)S(1)} %select_convert_fusion.1, bf16[32,40,2048]{2,1,0:T(8,128)(2,1)} %all-to-all-done.1), kind=kOutput, calls=%fused_computation.38 | convolution fusion | flops 1208745984 | bytes 5308416 | tf_op jit(solution)/shard_map/ncf,ncd->fd/dot_general | solution.py:97
  188.6 3.3 fusion.22
  192.0 1.9 pad_maximum_fusion.3
  193.9 1.0 copy-done.15
  195.0 4.9 %convolution_convert_fusion.1 = bf16[32,24,2048]{2,1,0:T(8,128)(2,1)S(1)} fusion(bf16[2,2048,768]{2,1,0:T(8,128)(2,1)} %param.11, bf16[32,24,384]{2,1,0:T(8,128)(2,1)S(1)} %copy-done.15, bf16[32,24,384]{2,1,0:T(8,128)(2,1)S(1)} %get-tuple-element.20), kind=kOutput, calls=%fused_computation.8 | convolution fusion | flops 2419851264 | bytes 7471104 | tf_op jit(solution)/shard_map/ncf,df->ncd/dot_general | solution.py:92
  200.0 0.9 copy-done.17
  201.1 4.8 %convolution_convert_fusion.2 = bf16[32,24,2048]{2,1,0:T(8,128)(2,1)S(1)} fusion(bf16[2,2048,768]{2,1,0:T(8,128)(2,1)} %param.11, bf16[32,24,384]{2,1,0:T(8,128)(2,1)S(1)} %copy-done.19, bf16[32,24,384]{2,1,0:T(8,128)(2,1)S(1)} %copy-done.17), kind=kOutput, calls=%fused_computation.9 | convolution fusion | flops 2419851264 | bytes 7471104 | tf_op jit(solution)/shard_map/ncf,df->ncd/dot_general | solution.py:92
  206.2 2.8 pad_maximum_fusion.2
  209.0 32.5 %reduce-scatter.3.cloned.1.call-done = bf16[2,512,768]{2,1,0:T(8,128)(2,1)} async-done(((bf16[2,2048,768]{2,1,0:T(8,128)(2,1)}), bf16[2,512,768]{2,1,0:T(8,128)(2,1)}) %reduce-scatter.3.cloned.1.call-update) | async-done | bytes 1572880 | tf_op jit(solution)/shard_map/reduce_scatter | solution.py:100
  241.5 8.8 %all-to-all-done.2 = bf16[32,40,2048]{2,1,0:T(8,128)(2,1)} async-done(((bf16[32,40,2048]{2,1,0:T(8,128)(2,1)}), bf16[32,40,2048]{2,1,0:T(8,128)(2,1)}, u32[]{:S(2)}, u32[]{:S(2)}) %all-to-all-start.2) | async-done | bytes 5242912 | tf_op jit(solution)/shard_map/all_to_all | solution.py:78
  250.3 4.9 %all-to-all-start.3 = ((bf16[32,40,2048]{2,1,0:T(8,128)(2,1)}), bf16[32,40,2048]{2,1,0:T(8,128)(2,1)}, u32[]{:S(2)}, u32[]{:S(2)}) async-start(bf16[32,40,2048]{2,1,0:T(8,128)(2,1)} %pad_maximum_fusion.2), calls=%async_computation.4 | async-start | bytes 10485760 | tf_op jit(solution)/shard_map/all_to_all | solution.py:107
  255.3 0.8 select_reduce_fusion
  256.3 1.7 collective-permute-start
  258.0 0.9 fusion.48
  259.0 0.7 and.54
  259.7 0.6 fusion.52
  261.0 21.6 %reduce-scatter.5.cloned.1.call-done = bf16[2,384,512]{2,1,0:T(8,128)(2,1)} async-done(((bf16[2,384,2048]{2,1,0:T(8,128)(2,1)}), bf16[2,384,512]{2,1,0:T(8,128)(2,1)}) %reduce-scatter.5.cloned.1.call-update) | async-done | bytes 786448 | tf_op jit(solution)/shard_map/reduce_scatter | solution.py:103
  282.5 1.7 collective-permute-start.1
  284.2 4.0 %convolution_bitcast_fusion = f32[128,1280]{0,1:T(8,128)S(1)} fusion(bf16[1280,2048]{1,0:T(8,128)(2,1)} %bitcast.10, bf16[128,2048]{1,0:T(8,128)(2,1)S(1)} %copy-done), kind=kOutput, calls=%fused_computation.39 | convolution fusion | flops 671088640 | bytes 6422528 | tf_op jit(solution)/shard_map/dot_general | solution.py:118
  288.3 7.0 %gather_fusion = f32[1024]{0:T(1024)S(1)} fusion(f32[128,1280]{0,1:T(8,128)S(1)} %convolution_bitcast_fusion, s32[1024]{0:T(1024)S(1)} %reshape.146), kind=kCustom, calls=%fused_computation | custom fusion | bytes 16384 | tf_op jit(solution)/shard_map/jit(take_along_axis)/gather | solution.py:121
  295.4 0.6 and_select_fusion
  296.1 5.7 %convolution_convert_fusion.6 = bf16[128,2048]{1,0:T(8,128)(2,1)} fusion(f32[128,1280]{0,1:T(8,128)S(1)} %select_n.90, bf16[1280,2048]{1,0:T(8,128)(2,1)} %bitcast.10), kind=kOutput, calls=%fused_computation.41 | convolution fusion | flops 4026793984 | bytes 6422528 | tf_op jit(solution)/shard_map/dot_general | solution.py:114
  301.8 66.2 %collective-permute-done.1 = bf16[2,384,512]{2,1,0:T(8,128)(2,1)} collective-permute-done((bf16[2,384,512]{2,1,0:T(8,128)(2,1)}, bf16[2,384,512]{2,1,0:T(8,128)(2,1)}, u32[]{:S(2)}, u32[]{:S(2)}) %collective-permute-start.1) | collective-permute-done | bytes 786464 | tf_op jit(solution)/shard_map/ppermute | solution.py:18
  368.0 2.4 select_convert_fusion.3
  370.4 3.3 select_convert_fusion
  373.7 4.2 %convolution_convert_fusion.5 = bf16[128,2048]{1,0:T(8,128)(2,1)} fusion(pred[128,1280]{0,1:T(32,128)(4,1)S(1)} %copy-done.6, bf16[1280,2048]{1,0:T(8,128)(2,1)} %bitcast.17), kind=kOutput, calls=%fused_computation.40 | convolution fusion | flops 671350784 | bytes 5931008 | tf_op jit(solution)/shard_map/dot_general | solution.py:122
  (74 shorter events, 3.8 us)
Async XLA Ops:
  7.2 13.7 %copy-start = (bf16[128,2048]{1,0:T(8,128)(2,1)S(1)}, bf16[128,2048]{1,0:T(8,128)(2,1)}, u32[]{:S(2)}) copy-start(bf16[128,2048]{1,0:T(8,128)(2,1)} %param.10) | copy-start | bytes 1572868
  7.2 1.6 copy-start.8
  8.2 12.3 %copy-start.7 = (s32[128,64]{0,1:T(8,128)}, s32[128,64]{0,1:T(8,128)S(1)}, u32[]{:S(2)}) copy-start(s32[128,64]{0,1:T(8,128)S(1)} %subtract_select_fusion) | copy-start | bytes 98308
  12.7 7.7 %copy-start.9 = (s32[128,8]{0,1:T(8,128)S(1)}, s32[128,8]{0,1:T(8,128)}, u32[]{:S(2)}) copy-start(s32[128,8]{0,1:T(8,128)} %param.8) | copy-start | bytes 12292
  12.7 7.7 %copy-start.10 = (f32[128,8]{0,1:T(8,128)S(1)}, f32[128,8]{0,1:T(8,128)}, u32[]{:S(2)}) copy-start(f32[128,8]{0,1:T(8,128)} %param.9) | copy-start | bytes 12292
  12.7 73.6 %all-to-all-start = ((bf16[32,40,2048]{2,1,0:T(8,128)(2,1)}), bf16[32,40,2048]{2,1,0:T(8,128)(2,1)}, u32[]{:S(2)}, u32[]{:S(2)}) async-start(bf16[32,40,2048]{2,1,0:T(8,128)(2,1)} %bitcast.90), calls=%async_computation | async-start | bytes 10485760 | tf_op jit(solution)/shard_map/all_to_all | solution.py:49
  86.3 70.8 %all-to-all-start.1 = ((bf16[32,40,2048]{2,1,0:T(8,128)(2,1)}), bf16[32,40,2048]{2,1,0:T(8,128)(2,1)}, u32[]{:S(2)}, u32[]{:S(2)}) async-start(bf16[32,40,2048]{2,1,0:T(8,128)(2,1)} %bitcast.89), calls=%async_computation.1 | async-start | bytes 10485760 | tf_op jit(solution)/shard_map/all_to_all | solution.py:50
  91.1 150.3 %reduce-scatter.3.cloned.1.call-start = ((), (), s32[]{:S(2)}) async-start(), calls=%async_computation.6 | async-start | bytes 7864320 | tf_op jit(solution)/shard_map/reduce_scatter | solution.py:100
  91.8 7.4 %copy-start.11 = (bf16[2,384,2048]{2,1,0:T(8,128)(2,1)S(1)}, bf16[2,384,2048]{2,1,0:T(8,128)(2,1)}, u32[]{:S(2)}) copy-start(bf16[2,384,2048]{2,1,0:T(8,128)(2,1)} %param.12) | copy-start | bytes 9437188
  97.4 1.4 copy-start.3
  98.8 2.4 slice-start
  99.2 2.6 slice-start.1
  106.3 1.4 copy-start.1
  157.0 5.3 %copy-start.2 = (f32[32,24,768]{2,1,0:T(8,128)S(1)}, f32[32,24,768]{2,1,0:T(8,128)}, u32[]{:S(2)}) copy-start(f32[32,24,768]{2,1,0:T(8,128)} %copy-done.1) | copy-start | bytes 7077892
  157.0 5.3 %copy-start.12 = (bf16[2,384,2048]{2,1,0:T(8,128)(2,1)S(1)}, bf16[2,384,2048]{2,1,0:T(8,128)(2,1)}, u32[]{:S(2)}) copy-start(bf16[2,384,2048]{2,1,0:T(8,128)(2,1)} %param.12) | copy-start | bytes 9437188
  162.4 4.3 %copy-start.14 = (bf16[32,24,384]{2,1,0:T(8,128)(2,1)}, bf16[32,24,384]{2,1,0:T(8,128)(2,1)S(1)}, u32[]{:S(2)}) copy-start(bf16[32,24,384]{2,1,0:T(8,128)(2,1)S(1)} %get-tuple-element.21) | copy-start | bytes 1769476
  166.6 5.1 %copy-start.16 = (bf16[32,24,384]{2,1,0:T(8,128)(2,1)}, bf16[32,24,384]{2,1,0:T(8,128)(2,1)S(1)}, u32[]{:S(2)}) copy-start(bf16[32,24,384]{2,1,0:T(8,128)(2,1)S(1)} %get-tuple-element.18) | copy-start | bytes 1769476
  166.6 5.1 %copy-start.18 = (bf16[32,24,384]{2,1,0:T(8,128)(2,1)}, bf16[32,24,384]{2,1,0:T(8,128)(2,1)S(1)}, u32[]{:S(2)}) copy-start(bf16[32,24,384]{2,1,0:T(8,128)(2,1)S(1)} %get-tuple-element.19) | copy-start | bytes 1769476
  179.5 70.8 %all-to-all-start.2 = ((bf16[32,40,2048]{2,1,0:T(8,128)(2,1)}), bf16[32,40,2048]{2,1,0:T(8,128)(2,1)}, u32[]{:S(2)}, u32[]{:S(2)}) async-start(bf16[32,40,2048]{2,1,0:T(8,128)(2,1)} %pad_maximum_fusion.1), calls=%async_computation.2 | async-start | bytes 10485760 | tf_op jit(solution)/shard_map/all_to_all | solution.py:78
  184.4 98.1 %reduce-scatter.5.cloned.1.call-start = ((), (), s32[]{:S(2)}) async-start(), calls=%async_computation.7 | async-start | bytes 3932160 | tf_op jit(solution)/shard_map/reduce_scatter | solution.py:103
  193.9 1.1 copy-start.15
  199.8 1.1 copy-start.17
  199.8 1.2 copy-start.19
  209.0 50.7 %copy-start.13 = (s32[32]{0:T(128)S(1)}, s32[32]{0:T(128)}, u32[]{:S(2)}) copy-start(s32[32]{0:T(128)} %param.13) | copy-start | bytes 388
  241.5 14.8 %copy-start.4 = (bf16[2,512,768]{2,1,0:T(8,128)(2,1)S(1)}, bf16[2,512,768]{2,1,0:T(8,128)(2,1)}, u32[]{:S(2)}) copy-start(bf16[2,512,768]{2,1,0:T(8,128)(2,1)} %reduce-scatter.3.cloned.1.call-done) | copy-start | bytes 4718596
  250.3 123.4 %all-to-all-start.3 = ((bf16[32,40,2048]{2,1,0:T(8,128)(2,1)}), bf16[32,40,2048]{2,1,0:T(8,128)(2,1)}, u32[]{:S(2)}, u32[]{:S(2)}) async-start(bf16[32,40,2048]{2,1,0:T(8,128)(2,1)} %pad_maximum_fusion.2), calls=%async_computation.4 | async-start | bytes 10485760 | tf_op jit(solution)/shard_map/all_to_all | solution.py:107
  256.3 114.1 %collective-permute-start = (bf16[2,512,768]{2,1,0:T(8,128)(2,1)S(1)}, bf16[2,512,768]{2,1,0:T(8,128)(2,1)}, u32[]{:S(2)}, u32[]{:S(2)}) collective-permute-start(bf16[2,512,768]{2,1,0:T(8,128)(2,1)S(1)} %copy-done.4), channel_id=1, source_target_pairs={{0,8},{8,0},{4,12},{12,4},{16,24},{24,16},{20,28},{28,20},{32,40},... | collective-permute-start | bytes 4718600 | tf_op jit(solution)/shard_map/ppermute | solution.py:18
  282.5 85.5 %collective-permute-start.1 = (bf16[2,384,512]{2,1,0:T(8,128)(2,1)}, bf16[2,384,512]{2,1,0:T(8,128)(2,1)}, u32[]{:S(2)}, u32[]{:S(2)}) collective-permute-start(bf16[2,384,512]{2,1,0:T(8,128)(2,1)} %reduce-scatter.5.cloned.1.call-done), channel_id=1, source_target_pairs={{0,8},{8,0},{4,12},{12,4},{16,24},{24,16},{20,28},{28,20},{32,40},... | collective-permute-start | bytes 2359304 | tf_op jit(solution)/shard_map/ppermute | solution.py:18
  296.1 72.0 %copy-start.5 = (bf16[2,384,512]{2,1,0:T(8,128)(2,1)S(1)}, bf16[2,384,512]{2,1,0:T(8,128)(2,1)}, u32[]{:S(2)}) copy-start(bf16[2,384,512]{2,1,0:T(8,128)(2,1)} %reduce-scatter.5.cloned.1.call-done) | copy-start | bytes 2359300
  370.4 3.3 copy-start.6
Sparse Core Ops, SparseCore 0:
  179.6 61.7 reduce-scatter.2
  244.5 38.0 reduce-scatter.4

commit v5 on v3

--- a/solution.py
+++ b/solution.py
@@ -46,8 +46,11 @@
     lanes = per_device * CAP
     send_x = send_x.reshape(groups, lanes, model_width)
     send_grad = send_grad.reshape(groups, lanes, model_width)
-    recv_x = lax.all_to_all(send_x, "expert", split_axis=0, concat_axis=0, tiled=True)
-    recv_grad = lax.all_to_all(send_grad, "expert", split_axis=0, concat_axis=0, tiled=True)
+    recv_both = lax.all_to_all(
+        jnp.concatenate([send_x, send_grad], axis=1), "expert", split_axis=0, concat_axis=0, tiled=True
+    )
+    recv_x = recv_both[:, :lanes]
+    recv_grad = recv_both[:, lanes:]
     window = CAP + 4
     shift = lanes - window
     place = jnp.arange(window, dtype=jnp.int32)[None, :, None]

time: 386 us -> 411 us (1.065)
  waiting for transfers between devices: 235 us -> 265 us
  matrix products: 60 us -> 53.7 us
  starting transfers between devices: 25.8 us -> 20.8 us
  other arithmetic: 25.4 us -> 30.3 us
    all_to_all x2 -> x1, waiting for transfers between devices: 104 us -> 133 us  [body(): lax.all_to_all(jnp.concatenate([send_x, send_grad], axis=1), 'expert', sp...]
    concatenate x0 -> x1, other arithmetic: none -> 7.6 us  [body(): jnp.concatenate([send_x, send_grad], axis=1)]
    all_to_all x2 -> x1, starting transfers between devices: 12.6 us -> 7.54 us  [body(): lax.all_to_all(jnp.concatenate([send_x, send_grad], axis=1), 'expert', sp...]
  transfers between devices with their start and end apart: 8 -> 7, of which waited for: 6 -> 5; matrix products, arithmetic and copies ran while one was open for 19% -> 12% of each run, Pallas kernels for 0% -> 0%
where the time goes in v5:
time: 411 us; the launch traced here: 405 us
  waiting for transfers between devices  265 us (64%)
  matrix products  53.7 us (13%)
  other arithmetic  30.3 us (7%)
  starting transfers between devices  20.8 us (5%)
  local copies, waits for them, and re-layouts  20 us (5%)
  between operations  15.7 us (4%)
    all_to_all x1, waiting for transfers between devices, body(): lax.all_to_all(jnp.concatenate([send_x, send_grad], axis=1), 'expert', sp...  133 us
    ppermute x2, waiting for transfers between devices, swapped(): return lax.ppermute(block, axis, route)  66.5 us
    reduce_scatter x1, waiting for transfers between devices, body(): lax.psum_scatter(grad_first.astype(jnp.bfloat16), 'dp', scatter_dimension...  33.9 us
    reduce_scatter x1, waiting for transfers between devices, body(): lax.psum_scatter(grad_second.astype(jnp.bfloat16), 'dp', scatter_dimensio...  22.2 us
    dot_general x2, matrix products, body(): jnp.dot(proj_grad, weight_in[local].T, preferred_element_type=jnp.float32)  10 us
    all_to_all x1, waiting for transfers between devices, body(): lax.all_to_all(send_out, 'expert', split_axis=0, concat_axis=0, tiled=True)  8.93 us
  transfers between devices with their start and end apart: 7, of which 5 were waited for; matrix products, arithmetic and copies ran while one was open for 12% of the time, Pallas kernels for 0%

profile of v5, /device:TPU:0, one launch (start us, length us, event | category | flops | bytes accessed | tf_op | source)
XLA Modules:
  0.0 405.3 jit_solution(2761530618696694125)
XLA Ops:
  7.2 0.8 fusion.27
  8.0 0.7 select_reduce_fusion.1
  10.0 1.5 convolution_convert_fusion
  11.5 1.5 multiply_convert_fusion
  13.1 7.6 %pad_maximum_fusion = bf16[32,80,2048]{2,1,0:T(8,128)(2,1)} fusion(bf16[32,40,2048]{2,1,0:T(8,128)(2,1)S(1)} %bitcast.81, bf16[32,40,2048]{2,1,0:T(8,128)(2,1)S(1)} %bitcast.82), kind=kLoop, calls=%fused_computation.1 | loop fusion | flops 20971520 | bytes 20971520 | tf_op jit(solution)/shard_map/concatenate | solution.py:50
  20.7 7.5 %all-to-all-start = ((bf16[32,80,2048]{2,1,0:T(8,128)(2,1)}), bf16[32,80,2048]{2,1,0:T(8,128)(2,1)}, u32[]{:S(2)}, u32[]{:S(2)}) async-start(bf16[32,80,2048]{2,1,0:T(8,128)(2,1)} %pad_maximum_fusion), calls=%async_computation | async-start | bytes 20971520 | tf_op jit(solution)/shard_map/all_to_all | solution.py:49
  28.5 133.2 %all-to-all-done = bf16[32,80,2048]{2,1,0:T(8,128)(2,1)} async-done(((bf16[32,80,2048]{2,1,0:T(8,128)(2,1)}), bf16[32,80,2048]{2,1,0:T(8,128)(2,1)}, u32[]{:S(2)}, u32[]{:S(2)}) %all-to-all-start) | async-done | bytes 10485792 | tf_op jit(solution)/shard_map/all_to_all | solution.py:49
  161.6 3.6 fusion.35
  165.2 4.9 %fusion.1 = f32[768,768]{0,1:T(8,128)S(1)} fusion(bf16[768,2048]{1,0:T(8,128)(2,1)S(1)} %bitcast.97, bf16[2,2048,768]{2,1,0:T(8,128)(2,1)} %param.11), kind=kOutput, calls=%fused_computation.15 | convolution fusion | flops 2415919104 | bytes 8650752 | tf_op jit(solution)/shard_map/dot_general | solution.py:61
  170.1 0.4 multiply_convert_fusion.5
  170.5 2.9 fusion.4
  173.4 0.4 multiply_convert_fusion.6
  173.7 1.8 convolution_convert_fusion.6
  175.7 1.8 convolution_convert_fusion.5
  177.9 3.1 pad_maximum_fusion.2
  181.0 2.9 slice.103
  183.9 0.6 slice_select_fusion.1
  184.5 2.1 copy-done.14
  186.6 1.8 multiply_convert_fusion.4
  188.5 1.8 multiply_convert_fusion.2
  190.3 3.0 fusion.7
  193.3 3.0 fusion.6
  196.3 3.1 pad_maximum_fusion.1
  199.4 4.9 %all-to-all-start.1 = ((bf16[32,40,2048]{2,1,0:T(8,128)(2,1)}), bf16[32,40,2048]{2,1,0:T(8,128)(2,1)}, u32[]{:S(2)}, u32[]{:S(2)}) async-start(bf16[32,40,2048]{2,1,0:T(8,128)(2,1)} %pad_maximum_fusion.2), calls=%async_computation.1 | async-start | bytes 10485760 | tf_op jit(solution)/shard_map/all_to_all | solution.py:80
  204.4 4.2 %fusion.12 = bf16[1,384,2048]{2,1,0:T(8,128)(2,1)S(1)} fusion(bf16[768,384]{0,1:T(8,128)(2,1)S(1)} %multiply_convert_fusion.6, bf16[768,2048]{1,0:T(8,128)(2,1)} %bitcast.96), kind=kOutput, calls=%fused_computation.30 | convolution fusion | flops 1208745984 | bytes 5308416 | tf_op jit(solution)/shard_map/dot_general | solution.py:98
  208.6 1.4 fusion.13
  210.0 1.9 pad_maximum_fusion.4
  211.9 1.0 copy-done.16
  213.0 5.1 %convolution_convert_fusion.4 = bf16[768,2048]{1,0:T(8,128)(2,1)S(1)} fusion(bf16[2,2048,768]{2,1,0:T(8,128)(2,1)} %param.11, bf16[768,384]{0,1:T(8,128)(2,1)S(1)} %copy-done.16, bf16[768,384]{0,1:T(8,128)(2,1)S(1)} %get-tuple-element.22), kind=kOutput, calls=%fused_computation.10 | convolution fusion | flops 2419851264 | bytes 7471104 | tf_op jit(solution)/shard_map/dot_general | solution.py:93
  218.3 0.9 copy-done.18
  219.3 4.9 %convolution_convert_fusion.3 = bf16[768,2048]{1,0:T(8,128)(2,1)S(1)} fusion(bf16[2,2048,768]{2,1,0:T(8,128)(2,1)} %param.11, bf16[768,384]{0,1:T(8,128)(2,1)S(1)} %copy-done.20, bf16[768,384]{0,1:T(8,128)(2,1)S(1)} %copy-done.18), kind=kOutput, calls=%fused_computation.9 | convolution fusion | flops 2419851264 | bytes 7471104 | tf_op jit(solution)/shard_map/dot_general | solution.py:93
  224.6 2.8 pad_maximum_fusion.3
  227.4 33.9 %reduce-scatter.3.cloned.1.call-done = bf16[2,512,768]{2,1,0:T(8,128)(2,1)} async-done(((bf16[2,2048,768]{2,1,0:T(8,128)(2,1)}), bf16[2,512,768]{2,1,0:T(8,128)(2,1)}) %reduce-scatter.3.cloned.1.call-update) | async-done | bytes 1572880 | tf_op jit(solution)/shard_map/reduce_scatter | solution.py:101
  261.3 8.9 %all-to-all-done.1 = bf16[32,40,2048]{2,1,0:T(8,128)(2,1)} async-done(((bf16[32,40,2048]{2,1,0:T(8,128)(2,1)}), bf16[32,40,2048]{2,1,0:T(8,128)(2,1)}, u32[]{:S(2)}, u32[]{:S(2)}) %all-to-all-start.1) | async-done | bytes 5242912 | tf_op jit(solution)/shard_map/all_to_all | solution.py:80
  270.2 4.9 %all-to-all-start.2 = ((bf16[32,40,2048]{2,1,0:T(8,128)(2,1)}), bf16[32,40,2048]{2,1,0:T(8,128)(2,1)}, u32[]{:S(2)}, u32[]{:S(2)}) async-start(bf16[32,40,2048]{2,1,0:T(8,128)(2,1)} %pad_maximum_fusion.3), calls=%async_computation.3 | async-start | bytes 10485760 | tf_op jit(solution)/shard_map/all_to_all | solution.py:108
  275.5 1.7 collective-permute-start
  277.3 0.7 and.54
  278.1 1.3 fusion.30
  280.1 22.2 %reduce-scatter.5.cloned.1.call-done = bf16[2,384,512]{2,1,0:T(8,128)(2,1)} async-done(((bf16[2,384,2048]{2,1,0:T(8,128)(2,1)}), bf16[2,384,512]{2,1,0:T(8,128)(2,1)}) %reduce-scatter.5.cloned.1.call-update) | async-done | bytes 786448 | tf_op jit(solution)/shard_map/reduce_scatter | solution.py:104
  302.3 1.5 collective-permute-start.1
  303.8 4.0 convolution_bitcast_fusion
  307.9 7.0 %gather_fusion = f32[1024]{0:T(1024)S(1)} fusion(f32[128,1280]{0,1:T(8,128)S(1)} %convolution_bitcast_fusion, s32[1024]{0:T(1024)S(1)} %reshape.178), kind=kCustom, calls=%fused_computation | custom fusion | bytes 16384 | tf_op jit(solution)/shard_map/jit(take_along_axis)/gather | solution.py:122
  315.0 0.6 and_select_fusion
  315.7 5.8 %convolution_convert_fusion.10 = bf16[128,2048]{1,0:T(8,128)(2,1)} fusion(f32[128,1280]{0,1:T(8,128)S(1)} %select_n.84, bf16[1280,2048]{1,0:T(8,128)(2,1)} %bitcast.10), kind=kOutput, calls=%fused_computation.34 | convolution fusion | flops 4026793984 | bytes 6422528 | tf_op jit(solution)/shard_map/dot_general | solution.py:115
  321.4 66.5 %collective-permute-done.1 = bf16[2,384,512]{2,1,0:T(8,128)(2,1)} collective-permute-done((bf16[2,384,512]{2,1,0:T(8,128)(2,1)}, bf16[2,384,512]{2,1,0:T(8,128)(2,1)}, u32[]{:S(2)}, u32[]{:S(2)}) %collective-permute-start.1) | collective-permute-done | bytes 786464 | tf_op jit(solution)/shard_map/ppermute | solution.py:18
  387.9 2.4 select_convert_fusion.1
  390.3 3.5 select_convert_fusion
  393.8 4.2 %convolution_convert_fusion.9 = bf16[128,2048]{1,0:T(8,128)(2,1)} fusion(pred[128,1280]{0,1:T(32,128)(4,1)S(1)} %copy-done.6, bf16[1280,2048]{1,0:T(8,128)(2,1)} %bitcast.19), kind=kOutput, calls=%fused_computation.33 | convolution fusion | flops 671350784 | bytes 5931008 | tf_op jit(solution)/shard_map/dot_general | solution.py:123
  (77 shorter events, 3.3 us)
Async XLA Ops:
  7.2 4.4 %copy-start = (bf16[128,2048]{1,0:T(8,128)(2,1)S(1)}, bf16[128,2048]{1,0:T(8,128)(2,1)}, u32[]{:S(2)}) copy-start(bf16[128,2048]{1,0:T(8,128)(2,1)} %param.10) | copy-start | bytes 1572868
  7.2 2.8 copy-start.9
  9.0 0.6 copy-start.7
  20.7 140.9 %all-to-all-start = ((bf16[32,80,2048]{2,1,0:T(8,128)(2,1)}), bf16[32,80,2048]{2,1,0:T(8,128)(2,1)}, u32[]{:S(2)}, u32[]{:S(2)}) async-start(bf16[32,80,2048]{2,1,0:T(8,128)(2,1)} %pad_maximum_fusion), calls=%async_computation | async-start | bytes 20971520 | tf_op jit(solution)/shard_map/all_to_all | solution.py:49
  28.2 233.1 %reduce-scatter.3.cloned.1.call-start = ((), (), s32[]{:S(2)}) async-start(), calls=%async_computation.5 | async-start | bytes 7864320 | tf_op jit(solution)/shard_map/reduce_scatter | solution.py:101
  161.6 8.9 %slice-start = ((s8[6291456]{0:T(1024)(128)(4,1)}), s8[2097152]{0:T(1024)(128)(4,1)S(1)}, s32[]{:S(2)}) async-start(s8[6291456]{0:T(1024)(128)(4,1)} %bitcast.99), calls=%async_computation.7 | async-start | bytes 4194304
  165.2 5.3 %slice-start.1 = ((s8[6291456]{0:T(1024)(128)(4,1)}), s8[4194304]{0:T(1024)(128)(4,1)S(1)}, s32[]{:S(2)}) async-start(s8[6291456]{0:T(1024)(128)(4,1)} %bitcast.99), calls=%async_computation.8 | async-start | bytes 8388608
  170.5 3.2 copy-start.13
  183.9 2.7 copy-start.14
  184.5 3.9 copy-start.3
  184.5 3.9 copy-start.1
  188.5 4.8 %copy-start.15 = (bf16[768,384]{0,1:T(8,128)(2,1)}, bf16[768,384]{0,1:T(8,128)(2,1)S(1)}, u32[]{:S(2)}) copy-start(bf16[768,384]{0,1:T(8,128)(2,1)S(1)} %get-tuple-element.23) | copy-start | bytes 1769476
  190.3 3.0 copy-start.17
  190.3 3.0 copy-start.19
  199.4 70.8 %all-to-all-start.1 = ((bf16[32,40,2048]{2,1,0:T(8,128)(2,1)}), bf16[32,40,2048]{2,1,0:T(8,128)(2,1)}, u32[]{:S(2)}, u32[]{:S(2)}) async-start(bf16[32,40,2048]{2,1,0:T(8,128)(2,1)} %pad_maximum_fusion.2), calls=%async_computation.1 | async-start | bytes 10485760 | tf_op jit(solution)/shard_map/all_to_all | solution.py:80
  204.3 98.0 %reduce-scatter.5.cloned.1.call-start = ((), (), s32[]{:S(2)}) async-start(), calls=%async_computation.6 | async-start | bytes 3932160 | tf_op jit(solution)/shard_map/reduce_scatter | solution.py:104
  204.4 4.2 %copy-start.2 = (bf16[32,24,2048]{2,1,0:T(8,128)(2,1)S(1)}, bf16[32,24,2048]{2,1,0:T(8,128)(2,1)}, u32[]{:S(2)}) copy-start(bf16[32,24,2048]{2,1,0:T(8,128)(2,1)} %copy-done.1) | copy-start | bytes 9437188
  211.9 1.1 copy-start.16
  218.1 1.1 copy-start.18
  218.1 1.2 copy-start.20
  227.4 47.8 %copy-start.8 = (s32[128,64]{0,1:T(8,128)S(1)}, s32[128,64]{0,1:T(8,128)}, u32[]{:S(2)}) copy-start(s32[128,64]{0,1:T(8,128)} %copy-done.7) | copy-start | bytes 98308
  227.4 47.8 %copy-start.10 = (s32[128,8]{0,1:T(8,128)S(1)}, s32[128,8]{0,1:T(8,128)}, u32[]{:S(2)}) copy-start(s32[128,8]{0,1:T(8,128)} %param.8) | copy-start | bytes 12292
  261.3 14.2 %copy-start.4 = (bf16[2,512,768]{2,1,0:T(8,128)(2,1)S(1)}, bf16[2,512,768]{2,1,0:T(8,128)(2,1)}, u32[]{:S(2)}) copy-start(bf16[2,512,768]{2,1,0:T(8,128)(2,1)} %reduce-scatter.3.cloned.1.call-done) | copy-start | bytes 4718596
  270.2 123.6 %all-to-all-start.2 = ((bf16[32,40,2048]{2,1,0:T(8,128)(2,1)}), bf16[32,40,2048]{2,1,0:T(8,128)(2,1)}, u32[]{:S(2)}, u32[]{:S(2)}) async-start(bf16[32,40,2048]{2,1,0:T(8,128)(2,1)} %pad_maximum_fusion.3), calls=%async_computation.3 | async-start | bytes 10485760 | tf_op jit(solution)/shard_map/all_to_all | solution.py:108
  275.2 2.9 copy-start.11
  275.5 114.9 %collective-permute-start = (bf16[2,512,768]{2,1,0:T(8,128)(2,1)S(1)}, bf16[2,512,768]{2,1,0:T(8,128)(2,1)}, u32[]{:S(2)}, u32[]{:S(2)}) collective-permute-start(bf16[2,512,768]{2,1,0:T(8,128)(2,1)S(1)} %copy-done.4), channel_id=1, source_target_pairs={{0,8},{8,0},{4,12},{12,4},{16,24},{24,16},{20,28},{28,20},{32,40},... | collective-permute-start | bytes 4718600 | tf_op jit(solution)/shard_map/ppermute | solution.py:18
  302.3 85.6 %collective-permute-start.1 = (bf16[2,384,512]{2,1,0:T(8,128)(2,1)}, bf16[2,384,512]{2,1,0:T(8,128)(2,1)}, u32[]{:S(2)}, u32[]{:S(2)}) collective-permute-start(bf16[2,384,512]{2,1,0:T(8,128)(2,1)} %reduce-scatter.5.cloned.1.call-done), channel_id=1, source_target_pairs={{0,8},{8,0},{4,12},{12,4},{16,24},{24,16},{20,28},{28,20},{32,40},... | collective-permute-start | bytes 2359304 | tf_op jit(solution)/shard_map/ppermute | solution.py:18
  307.9 7.2 %copy-start.12 = (s32[128,8]{0,1:T(8,128)S(1)}, s32[128,8]{0,1:T(8,128)}, u32[]{:S(2)}) copy-start(s32[128,8]{0,1:T(8,128)} %copy-done.11) | copy-start | bytes 12292
  315.7 72.3 %copy-start.5 = (bf16[2,384,512]{2,1,0:T(8,128)(2,1)S(1)}, bf16[2,384,512]{2,1,0:T(8,128)(2,1)}, u32[]{:S(2)}) copy-start(bf16[2,384,512]{2,1,0:T(8,128)(2,1)} %reduce-scatter.5.cloned.1.call-done) | copy-start | bytes 2359300
  390.3 3.5 copy-start.6
Sparse Core Ops, SparseCore 0:
  199.5 61.6 reduce-scatter.2
  264.3 38.0 reduce-scatter.4

commit v6 on v3

--- a/solution.py
+++ b/solution.py
@@ -75,13 +75,24 @@
     send_out = merged([f[-1].reshape(groups, window, model_width) for f in forwards])
     send_out, recv_grad = lax.optimization_barrier((send_out, recv_grad))
     home_out = lax.all_to_all(send_out, "expert", split_axis=0, concat_axis=0, tiled=True)
-    backs, firsts, seconds = [], [], []
+    windows, seconds = [], []
     for local in range(per_device):
         low = local * shift
-        rows_x, pre_gate, up_part, sigmoid_gate, activated, hidden, _ = forwards[local]
+        hidden = forwards[local][5]
         own = (place < CAP) if local == 0 else (place >= window - CAP)
         rows_grad = jnp.where(own, recv_grad[:, low:low + window], jnp.zeros((), jnp.bfloat16))
         rows_grad = rows_grad.reshape(groups * window, model_width)
+        windows.append(rows_grad)
+        seconds.append(jnp.dot(hidden.T, rows_grad, preferred_element_type=jnp.float32))
+    grad_second = jnp.stack(seconds)
+    windows, grad_second = lax.optimization_barrier((windows, grad_second))
+    reduced_down = lax.psum_scatter(
+        grad_second.astype(jnp.bfloat16), "dp", scatter_dimension=2, tiled=True
+    )
+    backs, firsts = [], []
+    for local in range(per_device):
+        rows_x, pre_gate, up_part, sigmoid_gate, activated, hidden, _ = forwards[local]
+        rows_grad = windows[local]
         hidden_grad = jnp.dot(rows_grad, weight_down[local].T, preferred_element_type=jnp.float32)
         gate_grad = hidden_grad * up_part * sigmoid_gate * (1.0 + pre_gate * (1.0 - sigmoid_gate))
         proj_grad = jnp.concatenate([gate_grad, hidden_grad * activated], axis=-1).astype(
@@ -91,17 +102,13 @@
             jnp.bfloat16
         )
         backs.append(row_grad.reshape(groups, window, model_width))
-        firsts.append(jnp.dot(rows_x.T, proj_grad, preferred_element_type=jnp.float32))
-        seconds.append(jnp.dot(hidden.T, rows_grad, preferred_element_type=jnp.float32))
-    grad_first = jnp.stack(firsts)
-    grad_second = jnp.stack(seconds)
+        firsts.append((rows_x, proj_grad))
+    send_back, firsts, reduced_down = lax.optimization_barrier((merged(backs), firsts, reduced_down))
+    firsts = [jnp.dot(a.T, b, preferred_element_type=jnp.float32) for a, b in firsts]
+    grad_first, home_out = lax.optimization_barrier((jnp.stack(firsts), home_out))
     reduced_in = lax.psum_scatter(
         grad_first.astype(jnp.bfloat16), "dp", scatter_dimension=1, tiled=True
     )
-    reduced_down = lax.psum_scatter(
-        grad_second.astype(jnp.bfloat16), "dp", scatter_dimension=2, tiled=True
-    )
-    send_back, reduced_in = lax.optimization_barrier((merged(backs), reduced_in))
     home_grad = lax.all_to_all(send_back, "expert", split_axis=0, concat_axis=0, tiled=True)
     partner_in, partner_down = swapped((reduced_in, reduced_down), "expert", 1)
     held_in = jnp.where(my_flag == 1, partner_in, reduced_in).astype(jnp.float32)

time: 386 us -> 370 us (0.959)
  waiting for transfers between devices: 235 us -> 221 us
    ppermute x2, waiting for transfers between devices: 66.5 us -> 31 us  [swapped(): return lax.ppermute(block, axis, route)]
    reduce_scatter x1, waiting for transfers between devices: 34.1 us -> 52.6 us  [body(): lax.psum_scatter(grad_first.astype(jnp.bfloat16), 'dp', scatter_dimension...]
    all_to_all x1, waiting for transfers between devices: 8.82 us -> 23.3 us  [body(): lax.all_to_all(send_out, 'expert', split_axis=0, concat_axis=0, tiled=True)]
    reduce_scatter x1, waiting for transfers between devices: 21.6 us -> 9.61 us  [body(): lax.psum_scatter(grad_second.astype(jnp.bfloat16), 'dp', scatter_dimensio...]
  transfers between devices with their start and end apart: 8 -> 8, of which waited for: 6 -> 7; matrix products, arithmetic and copies ran while one was open for 19% -> 22% of each run, Pallas kernels for 0% -> 0%
where the time goes in v6:
time: 370 us; the launch traced here: 365 us
  waiting for transfers between devices  221 us (60%)
  matrix products  61.2 us (17%)
  starting transfers between devices  26.1 us (7%)
  other arithmetic  23.8 us (6%)
  local copies, waits for them, and re-layouts  18 us (5%)
  between operations  15.7 us (4%)
    all_to_all x1, waiting for transfers between devices, body(): lax.all_to_all(send_x, 'expert', split_axis=0, concat_axis=0, tiled=True)  61.6 us
    reduce_scatter x1, waiting for transfers between devices, body(): lax.psum_scatter(grad_first.astype(jnp.bfloat16), 'dp', scatter_dimension...  52.6 us
    all_to_all x1, waiting for transfers between devices, body(): lax.all_to_all(send_grad, 'expert', split_axis=0, concat_axis=0, tiled=True)  42.4 us
    ppermute x2, waiting for transfers between devices, swapped(): return lax.ppermute(block, axis, route)  31 us
    all_to_all x1, waiting for transfers between devices, body(): lax.all_to_all(send_out, 'expert', split_axis=0, concat_axis=0, tiled=True)  23.3 us
    dot_general x2, matrix products, body(): jnp.dot(rows_x, weight_in[local], preferred_element_type=jnp.float32)  9.69 us
    reduce_scatter x1, waiting for transfers between devices, body(): lax.psum_scatter(grad_second.astype(jnp.bfloat16), 'dp', scatter_dimensio...  9.61 us
    dot_general x2, matrix products, body(): jnp.dot(a.T, b, preferred_element_type=jnp.float32)  7.99 us
  transfers between devices with their start and end apart: 8, of which 7 were waited for; matrix products, arithmetic and copies ran while one was open for 22% of the time, Pallas kernels for 0%

profile of v6, /device:TPU:0, one launch (start us, length us, event | category | flops | bytes accessed | tf_op | source)
XLA Modules:
  0.0 365.4 jit_solution(18399215240360623781)
XLA Ops:
  7.2 0.8 fusion.23
  8.8 3.9 %convolution_convert_fusion = bf16[1280,2048]{1,0:T(8,128)(2,1)} fusion(pred[128,1280]{0,1:T(32,128)(4,1)S(1)} %compare_and_fusion, bf16[128,2048]{1,0:T(8,128)(2,1)S(1)} %copy-done.12), kind=kOutput, calls=%fused_computation.3 | convolution fusion | flops 673710080 | bytes 5931008 | tf_op jit(solution)/shard_map/dot_general | solution.py:43
  12.7 7.7 %all-to-all-start = ((bf16[32,40,2048]{2,1,0:T(8,128)(2,1)}), bf16[32,40,2048]{2,1,0:T(8,128)(2,1)}, u32[]{:S(2)}, u32[]{:S(2)}) async-start(bf16[32,40,2048]{2,1,0:T(8,128)(2,1)} %bitcast.84), calls=%async_computation | async-start | bytes 10485760 | tf_op jit(solution)/shard_map/all_to_all | solution.py:49
  20.9 3.9 %multiply_convert_fusion = bf16[1280,2048]{1,0:T(8,128)(2,1)} fusion(pred[128,1280]{0,1:T(32,128)(4,1)S(1)} %compare_and_fusion, bf16[128,2048]{1,0:T(8,128)(2,1)S(1)} %copy-done, f32[1280]{0:T(1024)S(1)} %mul.62), kind=kOutput, calls=%fused_computation.2 | convolution fusion | flops 676331520 | bytes 5936128 | tf_op jit(solution)/shard_map/dot_general | solution.py:44
  24.7 61.6 %all-to-all-done = bf16[32,40,2048]{2,1,0:T(8,128)(2,1)} async-done(((bf16[32,40,2048]{2,1,0:T(8,128)(2,1)}), bf16[32,40,2048]{2,1,0:T(8,128)(2,1)}, u32[]{:S(2)}, u32[]{:S(2)}) %all-to-all-start) | async-done | bytes 5242912 | tf_op jit(solution)/shard_map/all_to_all | solution.py:49
  86.3 4.9 %all-to-all-start.1 = ((bf16[32,40,2048]{2,1,0:T(8,128)(2,1)}), bf16[32,40,2048]{2,1,0:T(8,128)(2,1)}, u32[]{:S(2)}, u32[]{:S(2)}) async-start(bf16[32,40,2048]{2,1,0:T(8,128)(2,1)} %bitcast.83), calls=%async_computation.1 | async-start | bytes 10485760 | tf_op jit(solution)/shard_map/all_to_all | solution.py:50
  91.4 3.4 fusion.27
  94.9 7.0 %fusion.1 = f32[768,768]{0,1:T(8,128)S(1)} fusion(bf16[768,2048]{1,0:T(8,128)(2,1)S(1)} %bitcast.95, bf16[2,2048,768]{2,1,0:T(8,128)(2,1)} %param.11), kind=kOutput, calls=%fused_computation.14 | convolution fusion | flops 2415919104 | bytes 8650752 | tf_op jit(solution)/shard_map/dot_general | solution.py:58
  101.9 1.4 copy-done.9
  103.7 1.8 convolution_convert_fusion.3
  105.7 0.6 slice-done.1
  106.3 2.7 fusion.4
  109.3 1.8 convolution_convert_fusion.4
  111.6 3.1 pad_maximum_fusion.2
  114.7 42.4 %all-to-all-done.1 = bf16[32,40,2048]{2,1,0:T(8,128)(2,1)} async-done(((bf16[32,40,2048]{2,1,0:T(8,128)(2,1)}), bf16[32,40,2048]{2,1,0:T(8,128)(2,1)}, u32[]{:S(2)}, u32[]{:S(2)}) %all-to-all-start.1) | async-done | bytes 5242912 | tf_op jit(solution)/shard_map/all_to_all | solution.py:50
  157.0 3.1 slice_select_fusion
  160.2 1.4 convolution_bitcast_fusion.2
  161.8 1.0 copy-done.4
  162.9 1.4 convolution_bitcast_fusion.3
  164.3 1.9 pad_maximum_fusion.1
  166.2 4.9 %all-to-all-start.2 = ((bf16[32,40,2048]{2,1,0:T(8,128)(2,1)}), bf16[32,40,2048]{2,1,0:T(8,128)(2,1)}, u32[]{:S(2)}, u32[]{:S(2)}) async-start(bf16[32,40,2048]{2,1,0:T(8,128)(2,1)} %pad_maximum_fusion.2), calls=%async_computation.3 | async-start | bytes 10485760 | tf_op jit(solution)/shard_map/all_to_all | solution.py:77
  171.2 5.3 %multiply_convert_fusion.2 = (bf16[768,384]{0,1:T(8,128)(2,1)S(1)}, bf16[768,384]{0,1:T(8,128)(2,1)S(1)}) fusion(f32[768,768]{0,1:T(8,128)} %copy-done.9, bf16[768,2048]{1,0:T(8,128)(2,1)} %bitcast.100, bf16[2,384,2048]{2,1,0:T(8,128)(2,1)} %param.12), kind=kOutput, calls=%fused_computation.44 | convolution fusion | flops 1211793408 | bytes 8257536 | tf_op jit(solution)/shard_map/dot_general | solution.py:96
  176.5 5.0 %convolution_convert_fusion.1 = bf16[768,2048]{1,0:T(8,128)(2,1)S(1)} fusion(bf16[2,2048,768]{2,1,0:T(8,128)(2,1)} %param.11, bf16[768,384]{0,1:T(8,128)(2,1)S(1)} %get-tuple-element.43, bf16[768,384]{0,1:T(8,128)(2,1)S(1)} %get-tuple-element.42), kind=kOutput, calls=%fused_computation.9 | convolution fusion | flops 2419851264 | bytes 7471104 | tf_op jit(solution)/shard_map/dot_general | solution.py:101
  181.8 1.7 copy-done.5
  183.5 1.8 multiply_convert_fusion.4
  185.6 2.9 convolution_convert_fusion.2
  188.7 1.1 pad_maximum_fusion.5
  190.0 2.8 pad_maximum_fusion.3
  192.9 9.6 %reduce-scatter.3.cloned.1.call-done = bf16[2,384,512]{2,1,0:T(8,128)(2,1)} async-done(((bf16[2,384,2048]{2,1,0:T(8,128)(2,1)}), bf16[2,384,512]{2,1,0:T(8,128)(2,1)}) %reduce-scatter.3.cloned.1.call-update) | async-done | bytes 786448 | tf_op jit(solution)/shard_map/reduce_scatter | solution.py:89
  202.5 5.1 %convolution_bitcast_fusion = bf16[1,2048,768]{2,1,0:T(8,128)(2,1)S(1)} fusion(bf16[768,2048]{1,0:T(8,128)(2,1)} %bitcast.96, bf16[768,768]{0,1:T(8,128)(2,1)} %pad_maximum_fusion.5), kind=kOutput, calls=%fused_computation.7 | convolution fusion | flops 2415919104 | bytes 7471104 | tf_op jit(solution)/shard_map/dot_general | solution.py:107
  207.5 2.9 convolution_bitcast_fusion.1
  210.5 3.2 pad_maximum_fusion
  213.7 23.3 %all-to-all-done.2 = bf16[32,40,2048]{2,1,0:T(8,128)(2,1)} async-done(((bf16[32,40,2048]{2,1,0:T(8,128)(2,1)}), bf16[32,40,2048]{2,1,0:T(8,128)(2,1)}, u32[]{:S(2)}, u32[]{:S(2)}) %all-to-all-start.2) | async-done | bytes 5242912 | tf_op jit(solution)/shard_map/all_to_all | solution.py:77
  237.0 5.0 %all-to-all-start.3 = ((bf16[32,40,2048]{2,1,0:T(8,128)(2,1)}), bf16[32,40,2048]{2,1,0:T(8,128)(2,1)}, u32[]{:S(2)}, u32[]{:S(2)}) async-start(bf16[32,40,2048]{2,1,0:T(8,128)(2,1)} %pad_maximum_fusion.3), calls=%async_computation.4 | async-start | bytes 10485760 | tf_op jit(solution)/shard_map/all_to_all | solution.py:112
  242.6 0.7 and.54
  243.3 0.6 fusion.26
  244.6 1.7 collective-permute-start.1
  246.3 52.6 %reduce-scatter.5.cloned.1.call-done = bf16[2,512,768]{2,1,0:T(8,128)(2,1)} async-done(((bf16[2,2048,768]{2,1,0:T(8,128)(2,1)}), bf16[2,512,768]{2,1,0:T(8,128)(2,1)}) %reduce-scatter.5.cloned.1.call-update) | async-done | bytes 1572880 | tf_op jit(solution)/shard_map/reduce_scatter | solution.py:109
  299.0 1.7 collective-permute-start
  300.7 4.0 %convolution_bitcast_fusion.4 = f32[128,1280]{0,1:T(8,128)S(1)} fusion(bf16[1280,2048]{1,0:T(8,128)(2,1)} %bitcast.18, bf16[128,2048]{1,0:T(8,128)(2,1)S(1)} %copy-done), kind=kOutput, calls=%fused_computation.27 | convolution fusion | flops 671088640 | bytes 6422528 | tf_op jit(solution)/shard_map/dot_general | solution.py:123
  304.7 7.0 %gather_fusion = f32[1024]{0:T(1024)S(1)} fusion(f32[128,1280]{0,1:T(8,128)S(1)} %convolution_bitcast_fusion.4, s32[1024]{0:T(1024)S(1)} %reshape.178), kind=kCustom, calls=%fused_computation | custom fusion | bytes 16384 | tf_op jit(solution)/shard_map/jit(take_along_axis)/gather | solution.py:126
  311.9 0.6 and_select_fusion
  312.5 5.6 %convolution_convert_fusion.6 = bf16[128,2048]{1,0:T(8,128)(2,1)} fusion(f32[128,1280]{0,1:T(8,128)S(1)} %select_n.84, bf16[1280,2048]{1,0:T(8,128)(2,1)} %bitcast.18), kind=kOutput, calls=%fused_computation.29 | convolution fusion | flops 4026793984 | bytes 6422528 | tf_op jit(solution)/shard_map/dot_general | solution.py:119
  318.1 3.5 collective-permute-done.1
  321.6 1.2 select_convert_fusion.1
  322.8 4.4 %convolution_convert_fusion.5 = bf16[128,2048]{1,0:T(8,128)(2,1)} fusion(pred[128,1280]{0,1:T(32,128)(4,1)} %and.54, bf16[1280,2048]{1,0:T(8,128)(2,1)} %bitcast.21), kind=kOutput, calls=%fused_computation.28 | convolution fusion | flops 671350784 | bytes 5931008 | tf_op jit(solution)/shard_map/dot_general | solution.py:127
  327.2 27.6 %collective-permute-done = bf16[2,512,768]{2,1,0:T(8,128)(2,1)} collective-permute-done((bf16[2,512,768]{2,1,0:T(8,128)(2,1)}, bf16[2,512,768]{2,1,0:T(8,128)(2,1)}, u32[]{:S(2)}, u32[]{:S(2)}) %collective-permute-start) | collective-permute-done | bytes 1572896 | tf_op jit(solution)/shard_map/ppermute | solution.py:18
  354.8 3.3 select_convert_fusion
  (78 shorter events, 4.4 us)
Async XLA Ops:
  7.2 13.7 %copy-start = (bf16[128,2048]{1,0:T(8,128)(2,1)S(1)}, bf16[128,2048]{1,0:T(8,128)(2,1)}, u32[]{:S(2)}) copy-start(bf16[128,2048]{1,0:T(8,128)(2,1)} %param.10) | copy-start | bytes 1572868
  7.2 1.6 copy-start.12
  12.7 7.7 %copy-start.13 = (s32[128,8]{0,1:T(8,128)S(1)}, s32[128,8]{0,1:T(8,128)}, u32[]{:S(2)}) copy-start(s32[128,8]{0,1:T(8,128)} %param.8) | copy-start | bytes 12292
  12.7 7.7 %copy-start.14 = (f32[128,8]{0,1:T(8,128)S(1)}, f32[128,8]{0,1:T(8,128)}, u32[]{:S(2)}) copy-start(f32[128,8]{0,1:T(8,128)} %param.9) | copy-start | bytes 12292
  12.7 73.6 %all-to-all-start = ((bf16[32,40,2048]{2,1,0:T(8,128)(2,1)}), bf16[32,40,2048]{2,1,0:T(8,128)(2,1)}, u32[]{:S(2)}, u32[]{:S(2)}) async-start(bf16[32,40,2048]{2,1,0:T(8,128)(2,1)} %bitcast.84), calls=%async_computation | async-start | bytes 10485760 | tf_op jit(solution)/shard_map/all_to_all | solution.py:49
  86.3 70.8 %all-to-all-start.1 = ((bf16[32,40,2048]{2,1,0:T(8,128)(2,1)}), bf16[32,40,2048]{2,1,0:T(8,128)(2,1)}, u32[]{:S(2)}, u32[]{:S(2)}) async-start(bf16[32,40,2048]{2,1,0:T(8,128)(2,1)} %bitcast.83), calls=%async_computation.1 | async-start | bytes 10485760 | tf_op jit(solution)/shard_map/all_to_all | solution.py:50
  91.2 111.3 %reduce-scatter.3.cloned.1.call-start = ((), (), s32[]{:S(2)}) async-start(), calls=%async_computation.6 | async-start | bytes 3932160 | tf_op jit(solution)/shard_map/reduce_scatter | solution.py:89
  94.8 7.0 %copy-start.3 = (bf16[32,24,2048]{2,1,0:T(8,128)(2,1)}, bf16[32,24,2048]{2,1,0:T(8,128)(2,1)S(1)}, u32[]{:S(2)}) copy-start(bf16[32,24,2048]{2,1,0:T(8,128)(2,1)S(1)} %get-tuple-element.39) | copy-start | bytes 9437188
  94.8 10.8 %copy-start.1 = (bf16[32,24,2048]{2,1,0:T(8,128)(2,1)}, bf16[32,24,2048]{2,1,0:T(8,128)(2,1)S(1)}, u32[]{:S(2)}) copy-start(bf16[32,24,2048]{2,1,0:T(8,128)(2,1)S(1)} %get-tuple-element.38) | copy-start | bytes 9437188
  94.9 8.8 %copy-start.15 = (bf16[2,384,2048]{2,1,0:T(8,128)(2,1)S(1)}, bf16[2,384,2048]{2,1,0:T(8,128)(2,1)}, u32[]{:S(2)}) copy-start(bf16[2,384,2048]{2,1,0:T(8,128)(2,1)} %param.12) | copy-start | bytes 9437188
  101.9 1.4 copy-start.9
  103.3 2.4 slice-start
  103.7 2.6 slice-start.1
  109.0 2.2 copy-start.7
  160.2 1.7 copy-start.6
  160.2 2.7 copy-start.4
  166.2 70.8 %all-to-all-start.2 = ((bf16[32,40,2048]{2,1,0:T(8,128)(2,1)}), bf16[32,40,2048]{2,1,0:T(8,128)(2,1)}, u32[]{:S(2)}, u32[]{:S(2)}) async-start(bf16[32,40,2048]{2,1,0:T(8,128)(2,1)} %pad_maximum_fusion.2), calls=%async_computation.3 | async-start | bytes 10485760 | tf_op jit(solution)/shard_map/all_to_all | solution.py:77
  171.1 127.9 %reduce-scatter.5.cloned.1.call-start = ((), (), s32[]{:S(2)}) async-start(), calls=%async_computation.7 | async-start | bytes 7864320 | tf_op jit(solution)/shard_map/reduce_scatter | solution.py:109
  176.5 5.2 %copy-start.8 = (f32[768,768]{0,1:T(8,128)S(1)}, f32[768,768]{0,1:T(8,128)}, u32[]{:S(2)}) copy-start(f32[768,768]{0,1:T(8,128)} %copy-done.7) | copy-start | bytes 7077892
  176.5 5.2 %copy-start.16 = (bf16[2,384,2048]{2,1,0:T(8,128)(2,1)S(1)}, bf16[2,384,2048]{2,1,0:T(8,128)(2,1)}, u32[]{:S(2)}) copy-start(bf16[2,384,2048]{2,1,0:T(8,128)(2,1)} %param.12) | copy-start | bytes 9437188
  181.6 1.9 copy-start.5
  181.6 3.7 %slice-start.2 = ((s8[6291456]{0:T(1024)(128)(4,1)}), s8[4194304]{0:T(1024)(128)(4,1)S(1)}, s32[]{:S(2)}) async-start(s8[6291456]{0:T(1024)(128)(4,1)} %bitcast.103), calls=%async_computation.10 | async-start | bytes 8388608
  183.5 2.1 slice-start.3
  202.5 5.1 %copy-start.2 = (bf16[32,24,2048]{2,1,0:T(8,128)(2,1)S(1)}, bf16[32,24,2048]{2,1,0:T(8,128)(2,1)}, u32[]{:S(2)}) copy-start(bf16[32,24,2048]{2,1,0:T(8,128)(2,1)} %copy-done.1) | copy-start | bytes 9437188
  237.0 6.3 %copy-start.17 = (s32[32]{0:T(128)S(1)}, s32[32]{0:T(128)}, u32[]{:S(2)}) copy-start(s32[32]{0:T(128)} %param.13) | copy-start | bytes 388
  237.0 7.6 %copy-start.11 = (bf16[2,384,512]{2,1,0:T(8,128)(2,1)S(1)}, bf16[2,384,512]{2,1,0:T(8,128)(2,1)}, u32[]{:S(2)}) copy-start(bf16[2,384,512]{2,1,0:T(8,128)(2,1)} %reduce-scatter.3.cloned.1.call-done) | copy-start | bytes 2359300
  237.0 85.8 %all-to-all-start.3 = ((bf16[32,40,2048]{2,1,0:T(8,128)(2,1)}), bf16[32,40,2048]{2,1,0:T(8,128)(2,1)}, u32[]{:S(2)}, u32[]{:S(2)}) async-start(bf16[32,40,2048]{2,1,0:T(8,128)(2,1)} %pad_maximum_fusion.3), calls=%async_computation.4 | async-start | bytes 10485760 | tf_op jit(solution)/shard_map/all_to_all | solution.py:112
  244.6 77.0 %collective-permute-start.1 = (bf16[2,384,512]{2,1,0:T(8,128)(2,1)S(1)}, bf16[2,384,512]{2,1,0:T(8,128)(2,1)S(1)}, u32[]{:S(2)}, u32[]{:S(2)}) collective-permute-start(bf16[2,384,512]{2,1,0:T(8,128)(2,1)S(1)} %copy-done.11), channel_id=1, source_target_pairs={{0,8},{8,0},{4,12},{12,4},{16,24},{24,16},{20,28},{28,20},{32,40},... | collective-permute-start | bytes 2359304 | tf_op jit(solution)/shard_map/ppermute | solution.py:18
  299.0 55.9 %collective-permute-start = (bf16[2,512,768]{2,1,0:T(8,128)(2,1)}, bf16[2,512,768]{2,1,0:T(8,128)(2,1)}, u32[]{:S(2)}, u32[]{:S(2)}) collective-permute-start(bf16[2,512,768]{2,1,0:T(8,128)(2,1)} %reduce-scatter.5.cloned.1.call-done), channel_id=1, source_target_pairs={{0,8},{8,0},{4,12},{12,4},{16,24},{24,16},{20,28},{28,20},{32,40},... | collective-permute-start | bytes 4718600 | tf_op jit(solution)/shard_map/ppermute | solution.py:18
  322.8 32.0 %copy-start.10 = (bf16[2,512,768]{2,1,0:T(8,128)(2,1)S(1)}, bf16[2,512,768]{2,1,0:T(8,128)(2,1)}, u32[]{:S(2)}) copy-start(bf16[2,512,768]{2,1,0:T(8,128)(2,1)} %reduce-scatter.5.cloned.1.call-done) | copy-start | bytes 4718596
Sparse Core Ops, SparseCore 0:
  166.3 36.0 reduce-scatter.2
  237.1 61.7 reduce-scatter.4

commit v7 on v6

--- a/solution.py
+++ b/solution.py
@@ -75,20 +75,27 @@
     send_out = merged([f[-1].reshape(groups, window, model_width) for f in forwards])
     send_out, recv_grad = lax.optimization_barrier((send_out, recv_grad))
     home_out = lax.all_to_all(send_out, "expert", split_axis=0, concat_axis=0, tiled=True)
+    whole_grad = recv_grad.reshape(groups * lanes, model_width)
+    lane = jnp.arange(lanes, dtype=jnp.int32)[None, :, None]
     windows, seconds = [], []
     for local in range(per_device):
         low = local * shift
-        hidden = forwards[local][5]
+        hidden = forwards[local][5].reshape(groups, window, FF)
+        own = (place < CAP) if local == 0 else (place >= window - CAP)
+        padded = jnp.pad(hidden, ((0, 0), (low, lanes - window - low), (0, 0)))
+        mine = (lane < CAP) if local == 0 else (lane >= CAP)
+        padded = jnp.where(mine, padded, jnp.zeros((), jnp.bfloat16)).reshape(groups * lanes, FF)
+        seconds.append(jnp.dot(padded.T, whole_grad, preferred_element_type=jnp.float32))
+    recv_grad, seconds = lax.optimization_barrier((recv_grad, seconds))
+    for local in range(per_device):
+        low = local * shift
         own = (place < CAP) if local == 0 else (place >= window - CAP)
         rows_grad = jnp.where(own, recv_grad[:, low:low + window], jnp.zeros((), jnp.bfloat16))
-        rows_grad = rows_grad.reshape(groups * window, model_width)
-        windows.append(rows_grad)
-        seconds.append(jnp.dot(hidden.T, rows_grad, preferred_element_type=jnp.float32))
-    grad_second = jnp.stack(seconds)
-    windows, grad_second = lax.optimization_barrier((windows, grad_second))
-    reduced_down = lax.psum_scatter(
-        grad_second.astype(jnp.bfloat16), "dp", scatter_dimension=2, tiled=True
-    )
+        windows.append(rows_grad.reshape(groups * window, model_width))
+    reduced_down = jnp.stack([
+        lax.psum_scatter(part.astype(jnp.bfloat16), "dp", scatter_dimension=1, tiled=True)
+        for part in seconds
+    ])
     backs, firsts = [], []
     for local in range(per_device):
         rows_x, pre_gate, up_part, sigmoid_gate, activated, hidden, _ = forwards[local]

time: 370 us -> 373 us (level)
  matrix products: 61.2 us -> 65 us
    all_to_all x1, waiting for transfers between devices: 23.3 us -> 6.22 us  [body(): lax.all_to_all(send_out, 'expert', split_axis=0, concat_axis=0, tiled=True)]
    reduce_scatter x1 -> x2, waiting for transfers between devices: 9.61 us -> 25.5 us  [body(): lax.psum_scatter(part.astype(jnp.bfloat16), 'dp', scatter_dimension=1, ti...]
    dot_general x2, matrix products: 2.82 us -> 12 us  [body(): jnp.dot(padded.T, whole_grad, preferred_element_type=jnp.float32)]
  transfers between devices with their start and end apart: 8 -> 9, of which waited for: 7 -> 7; matrix products, arithmetic and copies ran while one was open for 22% -> 22% of each run, Pallas kernels for 0% -> 0%
where the time goes in v7:
time: 373 us; the launch traced here: 368 us
  waiting for transfers between devices  219 us (59%)
  matrix products  65 us (17%)
  starting transfers between devices  26 us (7%)
  other arithmetic  24.8 us (7%)
  local copies, waits for them, and re-layouts  17.4 us (5%)
  between operations  15.4 us (4%)
    all_to_all x1, waiting for transfers between devices, body(): lax.all_to_all(send_x, 'expert', split_axis=0, concat_axis=0, tiled=True)  61.6 us
    reduce_scatter x1, waiting for transfers between devices, body(): lax.psum_scatter(grad_first.astype(jnp.bfloat16), 'dp', scatter_dimension...  50.6 us
    all_to_all x1, waiting for transfers between devices, body(): lax.all_to_all(send_grad, 'expert', split_axis=0, concat_axis=0, tiled=True)  43.5 us
    ppermute x2, waiting for transfers between devices, swapped(): return lax.ppermute(block, axis, route)  31.1 us
    reduce_scatter x2, waiting for transfers between devices, body(): lax.psum_scatter(part.astype(jnp.bfloat16), 'dp', scatter_dimension=1, ti...  25.5 us
    dot_general x2, matrix products, body(): jnp.dot(padded.T, whole_grad, preferred_element_type=jnp.float32)  12 us
    dot_general x2, matrix products, body(): jnp.dot(rows_x, weight_in[local], preferred_element_type=jnp.float32)  9.38 us
    dot_general x2, matrix products, body(): jnp.dot(a.T, b, preferred_element_type=jnp.float32)  7.97 us
  transfers between devices with their start and end apart: 9, of which 7 were waited for; matrix products, arithmetic and copies ran while one was open for 22% of the time, Pallas kernels for 0%

profile of v7, /device:TPU:0, one launch (start us, length us, event | category | flops | bytes accessed | tf_op | source)
XLA Modules:
  0.0 367.8 jit_solution(9523542183120503879)
XLA Ops:
  7.2 0.8 fusion.31
  8.8 3.8 %convolution_convert_fusion = bf16[1280,2048]{1,0:T(8,128)(2,1)} fusion(pred[128,1280]{0,1:T(32,128)(4,1)S(1)} %compare_and_fusion, bf16[128,2048]{1,0:T(8,128)(2,1)S(1)} %copy-done.12), kind=kOutput, calls=%fused_computation.3 | convolution fusion | flops 673710080 | bytes 5931008 | tf_op jit(solution)/shard_map/dot_general | solution.py:43
  12.7 7.7 %all-to-all-start = ((bf16[32,40,2048]{2,1,0:T(8,128)(2,1)}), bf16[32,40,2048]{2,1,0:T(8,128)(2,1)}, u32[]{:S(2)}, u32[]{:S(2)}) async-start(bf16[32,40,2048]{2,1,0:T(8,128)(2,1)} %bitcast.86), calls=%async_computation | async-start | bytes 10485760 | tf_op jit(solution)/shard_map/all_to_all | solution.py:49
  20.8 3.8 %multiply_convert_fusion = bf16[1280,2048]{1,0:T(8,128)(2,1)} fusion(pred[128,1280]{0,1:T(32,128)(4,1)S(1)} %compare_and_fusion, bf16[128,2048]{1,0:T(8,128)(2,1)S(1)} %copy-done, f32[1280]{0:T(1024)S(1)} %mul.62), kind=kOutput, calls=%fused_computation.2 | convolution fusion | flops 676331520 | bytes 5936128 | tf_op jit(solution)/shard_map/dot_general | solution.py:44
  24.7 61.6 %all-to-all-done = bf16[32,40,2048]{2,1,0:T(8,128)(2,1)} async-done(((bf16[32,40,2048]{2,1,0:T(8,128)(2,1)}), bf16[32,40,2048]{2,1,0:T(8,128)(2,1)}, u32[]{:S(2)}, u32[]{:S(2)}) %all-to-all-start) | async-done | bytes 5242912 | tf_op jit(solution)/shard_map/all_to_all | solution.py:49
  86.2 4.9 %all-to-all-start.1 = ((bf16[32,40,2048]{2,1,0:T(8,128)(2,1)}), bf16[32,40,2048]{2,1,0:T(8,128)(2,1)}, u32[]{:S(2)}, u32[]{:S(2)}) async-start(bf16[32,40,2048]{2,1,0:T(8,128)(2,1)} %bitcast.85), calls=%async_computation.1 | async-start | bytes 10485760 | tf_op jit(solution)/shard_map/all_to_all | solution.py:50
  91.4 3.4 fusion.37
  94.9 6.8 %fusion.4 = f32[768,768]{1,0:T(8,128)S(1)} fusion(bf16[768,2048]{1,0:T(8,128)(2,1)S(1)} %bitcast.97, bf16[2,2048,768]{2,1,0:T(8,128)(2,1)} %param.11), kind=kOutput, calls=%fused_computation.16 | convolution fusion | flops 2415919104 | bytes 8650752 | tf_op jit(solution)/shard_map/dot_general | solution.py:58
  102.0 1.8 convolution_convert_fusion.4
  104.0 0.7 slice-done
  105.4 2.6 fusion.1
  108.3 1.8 convolution_convert_fusion.3
  110.5 3.0 pad_maximum_fusion.1
  113.5 43.5 %all-to-all-done.1 = bf16[32,40,2048]{2,1,0:T(8,128)(2,1)} async-done(((bf16[32,40,2048]{2,1,0:T(8,128)(2,1)}), bf16[32,40,2048]{2,1,0:T(8,128)(2,1)}, u32[]{:S(2)}, u32[]{:S(2)}) %all-to-all-start.1) | async-done | bytes 5242912 | tf_op jit(solution)/shard_map/all_to_all | solution.py:50
  157.0 6.0 %convolution_bitcast_fusion.2 = bf16[384,2048]{1,0:T(8,128)(2,1)} fusion(bf16[32,40,2048]{2,1,0:T(8,128)(2,1)} %all-to-all-done.1, bf16[32,24,384]{2,1,0:T(8,128)(2,1)S(1)} %bitcast.102, pred[40]{0:T(512)(128)(4,1)S(1)} %iota_compare_fusion.7), kind=kOutput, calls=%fused_computation.20 | convolution fusion | flops 2013757440 | bytes 7405608 | tf_op jit(solution)/shard_map/dot_general | solution.py:88
  163.0 6.1 %convolution_bitcast_fusion.3 = bf16[384,2048]{1,0:T(8,128)(2,1)} fusion(bf16[32,40,2048]{2,1,0:T(8,128)(2,1)} %all-to-all-done.1, bf16[32,24,384]{2,1,0:T(8,128)(2,1)S(1)} %bitcast.101, pred[40]{0:T(512)(128)(4,1)S(1)} %iota_compare_fusion.8), kind=kOutput, calls=%fused_computation.21 | convolution fusion | flops 2013757440 | bytes 7405608 | tf_op jit(solution)/shard_map/dot_general | solution.py:88
  169.1 4.9 %all-to-all-start.2 = ((bf16[32,40,2048]{2,1,0:T(8,128)(2,1)}), bf16[32,40,2048]{2,1,0:T(8,128)(2,1)}, u32[]{:S(2)}, u32[]{:S(2)}) async-start(bf16[32,40,2048]{2,1,0:T(8,128)(2,1)} %pad_maximum_fusion.1), calls=%async_computation.4 | async-start | bytes 10485760 | tf_op jit(solution)/shard_map/all_to_all | solution.py:77
  174.0 0.7 reduce-scatter.6.cloned.1.call-update
  174.8 3.5 slice_select_fusion.1
  178.6 0.9 copy-done.18
  179.5 2.1 multiply_convert_fusion.4
  181.7 2.9 convolution_convert_fusion.2
  184.8 1.5 copy-done.5
  186.3 2.2 multiply_convert_fusion.2
  188.5 2.9 convolution_convert_fusion.1
  191.6 1.2 pad_maximum_fusion.3
  192.9 2.8 pad_maximum_fusion.2
  195.7 25.5 %reduce-scatter.6.cloned.1.call-done = bf16[384,512]{1,0:T(8,128)(2,1)} async-done(((bf16[384,2048]{1,0:T(8,128)(2,1)}), bf16[384,512]{1,0:T(8,128)(2,1)}) %reduce-scatter.6.cloned.1.call-update) | async-done | bytes 393232 | tf_op jit(solution)/shard_map/reduce_scatter | solution.py:96
  221.2 1.2 pad_maximum_fusion.5
  222.4 5.0 %convolution_bitcast_fusion.1 = bf16[1,2048,768]{2,1,0:T(8,128)(2,1)S(1)} fusion(bf16[768,2048]{1,0:T(8,128)(2,1)} %bitcast.98, bf16[768,768]{1,0:T(8,128)(2,1)} %pad_maximum_fusion.3), kind=kOutput, calls=%fused_computation.7 | convolution fusion | flops 2415919104 | bytes 7471104 | tf_op jit(solution)/shard_map/dot_general | solution.py:114
  227.5 2.9 convolution_bitcast_fusion
  230.4 3.2 pad_maximum_fusion
  233.6 6.2 %all-to-all-done.2 = bf16[32,40,2048]{2,1,0:T(8,128)(2,1)} async-done(((bf16[32,40,2048]{2,1,0:T(8,128)(2,1)}), bf16[32,40,2048]{2,1,0:T(8,128)(2,1)}, u32[]{:S(2)}, u32[]{:S(2)}) %all-to-all-start.2) | async-done | bytes 5242912 | tf_op jit(solution)/shard_map/all_to_all | solution.py:77
  239.9 4.9 %all-to-all-start.3 = ((bf16[32,40,2048]{2,1,0:T(8,128)(2,1)}), bf16[32,40,2048]{2,1,0:T(8,128)(2,1)}, u32[]{:S(2)}, u32[]{:S(2)}) async-start(bf16[32,40,2048]{2,1,0:T(8,128)(2,1)} %pad_maximum_fusion.2), calls=%async_computation.5 | async-start | bytes 10485760 | tf_op jit(solution)/shard_map/all_to_all | solution.py:119
  244.8 2.0 collective-permute-start.1
  247.6 0.9 fusion.28
  248.6 0.7 and.54
  249.3 1.3 fusion.34
  251.3 50.6 %reduce-scatter.8.cloned.1.call-done = bf16[2,512,768]{2,1,0:T(8,128)(2,1)} async-done(((bf16[2,2048,768]{2,1,0:T(8,128)(2,1)}), bf16[2,512,768]{2,1,0:T(8,128)(2,1)}) %reduce-scatter.8.cloned.1.call-update) | async-done | bytes 1572880 | tf_op jit(solution)/shard_map/reduce_scatter | solution.py:116
  301.8 1.5 collective-permute-start
  303.3 21.0 %collective-permute-done.1 = bf16[2,384,512]{2,1,0:T(8,128)(2,1)S(1)} collective-permute-done((bf16[2,384,512]{2,1,0:T(8,128)(2,1)S(1)}, bf16[2,384,512]{2,1,0:T(8,128)(2,1)S(1)}, u32[]{:S(2)}, u32[]{:S(2)}) %collective-permute-start.1) | collective-permute-done | bytes 786464 | tf_op jit(solution)/shard_map/ppermute | solution.py:18
  324.3 1.2 select_convert_fusion.1
  325.6 4.0 %convolution_bitcast_fusion.4 = f32[128,1280]{0,1:T(8,128)S(1)} fusion(bf16[1280,2048]{1,0:T(8,128)(2,1)} %bitcast.22, bf16[128,2048]{1,0:T(8,128)(2,1)S(1)} %copy-done), kind=kOutput, calls=%fused_computation.26 | convolution fusion | flops 671088640 | bytes 6422528 | tf_op jit(solution)/shard_map/dot_general | solution.py:130
  329.6 7.0 %gather_fusion = f32[1024]{0:T(1024)S(1)} fusion(f32[128,1280]{0,1:T(8,128)S(1)} %convolution_bitcast_fusion.4, s32[1024]{0:T(1024)S(1)} %reshape.199), kind=kCustom, calls=%fused_computation | custom fusion | bytes 16384 | tf_op jit(solution)/shard_map/jit(take_along_axis)/gather | solution.py:133
  337.4 5.7 %convolution_convert_fusion.6 = bf16[128,2048]{1,0:T(8,128)(2,1)} fusion(f32[128,1280]{0,1:T(8,128)S(1)} %select_n.91, bf16[1280,2048]{1,0:T(8,128)(2,1)} %bitcast.22), kind=kOutput, calls=%fused_computation.28 | convolution fusion | flops 4026793984 | bytes 6422528 | tf_op jit(solution)/shard_map/dot_general | solution.py:126
  343.1 4.3 %convolution_convert_fusion.5 = bf16[128,2048]{1,0:T(8,128)(2,1)} fusion(pred[128,1280]{0,1:T(32,128)(4,1)S(1)} %copy-done.9, bf16[1280,2048]{1,0:T(8,128)(2,1)} %bitcast.25), kind=kOutput, calls=%fused_computation.27 | convolution fusion | flops 671350784 | bytes 5931008 | tf_op jit(solution)/shard_map/dot_general | solution.py:134
  347.5 10.1 %collective-permute-done = bf16[2,512,768]{2,1,0:T(8,128)(2,1)} collective-permute-done((bf16[2,512,768]{2,1,0:T(8,128)(2,1)}, bf16[2,512,768]{2,1,0:T(8,128)(2,1)}, u32[]{:S(2)}, u32[]{:S(2)}) %collective-permute-start) | collective-permute-done | bytes 1572896 | tf_op jit(solution)/shard_map/ppermute | solution.py:18
  357.5 3.3 select_convert_fusion
  (85 shorter events, 5.8 us)
Async XLA Ops:
  7.2 13.7 %copy-start = (bf16[128,2048]{1,0:T(8,128)(2,1)S(1)}, bf16[128,2048]{1,0:T(8,128)(2,1)}, u32[]{:S(2)}) copy-start(bf16[128,2048]{1,0:T(8,128)(2,1)} %param.10) | copy-start | bytes 1572868
  7.2 1.6 copy-start.12
  8.2 12.3 %copy-start.10 = (s32[128,64]{0,1:T(8,128)}, s32[128,64]{0,1:T(8,128)S(1)}, u32[]{:S(2)}) copy-start(s32[128,64]{0,1:T(8,128)S(1)} %subtract_select_fusion) | copy-start | bytes 98308
  12.7 7.7 %copy-start.13 = (s32[128,8]{0,1:T(8,128)S(1)}, s32[128,8]{0,1:T(8,128)}, u32[]{:S(2)}) copy-start(s32[128,8]{0,1:T(8,128)} %param.8) | copy-start | bytes 12292
  12.7 7.7 %copy-start.16 = (f32[128,8]{0,1:T(8,128)S(1)}, f32[128,8]{0,1:T(8,128)}, u32[]{:S(2)}) copy-start(f32[128,8]{0,1:T(8,128)} %param.9) | copy-start | bytes 12292
  12.7 73.6 %all-to-all-start = ((bf16[32,40,2048]{2,1,0:T(8,128)(2,1)}), bf16[32,40,2048]{2,1,0:T(8,128)(2,1)}, u32[]{:S(2)}, u32[]{:S(2)}) async-start(bf16[32,40,2048]{2,1,0:T(8,128)(2,1)} %bitcast.86), calls=%async_computation | async-start | bytes 10485760 | tf_op jit(solution)/shard_map/all_to_all | solution.py:49
  86.2 70.8 %all-to-all-start.1 = ((bf16[32,40,2048]{2,1,0:T(8,128)(2,1)}), bf16[32,40,2048]{2,1,0:T(8,128)(2,1)}, u32[]{:S(2)}, u32[]{:S(2)}) async-start(bf16[32,40,2048]{2,1,0:T(8,128)(2,1)} %bitcast.85), calls=%async_computation.1 | async-start | bytes 10485760 | tf_op jit(solution)/shard_map/all_to_all | solution.py:50
  91.1 104.6 %reduce-scatter.4.cloned.1.call-start = ((), (), s32[]{:S(2)}) async-start(), calls=%async_computation.7 | async-start | bytes 1966080 | tf_op jit(solution)/shard_map/reduce_scatter | solution.py:96
  94.8 6.8 %copy-start.3 = (bf16[32,24,2048]{2,1,0:T(8,128)(2,1)}, bf16[32,24,2048]{2,1,0:T(8,128)(2,1)S(1)}, u32[]{:S(2)}) copy-start(bf16[32,24,2048]{2,1,0:T(8,128)(2,1)S(1)} %get-tuple-element.38) | copy-start | bytes 9437188
  94.8 9.2 %copy-start.1 = (bf16[32,24,2048]{2,1,0:T(8,128)(2,1)}, bf16[32,24,2048]{2,1,0:T(8,128)(2,1)S(1)}, u32[]{:S(2)}) copy-start(bf16[32,24,2048]{2,1,0:T(8,128)(2,1)S(1)} %get-tuple-element.39) | copy-start | bytes 9437188
  94.8 7.2 %copy-start.17 = (bf16[2,384,2048]{2,1,0:T(8,128)(2,1)S(1)}, bf16[2,384,2048]{2,1,0:T(8,128)(2,1)}, u32[]{:S(2)}) copy-start(bf16[2,384,2048]{2,1,0:T(8,128)(2,1)} %param.12) | copy-start | bytes 9437188
  101.7 2.2 copy-start.6
  101.7 3.0 slice-start
  102.0 3.3 slice-start.1
  108.0 2.2 copy-start.4
  169.1 70.8 %all-to-all-start.2 = ((bf16[32,40,2048]{2,1,0:T(8,128)(2,1)}), bf16[32,40,2048]{2,1,0:T(8,128)(2,1)}, u32[]{:S(2)}, u32[]{:S(2)}) async-start(bf16[32,40,2048]{2,1,0:T(8,128)(2,1)} %pad_maximum_fusion.1), calls=%async_computation.4 | async-start | bytes 10485760 | tf_op jit(solution)/shard_map/all_to_all | solution.py:77
  174.0 47.3 %reduce-scatter.6.cloned.1.call-start = ((), (), s32[]{:S(2)}) async-start(), calls=%async_computation.8 | async-start | bytes 1966080 | tf_op jit(solution)/shard_map/reduce_scatter | solution.py:96
  174.7 127.1 %reduce-scatter.8.cloned.1.call-start = ((), (), s32[]{:S(2)}) async-start(), calls=%async_computation.9 | async-start | bytes 7864320 | tf_op jit(solution)/shard_map/reduce_scatter | solution.py:116
  174.8 3.8 %copy-start.7 = (f32[768,768]{1,0:T(8,128)S(1)}, f32[768,768]{1,0:T(8,128)}, u32[]{:S(2)}) copy-start(f32[768,768]{1,0:T(8,128)} %copy-done.6) | copy-start | bytes 7077892
  174.8 4.7 %copy-start.18 = (bf16[2,384,2048]{2,1,0:T(8,128)(2,1)S(1)}, bf16[2,384,2048]{2,1,0:T(8,128)(2,1)}, u32[]{:S(2)}) copy-start(bf16[2,384,2048]{2,1,0:T(8,128)(2,1)} %param.12) | copy-start | bytes 9437188
  174.8 6.9 %slice-start.2 = ((s8[6291456]{0:T(1024)(128)(4,1)}), s8[4194304]{0:T(1024)(128)(4,1)S(1)}, s32[]{:S(2)}) async-start(s8[6291456]{0:T(1024)(128)(4,1)} %bitcast.107), calls=%async_computation.12 | async-start | bytes 8388608
  179.5 2.2 slice-start.3
  184.6 1.7 copy-start.5
  222.4 5.1 %copy-start.2 = (bf16[32,24,2048]{2,1,0:T(8,128)(2,1)S(1)}, bf16[32,24,2048]{2,1,0:T(8,128)(2,1)}, u32[]{:S(2)}) copy-start(bf16[32,24,2048]{2,1,0:T(8,128)(2,1)} %copy-done.1) | copy-start | bytes 9437188
  239.9 6.9 %copy-start.11 = (s32[128,64]{0,1:T(8,128)S(1)}, s32[128,64]{0,1:T(8,128)}, u32[]{:S(2)}) copy-start(s32[128,64]{0,1:T(8,128)} %copy-done.10) | copy-start | bytes 98308
  239.9 103.3 %all-to-all-start.3 = ((bf16[32,40,2048]{2,1,0:T(8,128)(2,1)}), bf16[32,40,2048]{2,1,0:T(8,128)(2,1)}, u32[]{:S(2)}, u32[]{:S(2)}) async-start(bf16[32,40,2048]{2,1,0:T(8,128)(2,1)} %pad_maximum_fusion.2), calls=%async_computation.5 | async-start | bytes 10485760 | tf_op jit(solution)/shard_map/all_to_all | solution.py:119
  244.8 79.5 %collective-permute-start.1 = (bf16[2,384,512]{2,1,0:T(8,128)(2,1)S(1)}, bf16[2,384,512]{2,1,0:T(8,128)(2,1)S(1)}, u32[]{:S(2)}, u32[]{:S(2)}) collective-permute-start(bf16[2,384,512]{2,1,0:T(8,128)(2,1)S(1)} %pad_maximum_fusion.5), channel_id=1, source_target_pairs={{0,8},{8,0},{4,12},{12,4},{16,24},{24,16},{20,28},{28,20},{32,40},... | collective-permute-start | bytes 2359304 | tf_op jit(solution)/shard_map/ppermute | solution.py:18
  246.8 0.6 copy-start.14
  301.8 55.7 %collective-permute-start = (bf16[2,512,768]{2,1,0:T(8,128)(2,1)}, bf16[2,512,768]{2,1,0:T(8,128)(2,1)}, u32[]{:S(2)}, u32[]{:S(2)}) collective-permute-start(bf16[2,512,768]{2,1,0:T(8,128)(2,1)} %reduce-scatter.8.cloned.1.call-done), channel_id=1, source_target_pairs={{0,8},{8,0},{4,12},{12,4},{16,24},{24,16},{20,28},{28,20},{32,40},... | collective-permute-start | bytes 4718600 | tf_op jit(solution)/shard_map/ppermute | solution.py:18
  329.6 7.2 %copy-start.15 = (s32[128,8]{0,1:T(8,128)S(1)}, s32[128,8]{0,1:T(8,128)}, u32[]{:S(2)}) copy-start(s32[128,8]{0,1:T(8,128)} %copy-done.14) | copy-start | bytes 12292
  337.4 5.8 %copy-start.9 = (pred[128,1280]{0,1:T(32,128)(4,1)S(1)}, pred[128,1280]{0,1:T(32,128)(4,1)}, u32[]{:S(2)}) copy-start(pred[128,1280]{0,1:T(32,128)(4,1)} %and.54) | copy-start | bytes 491524
  343.1 14.4 %copy-start.8 = (bf16[2,512,768]{2,1,0:T(8,128)(2,1)S(1)}, bf16[2,512,768]{2,1,0:T(8,128)(2,1)}, u32[]{:S(2)}) copy-start(bf16[2,512,768]{2,1,0:T(8,128)(2,1)} %reduce-scatter.8.cloned.1.call-done) | copy-start | bytes 4718596
Sparse Core Ops, SparseCore 0:
  169.2 23.4 reduce-scatter.3
  195.7 25.4 reduce-scatter.5
  240.0 61.7 reduce-scatter.7

commit v8 on v7

--- a/solution.py
+++ b/solution.py
@@ -77,25 +77,25 @@
     home_out = lax.all_to_all(send_out, "expert", split_axis=0, concat_axis=0, tiled=True)
     whole_grad = recv_grad.reshape(groups * lanes, model_width)
     lane = jnp.arange(lanes, dtype=jnp.int32)[None, :, None]
-    windows, seconds = [], []
+    seconds = []
     for local in range(per_device):
         low = local * shift
         hidden = forwards[local][5].reshape(groups, window, FF)
-        own = (place < CAP) if local == 0 else (place >= window - CAP)
         padded = jnp.pad(hidden, ((0, 0), (low, lanes - window - low), (0, 0)))
         mine = (lane < CAP) if local == 0 else (lane >= CAP)
         padded = jnp.where(mine, padded, jnp.zeros((), jnp.bfloat16)).reshape(groups * lanes, FF)
         seconds.append(jnp.dot(padded.T, whole_grad, preferred_element_type=jnp.float32))
-    recv_grad, seconds = lax.optimization_barrier((recv_grad, seconds))
+    grad_second = jnp.stack(seconds)
+    recv_grad, grad_second = lax.optimization_barrier((recv_grad, grad_second))
+    windows = []
     for local in range(per_device):
         low = local * shift
         own = (place < CAP) if local == 0 else (place >= window - CAP)
         rows_grad = jnp.where(own, recv_grad[:, low:low + window], jnp.zeros((), jnp.bfloat16))
         windows.append(rows_grad.reshape(groups * window, model_width))
-    reduced_down = jnp.stack([
-        lax.psum_scatter(part.astype(jnp.bfloat16), "dp", scatter_dimension=1, tiled=True)
-        for part in seconds
-    ])
+    reduced_down = lax.psum_scatter(
+        grad_second.astype(jnp.bfloat16), "dp", scatter_dimension=2, tiled=True
+    )
     backs, firsts = [], []
     for local in range(per_device):
         rows_x, pre_gate, up_part, sigmoid_gate, activated, hidden, _ = forwards[local]

time: 373 us -> 373 us (level)
    all_to_all x1, waiting for transfers between devices: 6.22 us -> 23.3 us  [body(): lax.all_to_all(send_out, 'expert', split_axis=0, concat_axis=0, tiled=True)]
    reduce_scatter x2 -> x1, waiting for transfers between devices: 25.5 us -> 10.1 us  [body(): lax.psum_scatter(grad_second.astype(jnp.bfloat16), 'dp', scatter_dimensio...]
  transfers between devices with their start and end apart: 9 -> 8, of which waited for: 7 -> 7; matrix products, arithmetic and copies ran while one was open for 22% -> 22% of each run, Pallas kernels for 0% -> 0%
where the time goes in v8:
time: 373 us; the launch traced here: 368 us
  waiting for transfers between devices  222 us (60%)
  matrix products  62.6 us (17%)
  starting transfers between devices  26.1 us (7%)
  other arithmetic  24.7 us (7%)
  local copies, waits for them, and re-layouts  16.7 us (4%)
  between operations  15.8 us (4%)
    all_to_all x1, waiting for transfers between devices, body(): lax.all_to_all(send_x, 'expert', split_axis=0, concat_axis=0, tiled=True)  61.6 us
    reduce_scatter x1, waiting for transfers between devices, body(): lax.psum_scatter(grad_first.astype(jnp.bfloat16), 'dp', scatter_dimension...  52.4 us
    all_to_all x1, waiting for transfers between devices, body(): lax.all_to_all(send_grad, 'expert', split_axis=0, concat_axis=0, tiled=True)  43.4 us
    ppermute x2, waiting for transfers between devices, swapped(): return lax.ppermute(block, axis, route)  31.2 us
    all_to_all x1, waiting for transfers between devices, body(): lax.all_to_all(send_out, 'expert', split_axis=0, concat_axis=0, tiled=True)  23.3 us
    reduce_scatter x1, waiting for transfers between devices, body(): lax.psum_scatter(grad_second.astype(jnp.bfloat16), 'dp', scatter_dimensio...  10.1 us
    dot_general x2, matrix products, body(): jnp.dot(padded.T, whole_grad, preferred_element_type=jnp.float32)  9.64 us
    dot_general x2, matrix products, body(): jnp.dot(rows_x, weight_in[local], preferred_element_type=jnp.float32)  9.38 us
  transfers between devices with their start and end apart: 8, of which 7 were waited for; matrix products, arithmetic and copies ran while one was open for 22% of the time, Pallas kernels for 0%

profile of v8, /device:TPU:0, one launch (start us, length us, event | category | flops | bytes accessed | tf_op | source)
XLA Modules:
  0.0 367.9 jit_solution(18055465511038175690)
XLA Ops:
  7.2 0.8 fusion.31
  8.8 3.8 %convolution_convert_fusion = bf16[1280,2048]{1,0:T(8,128)(2,1)} fusion(pred[128,1280]{0,1:T(32,128)(4,1)S(1)} %compare_and_fusion, bf16[128,2048]{1,0:T(8,128)(2,1)S(1)} %copy-done.10), kind=kOutput, calls=%fused_computation.3 | convolution fusion | flops 673710080 | bytes 5931008 | tf_op jit(solution)/shard_map/dot_general | solution.py:43
  12.7 7.7 %all-to-all-start = ((bf16[32,40,2048]{2,1,0:T(8,128)(2,1)}), bf16[32,40,2048]{2,1,0:T(8,128)(2,1)}, u32[]{:S(2)}, u32[]{:S(2)}) async-start(bf16[32,40,2048]{2,1,0:T(8,128)(2,1)} %bitcast.86), calls=%async_computation | async-start | bytes 10485760 | tf_op jit(solution)/shard_map/all_to_all | solution.py:49
  20.8 3.9 %multiply_convert_fusion = bf16[1280,2048]{1,0:T(8,128)(2,1)} fusion(pred[128,1280]{0,1:T(32,128)(4,1)S(1)} %compare_and_fusion, bf16[128,2048]{1,0:T(8,128)(2,1)S(1)} %copy-done, f32[1280]{0:T(1024)S(1)} %mul.62), kind=kOutput, calls=%fused_computation.2 | convolution fusion | flops 676331520 | bytes 5936128 | tf_op jit(solution)/shard_map/dot_general | solution.py:44
  24.7 61.6 %all-to-all-done = bf16[32,40,2048]{2,1,0:T(8,128)(2,1)} async-done(((bf16[32,40,2048]{2,1,0:T(8,128)(2,1)}), bf16[32,40,2048]{2,1,0:T(8,128)(2,1)}, u32[]{:S(2)}, u32[]{:S(2)}) %all-to-all-start) | async-done | bytes 5242912 | tf_op jit(solution)/shard_map/all_to_all | solution.py:49
  86.2 4.9 %all-to-all-start.1 = ((bf16[32,40,2048]{2,1,0:T(8,128)(2,1)}), bf16[32,40,2048]{2,1,0:T(8,128)(2,1)}, u32[]{:S(2)}, u32[]{:S(2)}) async-start(bf16[32,40,2048]{2,1,0:T(8,128)(2,1)} %bitcast.85), calls=%async_computation.1 | async-start | bytes 10485760 | tf_op jit(solution)/shard_map/all_to_all | solution.py:50
  91.4 3.4 fusion.37
  94.8 6.8 %fusion.4 = f32[768,768]{1,0:T(8,128)S(1)} fusion(bf16[768,2048]{1,0:T(8,128)(2,1)S(1)} %bitcast.97, bf16[2,2048,768]{2,1,0:T(8,128)(2,1)} %param.11), kind=kOutput, calls=%fused_computation.17 | convolution fusion | flops 2415919104 | bytes 8650752 | tf_op jit(solution)/shard_map/dot_general | solution.py:58
  102.0 1.8 convolution_convert_fusion.4
  104.0 0.7 slice-done
  104.7 0.7 slice-done.1
  105.4 2.6 fusion.1
  108.3 1.8 convolution_convert_fusion.3
  110.5 3.1 pad_maximum_fusion.2
  113.6 43.4 %all-to-all-done.1 = bf16[32,40,2048]{2,1,0:T(8,128)(2,1)} async-done(((bf16[32,40,2048]{2,1,0:T(8,128)(2,1)}), bf16[32,40,2048]{2,1,0:T(8,128)(2,1)}, u32[]{:S(2)}, u32[]{:S(2)}) %all-to-all-start.1) | async-done | bytes 5242912 | tf_op jit(solution)/shard_map/all_to_all | solution.py:50
  157.0 4.8 %convolution_bitcast_fusion.2 = bf16[1,384,2048]{2,1,0:T(8,128)(2,1)S(1)} fusion(bf16[32,40,2048]{2,1,0:T(8,128)(2,1)} %all-to-all-done.1, bf16[32,24,384]{2,1,0:T(8,128)(2,1)S(1)} %bitcast.102, pred[40]{0:T(512)(128)(4,1)S(1)} %iota_compare_fusion.7), kind=kOutput, calls=%fused_computation.21 | convolution fusion | flops 2013757440 | bytes 7405608 | tf_op jit(solution)/shard_map/dot_general | solution.py:87
  161.8 4.8 %convolution_bitcast_fusion.3 = bf16[1,384,2048]{2,1,0:T(8,128)(2,1)S(1)} fusion(bf16[32,40,2048]{2,1,0:T(8,128)(2,1)} %all-to-all-done.1, bf16[32,24,384]{2,1,0:T(8,128)(2,1)S(1)} %bitcast.101, pred[40]{0:T(512)(128)(4,1)S(1)} %iota_compare_fusion.8), kind=kOutput, calls=%fused_computation.22 | convolution fusion | flops 2013757440 | bytes 7405608 | tf_op jit(solution)/shard_map/dot_general | solution.py:87
  166.6 2.0 pad_maximum_fusion.1
  168.7 4.9 %all-to-all-start.2 = ((bf16[32,40,2048]{2,1,0:T(8,128)(2,1)}), bf16[32,40,2048]{2,1,0:T(8,128)(2,1)}, u32[]{:S(2)}, u32[]{:S(2)}) async-start(bf16[32,40,2048]{2,1,0:T(8,128)(2,1)} %pad_maximum_fusion.2), calls=%async_computation.3 | async-start | bytes 10485760 | tf_op jit(solution)/shard_map/all_to_all | solution.py:77
  173.7 3.9 %slice_select_fusion.1 = (bf16[32,24,2048]{2,1,0:T(8,128)(2,1)S(1)}, bf16[32,24,2048]{2,1,0:T(8,128)(2,1)S(1)}) fusion(bf16[32,40,2048]{2,1,0:T(8,128)(2,1)} %all-to-all-done.1, pred[24]{0:T(512)(128)(4,1)S(1)} %get-tuple-element.45, pred[24]{0:T(512)(128)(4,1)S(1)} %get-tuple-element.44), kind=kLoop, calls=%fused_computation.20 | loop fusion | flops 3145728 | bytes 12582960 | tf_op jit(solution)/shard_map/jit(_where)/select_n | solution.py:94
  177.8 0.9 copy-done.14
  178.8 2.1 multiply_convert_fusion.4
  180.9 2.9 convolution_convert_fusion.2
  184.0 1.6 copy-done.5
  185.5 2.2 multiply_convert_fusion.2
  187.7 2.9 convolution_convert_fusion.1
  190.8 1.1 pad_maximum_fusion.4
  192.1 2.8 pad_maximum_fusion.3
  194.9 10.1 %reduce-scatter.3.cloned.1.call-done = bf16[2,384,512]{2,1,0:T(8,128)(2,1)} async-done(((bf16[2,384,2048]{2,1,0:T(8,128)(2,1)}), bf16[2,384,512]{2,1,0:T(8,128)(2,1)}) %reduce-scatter.3.cloned.1.call-update) | async-done | bytes 786448 | tf_op jit(solution)/shard_map/reduce_scatter | solution.py:96
  205.0 5.0 %convolution_bitcast_fusion.1 = bf16[1,2048,768]{2,1,0:T(8,128)(2,1)S(1)} fusion(bf16[768,2048]{1,0:T(8,128)(2,1)} %bitcast.98, bf16[768,768]{1,0:T(8,128)(2,1)} %pad_maximum_fusion.4), kind=kOutput, calls=%fused_computation.8 | convolution fusion | flops 2415919104 | bytes 7471104 | tf_op jit(solution)/shard_map/dot_general | solution.py:114
  210.1 2.9 convolution_bitcast_fusion
  213.0 3.2 pad_maximum_fusion
  216.2 23.3 %all-to-all-done.2 = bf16[32,40,2048]{2,1,0:T(8,128)(2,1)} async-done(((bf16[32,40,2048]{2,1,0:T(8,128)(2,1)}), bf16[32,40,2048]{2,1,0:T(8,128)(2,1)}, u32[]{:S(2)}, u32[]{:S(2)}) %all-to-all-start.2) | async-done | bytes 5242912 | tf_op jit(solution)/shard_map/all_to_all | solution.py:77
  239.5 5.0 %all-to-all-start.3 = ((bf16[32,40,2048]{2,1,0:T(8,128)(2,1)}), bf16[32,40,2048]{2,1,0:T(8,128)(2,1)}, u32[]{:S(2)}, u32[]{:S(2)}) async-start(bf16[32,40,2048]{2,1,0:T(8,128)(2,1)} %pad_maximum_fusion.3), calls=%async_computation.4 | async-start | bytes 10485760 | tf_op jit(solution)/shard_map/all_to_all | solution.py:119
  245.0 0.7 and.54
  245.8 0.6 fusion.34
  247.1 1.9 collective-permute-start.1
  249.1 52.4 %reduce-scatter.5.cloned.1.call-done = bf16[2,512,768]{2,1,0:T(8,128)(2,1)} async-done(((bf16[2,2048,768]{2,1,0:T(8,128)(2,1)}), bf16[2,512,768]{2,1,0:T(8,128)(2,1)}) %reduce-scatter.5.cloned.1.call-update) | async-done | bytes 1572880 | tf_op jit(solution)/shard_map/reduce_scatter | solution.py:116
  301.5 1.5 collective-permute-start
  302.9 4.0 %convolution_bitcast_fusion.4 = f32[128,1280]{0,1:T(8,128)S(1)} fusion(bf16[1280,2048]{1,0:T(8,128)(2,1)} %bitcast.22, bf16[128,2048]{1,0:T(8,128)(2,1)S(1)} %copy-done), kind=kOutput, calls=%fused_computation.27 | convolution fusion | flops 671088640 | bytes 6422528 | tf_op jit(solution)/shard_map/dot_general | solution.py:130
  307.0 7.0 %gather_fusion = f32[1024]{0:T(1024)S(1)} fusion(f32[128,1280]{0,1:T(8,128)S(1)} %convolution_bitcast_fusion.4, s32[1024]{0:T(1024)S(1)} %reshape.199), kind=kCustom, calls=%fused_computation | custom fusion | bytes 16384 | tf_op jit(solution)/shard_map/jit(take_along_axis)/gather | solution.py:133
  314.1 0.6 and_select_fusion
  314.8 5.7 %convolution_convert_fusion.6 = bf16[128,2048]{1,0:T(8,128)(2,1)} fusion(f32[128,1280]{0,1:T(8,128)S(1)} %select_n.91, bf16[1280,2048]{1,0:T(8,128)(2,1)} %bitcast.22), kind=kOutput, calls=%fused_computation.29 | convolution fusion | flops 4026793984 | bytes 6422528 | tf_op jit(solution)/shard_map/dot_general | solution.py:126
  320.5 3.6 collective-permute-done.1
  324.1 1.2 select_convert_fusion.1
  325.3 4.4 %convolution_convert_fusion.5 = bf16[128,2048]{1,0:T(8,128)(2,1)} fusion(pred[128,1280]{0,1:T(32,128)(4,1)} %and.54, bf16[1280,2048]{1,0:T(8,128)(2,1)} %bitcast.25), kind=kOutput, calls=%fused_computation.28 | convolution fusion | flops 671350784 | bytes 5931008 | tf_op jit(solution)/shard_map/dot_general | solution.py:134
  329.7 27.6 %collective-permute-done = bf16[2,512,768]{2,1,0:T(8,128)(2,1)} collective-permute-done((bf16[2,512,768]{2,1,0:T(8,128)(2,1)}, bf16[2,512,768]{2,1,0:T(8,128)(2,1)}, u32[]{:S(2)}, u32[]{:S(2)}) %collective-permute-start) | collective-permute-done | bytes 1572896 | tf_op jit(solution)/shard_map/ppermute | solution.py:18
  357.3 3.3 select_convert_fusion
  (76 shorter events, 4.0 us)
Async XLA Ops:
  7.2 13.6 %copy-start = (bf16[128,2048]{1,0:T(8,128)(2,1)S(1)}, bf16[128,2048]{1,0:T(8,128)(2,1)}, u32[]{:S(2)}) copy-start(bf16[128,2048]{1,0:T(8,128)(2,1)} %param.10) | copy-start | bytes 1572868
  7.2 1.6 copy-start.10
  12.7 7.7 %copy-start.11 = (s32[128,8]{0,1:T(8,128)S(1)}, s32[128,8]{0,1:T(8,128)}, u32[]{:S(2)}) copy-start(s32[128,8]{0,1:T(8,128)} %param.8) | copy-start | bytes 12292
  12.7 7.7 %copy-start.12 = (f32[128,8]{0,1:T(8,128)S(1)}, f32[128,8]{0,1:T(8,128)}, u32[]{:S(2)}) copy-start(f32[128,8]{0,1:T(8,128)} %param.9) | copy-start | bytes 12292
  12.7 73.6 %all-to-all-start = ((bf16[32,40,2048]{2,1,0:T(8,128)(2,1)}), bf16[32,40,2048]{2,1,0:T(8,128)(2,1)}, u32[]{:S(2)}, u32[]{:S(2)}) async-start(bf16[32,40,2048]{2,1,0:T(8,128)(2,1)} %bitcast.86), calls=%async_computation | async-start | bytes 10485760 | tf_op jit(solution)/shard_map/all_to_all | solution.py:49
  86.2 70.8 %all-to-all-start.1 = ((bf16[32,40,2048]{2,1,0:T(8,128)(2,1)}), bf16[32,40,2048]{2,1,0:T(8,128)(2,1)}, u32[]{:S(2)}, u32[]{:S(2)}) async-start(bf16[32,40,2048]{2,1,0:T(8,128)(2,1)} %bitcast.85), calls=%async_computation.1 | async-start | bytes 10485760 | tf_op jit(solution)/shard_map/all_to_all | solution.py:50
  91.1 113.9 %reduce-scatter.3.cloned.1.call-start = ((), (), s32[]{:S(2)}) async-start(), calls=%async_computation.6 | async-start | bytes 3932160 | tf_op jit(solution)/shard_map/reduce_scatter | solution.py:96
  94.8 6.8 %copy-start.3 = (bf16[32,24,2048]{2,1,0:T(8,128)(2,1)}, bf16[32,24,2048]{2,1,0:T(8,128)(2,1)S(1)}, u32[]{:S(2)}) copy-start(bf16[32,24,2048]{2,1,0:T(8,128)(2,1)S(1)} %get-tuple-element.36) | copy-start | bytes 9437188
  94.8 9.2 %copy-start.1 = (bf16[32,24,2048]{2,1,0:T(8,128)(2,1)}, bf16[32,24,2048]{2,1,0:T(8,128)(2,1)S(1)}, u32[]{:S(2)}) copy-start(bf16[32,24,2048]{2,1,0:T(8,128)(2,1)S(1)} %get-tuple-element.37) | copy-start | bytes 9437188
  94.8 7.2 %copy-start.13 = (bf16[2,384,2048]{2,1,0:T(8,128)(2,1)S(1)}, bf16[2,384,2048]{2,1,0:T(8,128)(2,1)}, u32[]{:S(2)}) copy-start(bf16[2,384,2048]{2,1,0:T(8,128)(2,1)} %param.12) | copy-start | bytes 9437188
  101.6 2.2 copy-start.6
  101.7 3.0 slice-start
  102.0 3.3 slice-start.1
  108.0 2.2 copy-start.4
  168.7 70.8 %all-to-all-start.2 = ((bf16[32,40,2048]{2,1,0:T(8,128)(2,1)}), bf16[32,40,2048]{2,1,0:T(8,128)(2,1)}, u32[]{:S(2)}, u32[]{:S(2)}) async-start(bf16[32,40,2048]{2,1,0:T(8,128)(2,1)} %pad_maximum_fusion.2), calls=%async_computation.3 | async-start | bytes 10485760 | tf_op jit(solution)/shard_map/all_to_all | solution.py:77
  173.6 127.9 %reduce-scatter.5.cloned.1.call-start = ((), (), s32[]{:S(2)}) async-start(), calls=%async_computation.7 | async-start | bytes 7864320 | tf_op jit(solution)/shard_map/reduce_scatter | solution.py:116
  173.7 4.1 %copy-start.7 = (f32[768,768]{1,0:T(8,128)S(1)}, f32[768,768]{1,0:T(8,128)}, u32[]{:S(2)}) copy-start(f32[768,768]{1,0:T(8,128)} %copy-done.6) | copy-start | bytes 7077892
  173.7 5.1 %copy-start.14 = (bf16[2,384,2048]{2,1,0:T(8,128)(2,1)S(1)}, bf16[2,384,2048]{2,1,0:T(8,128)(2,1)}, u32[]{:S(2)}) copy-start(bf16[2,384,2048]{2,1,0:T(8,128)(2,1)} %param.12) | copy-start | bytes 9437188
  173.7 7.2 %slice-start.2 = ((s8[6291456]{0:T(1024)(128)(4,1)}), s8[4194304]{0:T(1024)(128)(4,1)S(1)}, s32[]{:S(2)}) async-start(s8[6291456]{0:T(1024)(128)(4,1)} %bitcast.105), calls=%async_computation.10 | async-start | bytes 8388608
  178.7 2.2 slice-start.3
  183.8 1.7 copy-start.5
  205.0 5.1 %copy-start.2 = (bf16[32,24,2048]{2,1,0:T(8,128)(2,1)S(1)}, bf16[32,24,2048]{2,1,0:T(8,128)(2,1)}, u32[]{:S(2)}) copy-start(bf16[32,24,2048]{2,1,0:T(8,128)(2,1)} %copy-done.1) | copy-start | bytes 9437188
  239.5 6.3 %copy-start.15 = (s32[32]{0:T(128)S(1)}, s32[32]{0:T(128)}, u32[]{:S(2)}) copy-start(s32[32]{0:T(128)} %param.13) | copy-start | bytes 388
  239.5 7.6 %copy-start.9 = (bf16[2,384,512]{2,1,0:T(8,128)(2,1)S(1)}, bf16[2,384,512]{2,1,0:T(8,128)(2,1)}, u32[]{:S(2)}) copy-start(bf16[2,384,512]{2,1,0:T(8,128)(2,1)} %reduce-scatter.3.cloned.1.call-done) | copy-start | bytes 2359300
  239.5 85.8 %all-to-all-start.3 = ((bf16[32,40,2048]{2,1,0:T(8,128)(2,1)}), bf16[32,40,2048]{2,1,0:T(8,128)(2,1)}, u32[]{:S(2)}, u32[]{:S(2)}) async-start(bf16[32,40,2048]{2,1,0:T(8,128)(2,1)} %pad_maximum_fusion.3), calls=%async_computation.4 | async-start | bytes 10485760 | tf_op jit(solution)/shard_map/all_to_all | solution.py:119
  247.1 76.9 %collective-permute-start.1 = (bf16[2,384,512]{2,1,0:T(8,128)(2,1)S(1)}, bf16[2,384,512]{2,1,0:T(8,128)(2,1)S(1)}, u32[]{:S(2)}, u32[]{:S(2)}) collective-permute-start(bf16[2,384,512]{2,1,0:T(8,128)(2,1)S(1)} %copy-done.9), channel_id=1, source_target_pairs={{0,8},{8,0},{4,12},{12,4},{16,24},{24,16},{20,28},{28,20},{32,40},... | collective-permute-start | bytes 2359304 | tf_op jit(solution)/shard_map/ppermute | solution.py:18
  301.5 55.9 %collective-permute-start = (bf16[2,512,768]{2,1,0:T(8,128)(2,1)}, bf16[2,512,768]{2,1,0:T(8,128)(2,1)}, u32[]{:S(2)}, u32[]{:S(2)}) collective-permute-start(bf16[2,512,768]{2,1,0:T(8,128)(2,1)} %reduce-scatter.5.cloned.1.call-done), channel_id=1, source_target_pairs={{0,8},{8,0},{4,12},{12,4},{16,24},{24,16},{20,28},{28,20},{32,40},... | collective-permute-start | bytes 4718600 | tf_op jit(solution)/shard_map/ppermute | solution.py:18
  325.3 32.0 %copy-start.8 = (bf16[2,512,768]{2,1,0:T(8,128)(2,1)S(1)}, bf16[2,512,768]{2,1,0:T(8,128)(2,1)}, u32[]{:S(2)}) copy-start(bf16[2,512,768]{2,1,0:T(8,128)(2,1)} %reduce-scatter.5.cloned.1.call-done) | copy-start | bytes 4718596
Sparse Core Ops, SparseCore 0:
  168.8 36.1 reduce-scatter.2
  239.6 61.7 reduce-scatter.4

commit v9 on v3

--- a/solution.py
+++ b/solution.py
@@ -91,17 +91,20 @@
             jnp.bfloat16
         )
         backs.append(row_grad.reshape(groups, window, model_width))
-        firsts.append(jnp.dot(rows_x.T, proj_grad, preferred_element_type=jnp.float32))
-        seconds.append(jnp.dot(hidden.T, rows_grad, preferred_element_type=jnp.float32))
-    grad_first = jnp.stack(firsts)
-    grad_second = jnp.stack(seconds)
+        firsts.append((rows_x, proj_grad))
+        seconds.append((hidden, rows_grad))
+    send_back, firsts, seconds = lax.optimization_barrier((merged(backs), firsts, seconds))
+    firsts = [jnp.dot(a.T, b, preferred_element_type=jnp.float32) for a, b in firsts]
+    seconds = [jnp.dot(a.T, b, preferred_element_type=jnp.float32) for a, b in seconds]
+    grad_first, grad_second, home_out = lax.optimization_barrier(
+        (jnp.stack(firsts), jnp.stack(seconds), home_out)
+    )
     reduced_in = lax.psum_scatter(
         grad_first.astype(jnp.bfloat16), "dp", scatter_dimension=1, tiled=True
     )
     reduced_down = lax.psum_scatter(
         grad_second.astype(jnp.bfloat16), "dp", scatter_dimension=2, tiled=True
     )
-    send_back, reduced_in = lax.optimization_barrier((merged(backs), reduced_in))
     home_grad = lax.all_to_all(send_back, "expert", split_axis=0, concat_axis=0, tiled=True)
     partner_in, partner_down = swapped((reduced_in, reduced_down), "expert", 1)
     held_in = jnp.where(my_flag == 1, partner_in, reduced_in).astype(jnp.float32)

time: 386 us -> 374 us (0.969)
  waiting for transfers between devices: 235 us -> 225 us
    ppermute x2, waiting for transfers between devices: 66.5 us -> 7.35 us  [swapped(): return lax.ppermute(block, axis, route)]
    all_to_all x1, waiting for transfers between devices: 8.82 us -> 31 us  [body(): lax.all_to_all(send_out, 'expert', split_axis=0, concat_axis=0, tiled=True)]
    reduce_scatter x1, waiting for transfers between devices: 34.1 us -> 53.8 us  [body(): lax.psum_scatter(grad_first.astype(jnp.bfloat16), 'dp', scatter_dimension...]
    reduce_scatter x1, waiting for transfers between devices: 21.6 us -> 28.4 us  [body(): lax.psum_scatter(grad_second.astype(jnp.bfloat16), 'dp', scatter_dimensio...]
  transfers between devices with their start and end apart: 8 -> 8, of which waited for: 6 -> 6; matrix products, arithmetic and copies ran while one was open for 19% -> 22% of each run, Pallas kernels for 0% -> 0%
where the time goes in v9:
time: 374 us; the launch traced here: 369 us
  waiting for transfers between devices  225 us (60%)
  matrix products  58.1 us (16%)
  starting transfers between devices  25.5 us (7%)
  other arithmetic  23.5 us (6%)
  local copies, waits for them, and re-layouts  20.8 us (6%)
  between operations  15.8 us (4%)
    all_to_all x1, waiting for transfers between devices, body(): lax.all_to_all(send_x, 'expert', split_axis=0, concat_axis=0, tiled=True)  61.6 us
    reduce_scatter x1, waiting for transfers between devices, body(): lax.psum_scatter(grad_first.astype(jnp.bfloat16), 'dp', scatter_dimension...  53.8 us
    all_to_all x1, waiting for transfers between devices, body(): lax.all_to_all(send_grad, 'expert', split_axis=0, concat_axis=0, tiled=True)  42.3 us
    all_to_all x1, waiting for transfers between devices, body(): lax.all_to_all(send_out, 'expert', split_axis=0, concat_axis=0, tiled=True)  31 us
    reduce_scatter x1, waiting for transfers between devices, body(): lax.psum_scatter(grad_second.astype(jnp.bfloat16), 'dp', scatter_dimensio...  28.4 us
    dot_general x4, matrix products, body(): jnp.dot(a.T, b, preferred_element_type=jnp.float32)  11.1 us
    dot_general x2, matrix products, body(): jnp.dot(rows_x, weight_in[local], preferred_element_type=jnp.float32)  9.77 us
    dot_general x2, matrix products, body(): jnp.dot(proj_grad, weight_in[local].T, preferred_element_type=jnp.float32)  8.12 us
  transfers between devices with their start and end apart: 8, of which 6 were waited for; matrix products, arithmetic and copies ran while one was open for 22% of the time, Pallas kernels for 0%

profile of v9, /device:TPU:0, one launch (start us, length us, event | category | flops | bytes accessed | tf_op | source)
XLA Modules:
  0.0 368.8 jit_solution(6374919766081263732)
XLA Ops:
  7.2 0.8 fusion.23
  8.8 3.9 %convolution_convert_fusion = bf16[1280,2048]{1,0:T(8,128)(2,1)} fusion(pred[128,1280]{0,1:T(32,128)(4,1)S(1)} %compare_and_fusion, bf16[128,2048]{1,0:T(8,128)(2,1)S(1)} %copy-done.19), kind=kOutput, calls=%fused_computation.3 | convolution fusion | flops 673710080 | bytes 5931008 | tf_op jit(solution)/shard_map/dot_general | solution.py:43
  12.7 7.7 %all-to-all-start = ((bf16[32,40,2048]{2,1,0:T(8,128)(2,1)}), bf16[32,40,2048]{2,1,0:T(8,128)(2,1)}, u32[]{:S(2)}, u32[]{:S(2)}) async-start(bf16[32,40,2048]{2,1,0:T(8,128)(2,1)} %bitcast.84), calls=%async_computation | async-start | bytes 10485760 | tf_op jit(solution)/shard_map/all_to_all | solution.py:49
  20.9 3.8 %multiply_convert_fusion = bf16[1280,2048]{1,0:T(8,128)(2,1)} fusion(pred[128,1280]{0,1:T(32,128)(4,1)S(1)} %compare_and_fusion, bf16[128,2048]{1,0:T(8,128)(2,1)S(1)} %copy-done, f32[1280]{0:T(1024)S(1)} %mul.62), kind=kOutput, calls=%fused_computation.2 | convolution fusion | flops 676331520 | bytes 5936128 | tf_op jit(solution)/shard_map/dot_general | solution.py:44
  24.7 61.6 %all-to-all-done = bf16[32,40,2048]{2,1,0:T(8,128)(2,1)} async-done(((bf16[32,40,2048]{2,1,0:T(8,128)(2,1)}), bf16[32,40,2048]{2,1,0:T(8,128)(2,1)}, u32[]{:S(2)}, u32[]{:S(2)}) %all-to-all-start) | async-done | bytes 5242912 | tf_op jit(solution)/shard_map/all_to_all | solution.py:49
  86.3 5.1 %all-to-all-start.1 = ((bf16[32,40,2048]{2,1,0:T(8,128)(2,1)}), bf16[32,40,2048]{2,1,0:T(8,128)(2,1)}, u32[]{:S(2)}, u32[]{:S(2)}) async-start(bf16[32,40,2048]{2,1,0:T(8,128)(2,1)} %bitcast.83), calls=%async_computation.1 | async-start | bytes 10485760 | tf_op jit(solution)/shard_map/all_to_all | solution.py:50
  91.4 3.6 fusion.27
  95.0 7.0 %fusion.1 = f32[768,768]{0,1:T(8,128)S(1)} fusion(bf16[768,2048]{1,0:T(8,128)(2,1)S(1)} %bitcast.95, bf16[2,2048,768]{2,1,0:T(8,128)(2,1)} %param.11), kind=kOutput, calls=%fused_computation.14 | convolution fusion | flops 2415919104 | bytes 8650752 | tf_op jit(solution)/shard_map/dot_general | solution.py:58
  102.1 2.8 fusion.4
  104.9 0.7 multiply_convert_fusion.5
  105.6 2.2 copy-done.22
  107.8 1.8 convolution_convert_fusion.3
  109.8 1.8 convolution_convert_fusion.4
  112.0 2.9 pad_maximum_fusion.2
  114.9 42.3 %all-to-all-done.1 = bf16[32,40,2048]{2,1,0:T(8,128)(2,1)} async-done(((bf16[32,40,2048]{2,1,0:T(8,128)(2,1)}), bf16[32,40,2048]{2,1,0:T(8,128)(2,1)}, u32[]{:S(2)}, u32[]{:S(2)}) %all-to-all-start.1) | async-done | bytes 5242912 | tf_op jit(solution)/shard_map/all_to_all | solution.py:50
  157.2 4.4 %slice_select_fusion.1 = (bf16[32,24,2048]{2,1,0:T(8,128)(2,1)}, bf16[32,24,2048]{2,1,0:T(8,128)(2,1)S(1)}) fusion(bf16[32,40,2048]{2,1,0:T(8,128)(2,1)} %all-to-all-done.1, pred[24]{0:T(512)(128)(4,1)S(1)} %get-tuple-element.49, pred[24]{0:T(512)(128)(4,1)S(1)} %get-tuple-element.48), kind=kLoop, calls=%fused_computation.20 | loop fusion | flops 3145728 | bytes 12582960 | tf_op jit(solution)/shard_map/jit(_where)/select_n | solution.py:83
  161.6 1.6 copy-done.5
  163.3 1.7 multiply_convert_fusion.2
  165.1 4.9 %all-to-all-start.2 = ((bf16[32,40,2048]{2,1,0:T(8,128)(2,1)}), bf16[32,40,2048]{2,1,0:T(8,128)(2,1)}, u32[]{:S(2)}, u32[]{:S(2)}) async-start(bf16[32,40,2048]{2,1,0:T(8,128)(2,1)} %pad_maximum_fusion.2), calls=%async_computation.2 | async-start | bytes 10485760 | tf_op jit(solution)/shard_map/all_to_all | solution.py:77
  170.1 5.2 %convolution_convert_fusion.1 = bf16[768,2048]{1,0:T(8,128)(2,1)S(1)} fusion(bf16[2,2048,768]{2,1,0:T(8,128)(2,1)} %param.11, bf16[768,384]{0,1:T(8,128)(2,1)S(1)} %get-tuple-element.45, bf16[768,384]{0,1:T(8,128)(2,1)S(1)} %get-tuple-element.44), kind=kOutput, calls=%fused_computation.9 | convolution fusion | flops 2419851264 | bytes 7471104 | tf_op jit(solution)/shard_map/dot_general | solution.py:90
  175.5 1.7 copy-done.4
  177.2 1.8 multiply_convert_fusion.4
  179.3 2.9 convolution_convert_fusion.2
  182.4 0.8 copy-done.16
  183.4 1.1 pad_maximum_fusion.5
  184.7 2.9 pad_maximum_fusion.3
  187.6 0.7 copy-done.6
  188.6 1.4 convolution_bitcast_fusion.2
  190.0 1.4 convolution_bitcast_fusion.3
  191.4 1.9 pad_maximum_fusion.1
  193.4 5.1 %convolution_bitcast_fusion = bf16[1,2048,768]{2,1,0:T(8,128)(2,1)S(1)} fusion(bf16[768,2048]{1,0:T(8,128)(2,1)} %bitcast.96, bf16[768,768]{0,1:T(8,128)(2,1)} %pad_maximum_fusion.5), kind=kOutput, calls=%fused_computation.7 | convolution fusion | flops 2415919104 | bytes 7471104 | tf_op jit(solution)/shard_map/dot_general | solution.py:97
  198.4 3.2 convolution_bitcast_fusion.1
  201.6 3.2 pad_maximum_fusion
  204.8 31.0 %all-to-all-done.2 = bf16[32,40,2048]{2,1,0:T(8,128)(2,1)} async-done(((bf16[32,40,2048]{2,1,0:T(8,128)(2,1)}), bf16[32,40,2048]{2,1,0:T(8,128)(2,1)}, u32[]{:S(2)}, u32[]{:S(2)}) %all-to-all-start.2) | async-done | bytes 5242912 | tf_op jit(solution)/shard_map/all_to_all | solution.py:77
  235.9 0.7 reduce-scatter.5.cloned.1.call-update
  236.6 4.9 %all-to-all-start.3 = ((bf16[32,40,2048]{2,1,0:T(8,128)(2,1)}), bf16[32,40,2048]{2,1,0:T(8,128)(2,1)}, u32[]{:S(2)}, u32[]{:S(2)}) async-start(bf16[32,40,2048]{2,1,0:T(8,128)(2,1)} %pad_maximum_fusion.3), calls=%async_computation.3 | async-start | bytes 10485760 | tf_op jit(solution)/shard_map/all_to_all | solution.py:108
  242.0 0.7 and.54
  244.1 53.8 %reduce-scatter.3.cloned.1.call-done = bf16[2,512,768]{2,1,0:T(8,128)(2,1)} async-done(((bf16[2,2048,768]{2,1,0:T(8,128)(2,1)}), bf16[2,512,768]{2,1,0:T(8,128)(2,1)}) %reduce-scatter.3.cloned.1.call-update) | async-done | bytes 1572880 | tf_op jit(solution)/shard_map/reduce_scatter | solution.py:102
  297.8 1.5 collective-permute-start
  299.3 4.0 %convolution_bitcast_fusion.4 = f32[128,1280]{0,1:T(8,128)S(1)} fusion(bf16[1280,2048]{1,0:T(8,128)(2,1)} %bitcast.18, bf16[128,2048]{1,0:T(8,128)(2,1)S(1)} %copy-done), kind=kOutput, calls=%fused_computation.27 | convolution fusion | flops 671088640 | bytes 6422528 | tf_op jit(solution)/shard_map/dot_general | solution.py:119
  303.3 7.0 %gather_fusion = f32[1024]{0:T(1024)S(1)} fusion(f32[128,1280]{0,1:T(8,128)S(1)} %convolution_bitcast_fusion.4, s32[1024]{0:T(1024)S(1)} %reshape.178), kind=kCustom, calls=%fused_computation | custom fusion | bytes 16384 | tf_op jit(solution)/shard_map/jit(take_along_axis)/gather | solution.py:122
  310.5 28.4 %reduce-scatter.5.cloned.1.call-done = bf16[2,384,512]{2,1,0:T(8,128)(2,1)} async-done(((bf16[2,384,2048]{2,1,0:T(8,128)(2,1)}), bf16[2,384,512]{2,1,0:T(8,128)(2,1)}) %reduce-scatter.5.cloned.1.call-update) | async-done | bytes 786448 | tf_op jit(solution)/shard_map/reduce_scatter | solution.py:105
  338.9 1.5 collective-permute-start.1
  341.0 4.3 %convolution_convert_fusion.5 = bf16[128,2048]{1,0:T(8,128)(2,1)} fusion(pred[128,1280]{0,1:T(32,128)(4,1)} %and.54, bf16[1280,2048]{1,0:T(8,128)(2,1)} %bitcast.21), kind=kOutput, calls=%fused_computation.28 | convolution fusion | flops 671350784 | bytes 5931008 | tf_op jit(solution)/shard_map/dot_general | solution.py:123
  345.3 5.7 %convolution_convert_fusion.6 = bf16[128,2048]{1,0:T(8,128)(2,1)} fusion(f32[128,1280]{0,1:T(8,128)S(1)} %select_n.84, bf16[1280,2048]{1,0:T(8,128)(2,1)} %bitcast.18), kind=kOutput, calls=%fused_computation.29 | convolution fusion | flops 4026793984 | bytes 6422528 | tf_op jit(solution)/shard_map/dot_general | solution.py:115
  351.0 7.4 %collective-permute-done.1 = bf16[2,384,512]{2,1,0:T(8,128)(2,1)S(1)} collective-permute-done((bf16[2,384,512]{2,1,0:T(8,128)(2,1)}, bf16[2,384,512]{2,1,0:T(8,128)(2,1)S(1)}, u32[]{:S(2)}, u32[]{:S(2)}) %collective-permute-start.1) | collective-permute-done | bytes 786464 | tf_op jit(solution)/shard_map/ppermute | solution.py:18
  358.4 1.2 select_convert_fusion.1
  359.6 1.9 select_convert_fusion
  (93 shorter events, 5.0 us)
Async XLA Ops:
  7.2 13.7 %copy-start = (bf16[128,2048]{1,0:T(8,128)(2,1)S(1)}, bf16[128,2048]{1,0:T(8,128)(2,1)}, u32[]{:S(2)}) copy-start(bf16[128,2048]{1,0:T(8,128)(2,1)} %param.10) | copy-start | bytes 1572868
  7.2 1.6 copy-start.19
  12.7 7.7 %copy-start.20 = (s32[128,8]{0,1:T(8,128)S(1)}, s32[128,8]{0,1:T(8,128)}, u32[]{:S(2)}) copy-start(s32[128,8]{0,1:T(8,128)} %param.8) | copy-start | bytes 12292
  12.7 7.7 %copy-start.21 = (f32[128,8]{0,1:T(8,128)S(1)}, f32[128,8]{0,1:T(8,128)}, u32[]{:S(2)}) copy-start(f32[128,8]{0,1:T(8,128)} %param.9) | copy-start | bytes 12292
  12.7 73.6 %all-to-all-start = ((bf16[32,40,2048]{2,1,0:T(8,128)(2,1)}), bf16[32,40,2048]{2,1,0:T(8,128)(2,1)}, u32[]{:S(2)}, u32[]{:S(2)}) async-start(bf16[32,40,2048]{2,1,0:T(8,128)(2,1)} %bitcast.84), calls=%async_computation | async-start | bytes 10485760 | tf_op jit(solution)/shard_map/all_to_all | solution.py:49
  86.3 70.9 %all-to-all-start.1 = ((bf16[32,40,2048]{2,1,0:T(8,128)(2,1)}), bf16[32,40,2048]{2,1,0:T(8,128)(2,1)}, u32[]{:S(2)}, u32[]{:S(2)}) async-start(bf16[32,40,2048]{2,1,0:T(8,128)(2,1)} %bitcast.83), calls=%async_computation.1 | async-start | bytes 10485760 | tf_op jit(solution)/shard_map/all_to_all | solution.py:50
  91.4 10.7 %slice-start = ((s8[6291456]{0:T(1024)(128)(4,1)}), s8[4194304]{0:T(1024)(128)(4,1)S(1)}, s32[]{:S(2)}) async-start(s8[6291456]{0:T(1024)(128)(4,1)} %bitcast.101), calls=%async_computation.8 | async-start | bytes 8388608
  95.0 7.0 %copy-start.3 = (bf16[32,24,2048]{2,1,0:T(8,128)(2,1)}, bf16[32,24,2048]{2,1,0:T(8,128)(2,1)S(1)}, u32[]{:S(2)}) copy-start(bf16[32,24,2048]{2,1,0:T(8,128)(2,1)S(1)} %get-tuple-element.41) | copy-start | bytes 9437188
  95.0 7.0 %copy-start.1 = (bf16[32,24,2048]{2,1,0:T(8,128)(2,1)}, bf16[32,24,2048]{2,1,0:T(8,128)(2,1)S(1)}, u32[]{:S(2)}) copy-start(bf16[32,24,2048]{2,1,0:T(8,128)(2,1)S(1)} %get-tuple-element.40) | copy-start | bytes 9437188
  95.0 7.0 %slice-start.1 = ((s8[6291456]{0:T(1024)(128)(4,1)}), s8[2097152]{0:T(1024)(128)(4,1)S(1)}, s32[]{:S(2)}) async-start(s8[6291456]{0:T(1024)(128)(4,1)} %bitcast.101), calls=%async_computation.9 | async-start | bytes 4194304
  102.0 2.8 copy-start.9
  104.9 4.8 %copy-start.7 = (f32[768,768]{0,1:T(8,128)}, f32[768,768]{0,1:T(8,128)S(1)}, u32[]{:S(2)}) copy-start(f32[768,768]{0,1:T(8,128)S(1)} %fusion.4) | copy-start | bytes 7077892
  104.9 3.0 copy-start.22
  105.6 4.1 %copy-start.13 = (bf16[768,384]{0,1:T(8,128)(2,1)}, bf16[768,384]{0,1:T(8,128)(2,1)S(1)}, u32[]{:S(2)}) copy-start(bf16[768,384]{0,1:T(8,128)(2,1)S(1)} %get-tuple-element.26) | copy-start | bytes 1769476
  157.2 6.0 %copy-start.10 = (f32[768,768]{0,1:T(8,128)S(1)}, f32[768,768]{0,1:T(8,128)}, u32[]{:S(2)}) copy-start(f32[768,768]{0,1:T(8,128)} %copy-done.9) | copy-start | bytes 7077892
  157.2 6.2 %copy-start.23 = (bf16[2,384,2048]{2,1,0:T(8,128)(2,1)S(1)}, bf16[2,384,2048]{2,1,0:T(8,128)(2,1)}, u32[]{:S(2)}) copy-start(bf16[2,384,2048]{2,1,0:T(8,128)(2,1)} %param.12) | copy-start | bytes 9437188
  161.6 1.6 copy-start.5
  165.1 5.0 %copy-start.15 = (bf16[768,384]{0,1:T(8,128)(2,1)}, bf16[768,384]{0,1:T(8,128)(2,1)S(1)}, u32[]{:S(2)}) copy-start(bf16[768,384]{0,1:T(8,128)(2,1)S(1)} %get-tuple-element.44) | copy-start | bytes 1769476
  165.1 5.0 %copy-start.17 = (bf16[768,384]{0,1:T(8,128)(2,1)}, bf16[768,384]{0,1:T(8,128)(2,1)S(1)}, u32[]{:S(2)}) copy-start(bf16[768,384]{0,1:T(8,128)(2,1)S(1)} %get-tuple-element.45) | copy-start | bytes 1769476
  165.1 70.8 %all-to-all-start.2 = ((bf16[32,40,2048]{2,1,0:T(8,128)(2,1)}), bf16[32,40,2048]{2,1,0:T(8,128)(2,1)}, u32[]{:S(2)}, u32[]{:S(2)}) async-start(bf16[32,40,2048]{2,1,0:T(8,128)(2,1)} %pad_maximum_fusion.2), calls=%async_computation.2 | async-start | bytes 10485760 | tf_op jit(solution)/shard_map/all_to_all | solution.py:77
  170.0 127.9 %reduce-scatter.3.cloned.1.call-start = ((), (), s32[]{:S(2)}) async-start(), calls=%async_computation.6 | async-start | bytes 7864320 | tf_op jit(solution)/shard_map/reduce_scatter | solution.py:102
  170.0 5.4 %copy-start.8 = (f32[768,768]{0,1:T(8,128)S(1)}, f32[768,768]{0,1:T(8,128)}, u32[]{:S(2)}) copy-start(f32[768,768]{0,1:T(8,128)} %copy-done.7) | copy-start | bytes 7077892
  170.1 5.4 %copy-start.24 = (bf16[2,384,2048]{2,1,0:T(8,128)(2,1)S(1)}, bf16[2,384,2048]{2,1,0:T(8,128)(2,1)}, u32[]{:S(2)}) copy-start(bf16[2,384,2048]{2,1,0:T(8,128)(2,1)} %param.12) | copy-start | bytes 9437188
  175.3 1.9 copy-start.4
  175.3 3.7 %slice-start.2 = ((s8[6291456]{0:T(1024)(128)(4,1)}), s8[4194304]{0:T(1024)(128)(4,1)S(1)}, s32[]{:S(2)}) async-start(s8[6291456]{0:T(1024)(128)(4,1)} %bitcast.103), calls=%async_computation.10 | async-start | bytes 8388608
  177.2 2.1 slice-start.3
  182.2 1.1 copy-start.16
  182.2 1.2 copy-start.18
  184.7 3.6 copy-start.6
  184.7 3.9 %copy-start.14 = (bf16[768,384]{0,1:T(8,128)(2,1)S(1)}, bf16[768,384]{0,1:T(8,128)(2,1)}, u32[]{:S(2)}) copy-start(bf16[768,384]{0,1:T(8,128)(2,1)} %copy-done.13) | copy-start | bytes 1769476
  193.4 5.1 %copy-start.2 = (bf16[32,24,2048]{2,1,0:T(8,128)(2,1)S(1)}, bf16[32,24,2048]{2,1,0:T(8,128)(2,1)}, u32[]{:S(2)}) copy-start(bf16[32,24,2048]{2,1,0:T(8,128)(2,1)} %copy-done.1) | copy-start | bytes 9437188
  235.9 103.1 %reduce-scatter.5.cloned.1.call-start = ((), (), s32[]{:S(2)}) async-start(), calls=%async_computation.7 | async-start | bytes 3932160 | tf_op jit(solution)/shard_map/reduce_scatter | solution.py:105
  236.6 6.2 %copy-start.25 = (s32[32]{0:T(128)S(1)}, s32[32]{0:T(128)}, u32[]{:S(2)}) copy-start(s32[32]{0:T(128)} %param.13) | copy-start | bytes 388
  236.6 104.4 %all-to-all-start.3 = ((bf16[32,40,2048]{2,1,0:T(8,128)(2,1)}), bf16[32,40,2048]{2,1,0:T(8,128)(2,1)}, u32[]{:S(2)}, u32[]{:S(2)}) async-start(bf16[32,40,2048]{2,1,0:T(8,128)(2,1)} %pad_maximum_fusion.3), calls=%async_computation.3 | async-start | bytes 10485760 | tf_op jit(solution)/shard_map/all_to_all | solution.py:108
  297.8 61.8 %collective-permute-start = (bf16[2,512,768]{2,1,0:T(8,128)(2,1)}, bf16[2,512,768]{2,1,0:T(8,128)(2,1)S(1)}, u32[]{:S(2)}, u32[]{:S(2)}) collective-permute-start(bf16[2,512,768]{2,1,0:T(8,128)(2,1)} %reduce-scatter.3.cloned.1.call-done), channel_id=1, source_target_pairs={{0,8},{8,0},{4,12},{12,4},{16,24},{24,16},{20,28},{28,20},{32,40},... | collective-permute-start | bytes 4718600 | tf_op jit(solution)/shard_map/ppermute | solution.py:18
  338.9 19.4 %collective-permute-start.1 = (bf16[2,384,512]{2,1,0:T(8,128)(2,1)}, bf16[2,384,512]{2,1,0:T(8,128)(2,1)S(1)}, u32[]{:S(2)}, u32[]{:S(2)}) collective-permute-start(bf16[2,384,512]{2,1,0:T(8,128)(2,1)} %reduce-scatter.5.cloned.1.call-done), channel_id=1, source_target_pairs={{0,8},{8,0},{4,12},{12,4},{16,24},{24,16},{20,28},{28,20},{32,40},... | collective-permute-start | bytes 2359304 | tf_op jit(solution)/shard_map/ppermute | solution.py:18
  345.3 13.1 %copy-start.12 = (bf16[2,384,512]{2,1,0:T(8,128)(2,1)S(1)}, bf16[2,384,512]{2,1,0:T(8,128)(2,1)}, u32[]{:S(2)}) copy-start(bf16[2,384,512]{2,1,0:T(8,128)(2,1)} %reduce-scatter.5.cloned.1.call-done) | copy-start | bytes 2359300
  351.0 8.6 %copy-start.11 = (bf16[2,512,768]{2,1,0:T(8,128)(2,1)S(1)}, bf16[2,512,768]{2,1,0:T(8,128)(2,1)}, u32[]{:S(2)}) copy-start(bf16[2,512,768]{2,1,0:T(8,128)(2,1)} %reduce-scatter.3.cloned.1.call-done) | copy-start | bytes 4718596
Sparse Core Ops, SparseCore 0:
  236.0 61.7 reduce-scatter.2
  300.8 38.0 reduce-scatter.4
